TPU v7x, 512 devices: a whole 4x8x8 slice. The times are simulated.
512 devices in a mesh: wide: 32 (over y, z_hi, core), loop: 16 (over z_lo, x).
Axes of the slice: x: 4, y: 8, z: 8 (z_hi: 2, z_lo: 4; z = z_hi * 4 + z_lo), core: 2. Of those that a mesh axis runs over, the one named last changes fastest.
Arguments:
- feats: bfloat16 [16384, 512], P('loop'), may hold values from -6 to 6
- tiles: bfloat16 [16, 32, 4, 128, 128], P('loop', 'wide'), may hold values from -0.1875 to 0.1875
- tile_rows: int32 [16, 32, 4], P('loop', 'wide'), may hold values from 0 to 7
- tile_cols: int32 [16, 32, 4], P('loop', 'wide'), may hold values from 0 to 15
- tile_count: int32 [16, 32], P('loop', 'wide'), may hold values from 1 to 4, as said below
- w_msg: bfloat16 [512, 512], replicated, may hold values from -0.25 to 0.25
- w_self: bfloat16 [512, 512], replicated, may hold values from -0.25 to 0.25
- readout: float32 [512], replicated, may hold values from -0.6 to 0.6
- labels: int32 [16384], P('loop'), may hold values from 0 to 1
Outputs:
- logits: float32 [16384], P('loop')
- grad_msg: bfloat16 [512, 512], replicated
- grad_self: bfloat16 [512, 512], replicated
Inputs may be any that keep to these rules, and one draw needn't show every extreme that they name: `tile_count`: some loop and wide index uses all 4 slots in every draw.
All inputs are finite; a program needn't handle non-finite values.
Results may differ from a plain program's by a relative error of at most 0.02.
Values may be sent and summed in bfloat16 or wider, within the bound.
No kernel may reach another device: no remote copies, remote signals or barrier semaphores. Data moves between devices by JAX's collectives and lax.ppermute only.
A program may use at most 64 MiB of HBM per device.

v0:
```python
import jax
import jax.numpy as jnp
from jax import lax
from jax.sharding import PartitionSpec as P


def copy_for_each(value, axis):
    copies = jnp.broadcast_to(value, (lax.axis_size(axis), *value.shape))
    return lax.all_to_all(copies, axis, split_axis=0, concat_axis=0, tiled=True)


def laid_out(blocks, dim):
    shape = list(blocks.shape[1:])
    shape[dim] *= blocks.shape[0]
    return jnp.moveaxis(blocks, 0, dim).reshape(shape)


def gather_directly(value, axis, dim):
    blocks = copy_for_each(value, axis)
    return laid_out(blocks, dim)


def in_blocks(value, dim, devices):
    before, after = (value.shape[:dim], value.shape[dim + 1 :])
    return jnp.moveaxis(value.reshape(*before, devices, -1, *after), dim, 0)


def sum_at_owner(value, axis, dim):
    devices = lax.axis_size(axis)
    blocks = lax.all_to_all(in_blocks(value, dim, devices), axis, 0, 0, tiled=True)
    return jnp.sum(blocks.astype(jnp.float32), axis=0)


def body(feats, tiles, tile_rows, tile_cols, tile_count, w_msg, w_self, readout, labels):
    rows_dev, feat_width = feats.shape
    size_tb = tiles.shape[-1]
    slot_count = tiles.shape[2]
    blocks_dev = rows_dev // size_tb
    wide_size = lax.axis_size("wide")
    cols_own = max(1, blocks_dev // wide_size)
    wide_pos = lax.axis_index("wide")
    picked_blocks = wide_pos % blocks_dev + wide_size * jnp.arange(cols_own, dtype=jnp.int32)
    own_blocks = jnp.take(feats.reshape(blocks_dev, size_tb, feat_width), picked_blocks, axis=0)
    gathered = gather_directly(own_blocks, "loop", 0)
    tile_vals = tiles.reshape(slot_count, size_tb, size_tb)
    chosen = jnp.take(gathered, tile_cols.reshape(slot_count), axis=0)
    product = jnp.einsum("sij,sjd->sid", tile_vals, chosen, preferred_element_type=jnp.float32)
    valid_slot = jnp.arange(slot_count, dtype=jnp.int32) < tile_count.reshape(())
    placing = (
        (tile_rows.reshape(slot_count)[:, None] == jnp.arange(blocks_dev, dtype=jnp.int32)[None, :])
        & valid_slot[:, None]
    ).astype(jnp.float32)
    partial_value = jnp.einsum(
        "sr,sid->rid", placing, product, precision=lax.Precision.HIGHEST
    ).reshape(rows_dev, feat_width)
    message = sum_at_owner(partial_value.astype(jnp.bfloat16), "wide", 0).astype(jnp.bfloat16)
    share_rows = rows_dev // wide_size
    node_feats = lax.dynamic_slice_in_dim(feats, wide_pos * share_rows, share_rows, 0)
    node_labels = lax.dynamic_slice_in_dim(labels, wide_pos * share_rows, share_rows, 0)
    pre_act = jnp.dot(message, w_msg, preferred_element_type=jnp.float32) + jnp.dot(
        node_feats, w_self, preferred_element_type=jnp.float32
    )
    hidden = node_feats.astype(jnp.float32) + jax.nn.silu(pre_act)
    logits = jnp.dot(hidden, readout, precision=lax.Precision.HIGHEST)
    residual_grad = jax.nn.sigmoid(logits) - node_labels.astype(jnp.float32)
    gate_sig = jax.nn.sigmoid(pre_act)
    pre_grad = (
        residual_grad[:, None] * readout[None, :] * gate_sig * (1.0 + pre_act * (1.0 - gate_sig))
    ).astype(jnp.bfloat16)
    grad_msg = jnp.einsum("na,nb->ab", message, pre_grad, preferred_element_type=jnp.float32)
    grad_self = jnp.einsum("na,nb->ab", node_feats, pre_grad, preferred_element_type=jnp.float32)
    grad_msg, grad_self = lax.psum((grad_msg, grad_self), ("wide", "loop"))
    out_logits = gather_directly(logits, "wide", 0)
    return (out_logits, grad_msg.astype(jnp.bfloat16), grad_self.astype(jnp.bfloat16))


def solution(mesh):
    placed = (
        P("loop", None),
        P("loop", "wide", None, None, None),
        P("loop", "wide", None),
        P("loop", "wide", None),
        P("loop", "wide"),
        P(),
        P(),
        P(),
        P("loop"),
    )
    return jax.shard_map(
        body, mesh=mesh, in_specs=placed, out_specs=(P("loop"), P(), P()), check_vma=False
    )
```

profile of v0, /device:TPU:1, one launch (start us, length us, event | category | flops | bytes accessed | tf_op | source)
XLA Modules:
  0.0 231.8 jit_solution(13406458065787893768)
XLA Ops:
  0.7 1.0 fusion.6
  1.6 1.5 broadcast_in_dim.36
  3.2 10.5 %all-to-all-start = ((bf16[16,1,128,512]{3,2,1,0:T(8,128)(2,1)}), bf16[16,1,128,512]{3,2,1,0:T(8,128)(2,1)S(1)}, u32[]{:S(2)}, u32[]{:S(2)}) async-start(bf16[16,1,128,512]{3,2,1,0:T(8,128)(2,1)} %broadcast_in_dim.36), calls=%async_computation | async-start | bytes 4194304 | tf_op jit(solution)/shard_map/all_to_all | solution.py:9
  14.4 40.8 %all-to-all-done = bf16[16,1,128,512]{3,2,1,0:T(8,128)(2,1)S(1)} async-done(((bf16[16,1,128,512]{3,2,1,0:T(8,128)(2,1)}), bf16[16,1,128,512]{3,2,1,0:T(8,128)(2,1)S(1)}, u32[]{:S(2)}, u32[]{:S(2)}) %all-to-all-start) | async-done | bytes 2097184 | tf_op jit(solution)/shard_map/all_to_all | solution.py:9
  55.2 0.6 gather_fusion
  55.8 0.4 fusion.1
  56.3 0.5 copy.13
  56.8 1.4 convolution_convert_fusion
  58.1 1.3 copy.12
  59.4 15.5 %all-to-all-start.1 = ((bf16[32,32,512]{2,1,0:T(8,128)(2,1)}), bf16[32,32,512]{2,1,0:T(8,128)(2,1)S(1)}, u32[]{:S(2)}, u32[]{:S(2)}) async-start(bf16[32,32,512]{2,1,0:T(8,128)(2,1)} %bitcast.14), calls=%async_computation.1 | async-start | bytes 2097152 | tf_op jit(solution)/shard_map/all_to_all | solution.py:30
  74.9 29.5 %all-to-all-done.1 = bf16[32,32,512]{2,1,0:T(8,128)(2,1)S(1)} async-done(((bf16[32,32,512]{2,1,0:T(8,128)(2,1)}), bf16[32,32,512]{2,1,0:T(8,128)(2,1)S(1)}, u32[]{:S(2)}, u32[]{:S(2)}) %all-to-all-start.1) | async-done | bytes 1048608 | tf_op jit(solution)/shard_map/all_to_all | solution.py:30
  104.4 0.2 reduce_sum.12
  104.6 0.2 fusion.27
  104.8 1.0 convolution_add_fusion
  105.8 0.0 copy-done.3
  105.8 0.9 divide_subtract_fusion
  106.7 1.1 fusion.11
  107.9 0.3 fusion.26
  108.2 0.6 broadcast_in_dim.38
  108.8 7.4 %all-to-all-start.2 = ((f32[32,1,32]{2,1,0:T(1,128)}), f32[32,1,32]{2,1,0:T(1,128)S(1)}, u32[]{:S(2)}, u32[]{:S(2)}) async-start(f32[32,1,32]{2,1,0:T(1,128)} %broadcast_in_dim.38), calls=%async_computation.2 | async-start | bytes 32768 | tf_op jit(solution)/shard_map/all_to_all | solution.py:9
  116.2 113.7 %all-reduce.2 = (bf16[512,512]{1,0:T(8,128)(2,1)}, bf16[512,512]{1,0:T(8,128)(2,1)}) all-reduce(f32[512,512]{1,0:T(8,128)S(1)} %fusion.26, f32[512,512]{1,0:T(8,128)S(1)} %fusion.11), channel_id=1, replica_groups=mesh['wide'=32,'loop'=16] {'wide','loop'}, use_global_device_ids=true, to_apply=%region_1.2 | all-reduce | flops 524288 | bytes 3145728 | tf_op jit(solution)/shard_map/psum | solution.py:72
  229.9 0.5 broadcast.84
  230.5 0.7 reduce.4
  231.2 0.7 reshape.92
  (16 shorter events, 0.1 us)
Async XLA Ops:
  0.6 104.0 %copy-start = (bf16[512,512]{1,0:T(8,128)(2,1)S(1)}, bf16[512,512]{1,0:T(8,128)(2,1)}, u32[]{:S(2)}) copy-start(bf16[512,512]{1,0:T(8,128)(2,1)} %param.14) | copy-start | bytes 1572868
  3.2 11.2 %copy-start.5 = (s32[1,1,4]{2,1,0:T(1,128)S(1)}, s32[1,1,4]{2,1,0:T(1,128)}, u32[]{:S(2)}) copy-start(s32[1,1,4]{2,1,0:T(1,128)} %param.12) | copy-start | bytes 52
  3.2 52.6 %copy-start.2 = (bf16[1,1,4,128,128]{4,3,2,1,0:T(8,128)(2,1)S(1)}, bf16[1,1,4,128,128]{4,3,2,1,0:T(8,128)(2,1)}, u32[]{:S(2)}) copy-start(bf16[1,1,4,128,128]{4,3,2,1,0:T(8,128)(2,1)} %param.10) | copy-start | bytes 393220
  3.2 52.0 %all-to-all-start = ((bf16[16,1,128,512]{3,2,1,0:T(8,128)(2,1)}), bf16[16,1,128,512]{3,2,1,0:T(8,128)(2,1)S(1)}, u32[]{:S(2)}, u32[]{:S(2)}) async-start(bf16[16,1,128,512]{3,2,1,0:T(8,128)(2,1)} %broadcast_in_dim.36), calls=%async_computation | async-start | bytes 4194304 | tf_op jit(solution)/shard_map/all_to_all | solution.py:9
  55.8 0.9 copy-start.4
  59.4 45.4 %copy-start.1 = (bf16[512,512]{1,0:T(8,128)(2,1)S(1)}, bf16[512,512]{1,0:T(8,128)(2,1)}, u32[]{:S(2)}) copy-start(bf16[512,512]{1,0:T(8,128)(2,1)} %param.15) | copy-start | bytes 1572868
  59.4 46.3 %copy-start.3 = (f32[512]{0:T(512)S(1)}, f32[512]{0:T(512)}, u32[]{:S(2)}) copy-start(f32[512]{0:T(512)} %param.16) | copy-start | bytes 6148
  59.4 45.0 %all-to-all-start.1 = ((bf16[32,32,512]{2,1,0:T(8,128)(2,1)}), bf16[32,32,512]{2,1,0:T(8,128)(2,1)S(1)}, u32[]{:S(2)}, u32[]{:S(2)}) async-start(bf16[32,32,512]{2,1,0:T(8,128)(2,1)} %bitcast.14), calls=%async_computation.1 | async-start | bytes 2097152 | tf_op jit(solution)/shard_map/all_to_all | solution.py:30
  108.8 121.1 %all-to-all-start.2 = ((f32[32,1,32]{2,1,0:T(1,128)}), f32[32,1,32]{2,1,0:T(1,128)S(1)}, u32[]{:S(2)}, u32[]{:S(2)}) async-start(f32[32,1,32]{2,1,0:T(1,128)} %broadcast_in_dim.38), calls=%async_computation.2 | async-start | bytes 32768 | tf_op jit(solution)/shard_map/all_to_all | solution.py:9
where the time goes:
time: 232 us
  blocking collectives  114 us (49%)
  waiting for transfers between devices  70.3 us (30%)
  starting transfers between devices  33.4 us (14%)
  local copies, waits for them, and re-layouts  5.73 us (2%)
  matrix products  5.34 us (2%)
    psum x1, blocking collectives, body(): grad_msg, grad_self = lax.psum((grad_msg, grad_self), ('wide', 'loop'))  114 us
    all_to_all x2, waiting for transfers between devices, copy_for_each(): return lax.all_to_all(copies, axis, split_axis=0, concat_axis=0, tiled=True)  40.8 us
    all_to_all x1, waiting for transfers between devices, sum_at_owner(): lax.all_to_all(in_blocks(value, dim, devices), axis, 0, 0, tiled=True)  29.5 us
    all_to_all x2, starting transfers between devices, copy_for_each(): return lax.all_to_all(copies, axis, split_axis=0, concat_axis=0, tiled=True)  17.9 us
    all_to_all x1, starting transfers between devices, sum_at_owner(): lax.all_to_all(in_blocks(value, dim, devices), axis, 0, 0, tiled=True)  15.5 us
  transfers between devices with their start and end apart: 3, of which 2 were waited for; matrix products, arithmetic and copies ran while one was open for 0% of the time, Pallas kernels for 0%

commit v1 on v0

--- a/solution.py
+++ b/solution.py
@@ -1,7 +1,7 @@
 import jax
 import jax.numpy as jnp
 from jax import lax
-from jax.sharding import PartitionSpec as P
+from jax.sharding import Mesh, PartitionSpec as P
 
 
 def copy_for_each(value, axis):
@@ -31,14 +31,19 @@
     return jnp.sum(blocks.astype(jnp.float32), axis=0)
 
 
+WIDE = ("wy", "wz", "wc")
+
+
 def body(feats, tiles, tile_rows, tile_cols, tile_count, w_msg, w_self, readout, labels):
     rows_dev, feat_width = feats.shape
     size_tb = tiles.shape[-1]
     slot_count = tiles.shape[2]
     blocks_dev = rows_dev // size_tb
-    wide_size = lax.axis_size("wide")
+    wide_size = lax.axis_size(WIDE)
     cols_own = max(1, blocks_dev // wide_size)
-    wide_pos = lax.axis_index("wide")
+    wide_pos = (lax.axis_index("wy") * lax.axis_size("wz") + lax.axis_index("wz")) * lax.axis_size(
+        "wc"
+    ) + lax.axis_index("wc")
     picked_blocks = wide_pos % blocks_dev + wide_size * jnp.arange(cols_own, dtype=jnp.int32)
     own_blocks = jnp.take(feats.reshape(blocks_dev, size_tb, feat_width), picked_blocks, axis=0)
     gathered = gather_directly(own_blocks, "loop", 0)
@@ -53,7 +58,17 @@
     partial_value = jnp.einsum(
         "sr,sid->rid", placing, product, precision=lax.Precision.HIGHEST
     ).reshape(rows_dev, feat_width)
-    message = sum_at_owner(partial_value.astype(jnp.bfloat16), "wide", 0).astype(jnp.bfloat16)
+    core = lax.axis_index("wc")
+    by_owner = partial_value.astype(jnp.bfloat16).reshape(
+        lax.axis_size("wy"), lax.axis_size("wz"), lax.axis_size("wc"), -1, feat_width
+    )
+    keep = lax.dynamic_index_in_dim(by_owner, core, 2, keepdims=False)
+    give = lax.dynamic_index_in_dim(by_owner, 1 - core, 2, keepdims=False)
+    got = lax.ppermute(give, "wc", [(0, 1), (1, 0)])
+    pair_sum = (keep.astype(jnp.float32) + got.astype(jnp.float32)).astype(jnp.bfloat16)
+    pair_sum = pair_sum.reshape(-1, pair_sum.shape[-2], feat_width)
+    message = sum_at_owner(pair_sum, ("wy", "wz"), 0).astype(jnp.bfloat16)
+    message = message.reshape(-1, feat_width)
     share_rows = rows_dev // wide_size
     node_feats = lax.dynamic_slice_in_dim(feats, wide_pos * share_rows, share_rows, 0)
     node_labels = lax.dynamic_slice_in_dim(labels, wide_pos * share_rows, share_rows, 0)
@@ -69,23 +84,25 @@
     ).astype(jnp.bfloat16)
     grad_msg = jnp.einsum("na,nb->ab", message, pre_grad, preferred_element_type=jnp.float32)
     grad_self = jnp.einsum("na,nb->ab", node_feats, pre_grad, preferred_element_type=jnp.float32)
-    grad_msg, grad_self = lax.psum((grad_msg, grad_self), ("wide", "loop"))
-    out_logits = gather_directly(logits, "wide", 0)
+    grad_msg, grad_self = lax.psum((grad_msg, grad_self), (*WIDE, "loop"))
+    out_logits = gather_directly(logits, WIDE, 0)
     return (out_logits, grad_msg.astype(jnp.bfloat16), grad_self.astype(jnp.bfloat16))
 
 
 def solution(mesh):
+    wide_devices, loop_devices = mesh.devices.shape
+    split = Mesh(mesh.devices.reshape(wide_devices // 4, 2, 2, loop_devices), (*WIDE, "loop"))
     placed = (
         P("loop", None),
-        P("loop", "wide", None, None, None),
-        P("loop", "wide", None),
-        P("loop", "wide", None),
-        P("loop", "wide"),
+        P("loop", WIDE, None, None, None),
+        P("loop", WIDE, None),
+        P("loop", WIDE, None),
+        P("loop", WIDE),
         P(),
         P(),
         P(),
         P("loop"),
     )
     return jax.shard_map(
-        body, mesh=mesh, in_specs=placed, out_specs=(P("loop"), P(), P()), check_vma=False
+        body, mesh=split, in_specs=placed, out_specs=(P("loop"), P(), P()), check_vma=False
     )

time: 232 us -> 226 us (0.974)
  waiting for transfers between devices: 70.3 us -> 62.4 us
    all_to_all x1, waiting for transfers between devices: 29.5 us -> 20.1 us  [sum_at_owner(): lax.all_to_all(in_blocks(value, dim, devices), axis, 0, 0, tiled=True)]
    ppermute x0 -> x1, starting transfers between devices: none -> 4.43 us  [body(): got = lax.ppermute(give, 'wc', [(0, 1), (1, 0)])]
    all_to_all x1, starting transfers between devices: 15.5 us -> 12.6 us  [sum_at_owner(): lax.all_to_all(in_blocks(value, dim, devices), axis, 0, 0, tiled=True)]
  transfers between devices with their start and end apart: 3 -> 4, of which waited for: 2 -> 3; matrix products, arithmetic and copies ran while one was open for 0% -> 0% of each run, Pallas kernels for 0% -> 0%
where the time goes in v1:
time: 226 us
  blocking collectives  116 us (51%)
  waiting for transfers between devices  62.4 us (28%)
  starting transfers between devices  33.4 us (15%)
  matrix products  5.34 us (2%)
  local copies, waits for them, and re-layouts  4.69 us (2%)
  other arithmetic  2.77 us (1%)
    psum x1, blocking collectives, body(): grad_msg, grad_self = lax.psum((grad_msg, grad_self), (*WIDE, 'loop'))  116 us
    all_to_all x2, waiting for transfers between devices, copy_for_each(): return lax.all_to_all(copies, axis, split_axis=0, concat_axis=0, tiled=True)  40.8 us
    all_to_all x1, waiting for transfers between devices, sum_at_owner(): lax.all_to_all(in_blocks(value, dim, devices), axis, 0, 0, tiled=True)  20.1 us
    all_to_all x2, starting transfers between devices, copy_for_each(): return lax.all_to_all(copies, axis, split_axis=0, concat_axis=0, tiled=True)  16.3 us
    all_to_all x1, starting transfers between devices, sum_at_owner(): lax.all_to_all(in_blocks(value, dim, devices), axis, 0, 0, tiled=True)  12.6 us
  transfers between devices with their start and end apart: 4, of which 3 were waited for; matrix products, arithmetic and copies ran while one was open for 0% of the time, Pallas kernels for 0%

profile of v1, /device:TPU:1, one launch (start us, length us, event | category | flops | bytes accessed | tf_op | source)
XLA Modules:
  0.0 225.9 jit_solution(3827690420925960240)
XLA Ops:
  0.7 1.0 fusion.5
  1.6 1.6 broadcast_in_dim.36
  3.2 10.5 %all-to-all-start = ((bf16[16,1,128,512]{3,2,1,0:T(8,128)(2,1)}), bf16[16,1,128,512]{3,2,1,0:T(8,128)(2,1)S(1)}, u32[]{:S(2)}, u32[]{:S(2)}) async-start(bf16[16,1,128,512]{3,2,1,0:T(8,128)(2,1)} %broadcast_in_dim.36), calls=%async_computation | async-start | bytes 4194304 | tf_op jit(solution)/shard_map/all_to_all | solution.py:9
  14.4 40.8 %all-to-all-done = bf16[16,1,128,512]{3,2,1,0:T(8,128)(2,1)S(1)} async-done(((bf16[16,1,128,512]{3,2,1,0:T(8,128)(2,1)}), bf16[16,1,128,512]{3,2,1,0:T(8,128)(2,1)S(1)}, u32[]{:S(2)}, u32[]{:S(2)}) %all-to-all-start) | async-done | bytes 2097184 | tf_op jit(solution)/shard_map/all_to_all | solution.py:9
  55.2 0.6 gather_fusion
  55.8 0.4 convolution_bitcast_fusion
  56.3 0.5 copy.24
  56.8 1.4 convolution_convert_fusion
  58.4 4.4 %collective-permute-start = (bf16[8,2,32,512]{3,2,1,0:T(8,128)(2,1)S(1)}, bf16[8,2,32,512]{3,2,1,0:T(8,128)(2,1)S(1)}, u32[]{:S(2)}, u32[]{:S(2)}) collective-permute-start(bf16[8,2,32,512]{3,2,1,0:T(8,128)(2,1)S(1)} %bitcast.47), channel_id=1, source_target_pairs={{0,16},{16,0},{1,17},{17,1},{2,18},{18,2},{3,19},{19,3},{4,20},{20... | collective-permute-start | bytes 1572872 | tf_op jit(solution)/shard_map/ppermute | solution.py:67
  62.9 1.5 collective-permute-done
  64.4 1.0 fusion
  65.4 12.6 %all-to-all-start.1 = ((bf16[16,1,32,512]{3,2,1,0:T(8,128)(2,1)}), bf16[16,1,32,512]{3,2,1,0:T(8,128)(2,1)S(1)}, u32[]{:S(2)}, u32[]{:S(2)}) async-start(bf16[16,1,32,512]{3,2,1,0:T(8,128)(2,1)} %bitcast.18), calls=%async_computation.1 | async-start | bytes 1048576 | tf_op jit(solution)/shard_map/all_to_all | solution.py:30
  78.0 20.1 %all-to-all-done.1 = bf16[16,1,32,512]{3,2,1,0:T(8,128)(2,1)S(1)} async-done(((bf16[16,1,32,512]{3,2,1,0:T(8,128)(2,1)}), bf16[16,1,32,512]{3,2,1,0:T(8,128)(2,1)S(1)}, u32[]{:S(2)}, u32[]{:S(2)}) %all-to-all-start.1) | async-done | bytes 524320 | tf_op jit(solution)/shard_map/all_to_all | solution.py:30
  98.2 0.2 fusion.26
  98.4 1.0 convolution_add_fusion
  99.4 0.9 divide_subtract_fusion
  100.3 1.1 fusion.10
  101.5 0.3 fusion.25
  101.8 0.6 broadcast_in_dim.38
  102.4 5.8 %all-to-all-start.2 = ((f32[32,1,32]{2,1,0:T(1,128)}), f32[32,1,32]{2,1,0:T(1,128)S(1)}, u32[]{:S(2)}, u32[]{:S(2)}) async-start(f32[32,1,32]{2,1,0:T(1,128)} %broadcast_in_dim.38), calls=%async_computation.2 | async-start | bytes 32768 | tf_op jit(solution)/shard_map/all_to_all | solution.py:9
  108.3 115.7 %all-reduce.2 = (bf16[512,512]{1,0:T(8,128)(2,1)}, bf16[512,512]{1,0:T(8,128)(2,1)}) all-reduce(f32[512,512]{1,0:T(8,128)S(1)} %fusion.25, f32[512,512]{1,0:T(8,128)S(1)} %fusion.10), channel_id=1, replica_groups=mesh['wy'=8,'wz'=2,'wc'=2,'loop'=16] {'wy','wz','wc','loop'}, use_global_device_ids=true, to_apply=%region_1.2 | all-reduce | flops 524288 | bytes 3145728 | tf_op jit(solution)/shard_map/psum | solution.py:87
  224.0 0.5 broadcast.84
  224.5 0.7 reduce.5
  225.2 0.7 reshape.97
  (20 shorter events, 0.4 us)
Async XLA Ops:
  0.6 97.6 %copy-start = (bf16[512,512]{1,0:T(8,128)(2,1)S(1)}, bf16[512,512]{1,0:T(8,128)(2,1)}, u32[]{:S(2)}) copy-start(bf16[512,512]{1,0:T(8,128)(2,1)} %param.14) | copy-start | bytes 1572868
  3.2 11.2 %copy-start.5 = (s32[1,1,4]{2,1,0:T(1,128)S(1)}, s32[1,1,4]{2,1,0:T(1,128)}, u32[]{:S(2)}) copy-start(s32[1,1,4]{2,1,0:T(1,128)} %param.12) | copy-start | bytes 52
  3.2 52.6 %copy-start.2 = (bf16[1,1,4,128,128]{4,3,2,1,0:T(8,128)(2,1)S(1)}, bf16[1,1,4,128,128]{4,3,2,1,0:T(8,128)(2,1)}, u32[]{:S(2)}) copy-start(bf16[1,1,4,128,128]{4,3,2,1,0:T(8,128)(2,1)} %param.10) | copy-start | bytes 393220
  3.2 52.0 %all-to-all-start = ((bf16[16,1,128,512]{3,2,1,0:T(8,128)(2,1)}), bf16[16,1,128,512]{3,2,1,0:T(8,128)(2,1)S(1)}, u32[]{:S(2)}, u32[]{:S(2)}) async-start(bf16[16,1,128,512]{3,2,1,0:T(8,128)(2,1)} %broadcast_in_dim.36), calls=%async_computation | async-start | bytes 4194304 | tf_op jit(solution)/shard_map/all_to_all | solution.py:9
  55.8 0.9 copy-start.4
  58.4 40.0 %copy-start.1 = (bf16[512,512]{1,0:T(8,128)(2,1)S(1)}, bf16[512,512]{1,0:T(8,128)(2,1)}, u32[]{:S(2)}) copy-start(bf16[512,512]{1,0:T(8,128)(2,1)} %param.15) | copy-start | bytes 1572868
  58.4 6.0 %collective-permute-start = (bf16[8,2,32,512]{3,2,1,0:T(8,128)(2,1)S(1)}, bf16[8,2,32,512]{3,2,1,0:T(8,128)(2,1)S(1)}, u32[]{:S(2)}, u32[]{:S(2)}) collective-permute-start(bf16[8,2,32,512]{3,2,1,0:T(8,128)(2,1)S(1)} %bitcast.47), channel_id=1, source_target_pairs={{0,16},{16,0},{1,17},{17,1},{2,18},{18,2},{3,19},{19,3},{4,20},{20... | collective-permute-start | bytes 1572872 | tf_op jit(solution)/shard_map/ppermute | solution.py:67
  64.4 35.0 %copy-start.3 = (f32[512]{0:T(512)S(1)}, f32[512]{0:T(512)}, u32[]{:S(2)}) copy-start(f32[512]{0:T(512)} %param.16) | copy-start | bytes 6148
  65.4 32.8 %all-to-all-start.1 = ((bf16[16,1,32,512]{3,2,1,0:T(8,128)(2,1)}), bf16[16,1,32,512]{3,2,1,0:T(8,128)(2,1)S(1)}, u32[]{:S(2)}, u32[]{:S(2)}) async-start(bf16[16,1,32,512]{3,2,1,0:T(8,128)(2,1)} %bitcast.18), calls=%async_computation.1 | async-start | bytes 1048576 | tf_op jit(solution)/shard_map/all_to_all | solution.py:30
  102.4 121.6 %all-to-all-start.2 = ((f32[32,1,32]{2,1,0:T(1,128)}), f32[32,1,32]{2,1,0:T(1,128)S(1)}, u32[]{:S(2)}, u32[]{:S(2)}) async-start(f32[32,1,32]{2,1,0:T(1,128)} %broadcast_in_dim.38), calls=%async_computation.2 | async-start | bytes 32768 | tf_op jit(solution)/shard_map/all_to_all | solution.py:9

commit v2 on v1

--- a/solution.py
+++ b/solution.py
@@ -84,9 +84,32 @@
     ).astype(jnp.bfloat16)
     grad_msg = jnp.einsum("na,nb->ab", message, pre_grad, preferred_element_type=jnp.float32)
     grad_self = jnp.einsum("na,nb->ab", node_feats, pre_grad, preferred_element_type=jnp.float32)
-    grad_msg, grad_self = lax.psum((grad_msg, grad_self), (*WIDE, "loop"))
-    out_logits = gather_directly(logits, WIDE, 0)
-    return (out_logits, grad_msg.astype(jnp.bfloat16), grad_self.astype(jnp.bfloat16))
+    loop_pos = lax.axis_index("loop")
+    all_logits = jnp.zeros((lax.axis_size("loop") * rows_dev,), jnp.float32)
+    all_logits = lax.dynamic_update_slice_in_dim(
+        all_logits, logits, loop_pos * rows_dev + wide_pos * share_rows, 0
+    ).reshape(-1, feat_width)
+    logit_hi = all_logits.astype(jnp.bfloat16).astype(jnp.float32)
+    logit_rest = all_logits - logit_hi
+    logit_mid = logit_rest.astype(jnp.bfloat16).astype(jnp.float32)
+    logit_lo = (logit_rest - logit_mid).astype(jnp.bfloat16).astype(jnp.float32)
+    msg_rows, self_rows = lax.psum(
+        (
+            jnp.concatenate([grad_msg, logit_hi, logit_mid], axis=0),
+            jnp.concatenate([grad_self, logit_lo], axis=0),
+        ),
+        (*WIDE, "loop"),
+    )
+    msg_rows = msg_rows.astype(jnp.bfloat16)
+    self_rows = self_rows.astype(jnp.bfloat16)
+    parts = logit_hi.shape[0]
+    all_logits = (
+        msg_rows[feat_width : feat_width + parts].astype(jnp.float32)
+        + msg_rows[feat_width + parts :].astype(jnp.float32)
+        + self_rows[feat_width:].astype(jnp.float32)
+    ).reshape(-1)
+    out_logits = lax.dynamic_slice_in_dim(all_logits, loop_pos * rows_dev, rows_dev, 0)
+    return (out_logits, msg_rows[:feat_width], self_rows[:feat_width])
 
 
 def solution(mesh):

time: 226 us -> 219 us (0.969)
  starting transfers between devices: 33.4 us -> 27.6 us
  blocking collectives: 116 us -> 111 us
    all_to_all x2 -> x1, starting transfers between devices: 16.3 us -> 10.5 us  [copy_for_each(): return lax.all_to_all(copies, axis, split_axis=0, concat_axis=0, tiled=True)]
    psum x1, blocking collectives: 116 us -> 111 us  [body(): lax.psum((jnp.concatenate([grad_msg, logit_hi, logit_mid], axis=0), jnp.c...]
    all_to_all x2 -> x1, waiting for transfers between devices: 40.8 us -> 40.8 us  [copy_for_each(): return lax.all_to_all(copies, axis, split_axis=0, concat_axis=0, tiled=True)]
  transfers between devices with their start and end apart: 4 -> 3, of which waited for: 3 -> 3; matrix products, arithmetic and copies ran while one was open for 0% -> 0% of each run, Pallas kernels for 0% -> 0%
where the time goes in v2:
time: 219 us; the launch traced here: 218 us
  blocking collectives  111 us (51%)
  waiting for transfers between devices  62.4 us (28%)
  starting transfers between devices  27.6 us (13%)
  local copies, waits for them, and re-layouts  6.68 us (3%)
  matrix products  6.31 us (3%)
  other arithmetic  3.03 us (1%)
    psum x1, blocking collectives, body(): lax.psum((jnp.concatenate([grad_msg, logit_hi, logit_mid], axis=0), jnp.c...  111 us
    all_to_all x1, waiting for transfers between devices, copy_for_each(): return lax.all_to_all(copies, axis, split_axis=0, concat_axis=0, tiled=True)  40.8 us
    all_to_all x1, waiting for transfers between devices, sum_at_owner(): lax.all_to_all(in_blocks(value, dim, devices), axis, 0, 0, tiled=True)  20.1 us
    all_to_all x1, starting transfers between devices, sum_at_owner(): lax.all_to_all(in_blocks(value, dim, devices), axis, 0, 0, tiled=True)  12.8 us
    all_to_all x1, starting transfers between devices, copy_for_each(): return lax.all_to_all(copies, axis, split_axis=0, concat_axis=0, tiled=True)  10.5 us
  transfers between devices with their start and end apart: 3, of which 3 were waited for; matrix products, arithmetic and copies ran while one was open for 0% of the time, Pallas kernels for 0%

profile of v2, /device:TPU:1, one launch (start us, length us, event | category | flops | bytes accessed | tf_op | source)
XLA Modules:
  0.0 218.4 jit_solution(7590164502829743196)
XLA Ops:
  0.7 1.0 fusion.5
  1.6 1.5 broadcast_in_dim.36
  3.2 10.5 %all-to-all-start = ((bf16[16,1,128,512]{3,2,1,0:T(8,128)(2,1)}), bf16[16,1,128,512]{3,2,1,0:T(8,128)(2,1)S(1)}, u32[]{:S(2)}, u32[]{:S(2)}) async-start(bf16[16,1,128,512]{3,2,1,0:T(8,128)(2,1)} %broadcast_in_dim.36), calls=%async_computation | async-start | bytes 4194304 | tf_op jit(solution)/shard_map/all_to_all | solution.py:9
  14.4 40.8 %all-to-all-done = bf16[16,1,128,512]{3,2,1,0:T(8,128)(2,1)S(1)} async-done(((bf16[16,1,128,512]{3,2,1,0:T(8,128)(2,1)}), bf16[16,1,128,512]{3,2,1,0:T(8,128)(2,1)S(1)}, u32[]{:S(2)}, u32[]{:S(2)}) %all-to-all-start) | async-done | bytes 2097184 | tf_op jit(solution)/shard_map/all_to_all | solution.py:9
  55.2 0.6 gather_fusion
  55.8 0.4 convolution_bitcast_fusion
  56.2 0.5 copy.24
  56.9 1.4 convolution_convert_fusion
  58.5 4.3 %collective-permute-start = (bf16[8,2,32,512]{3,2,1,0:T(8,128)(2,1)S(1)}, bf16[8,2,32,512]{3,2,1,0:T(8,128)(2,1)S(1)}, u32[]{:S(2)}, u32[]{:S(2)}) collective-permute-start(bf16[8,2,32,512]{3,2,1,0:T(8,128)(2,1)S(1)} %bitcast.50), channel_id=1, source_target_pairs={{0,16},{16,0},{1,17},{17,1},{2,18},{18,2},{3,19},{19,3},{4,20},{20... | collective-permute-start | bytes 1572872 | tf_op jit(solution)/shard_map/ppermute | solution.py:67
  62.8 1.5 collective-permute-done
  64.4 1.0 fusion
  65.4 12.8 %all-to-all-start.1 = ((bf16[16,1,32,512]{3,2,1,0:T(8,128)(2,1)}), bf16[16,1,32,512]{3,2,1,0:T(8,128)(2,1)S(1)}, u32[]{:S(2)}, u32[]{:S(2)}) async-start(bf16[16,1,32,512]{3,2,1,0:T(8,128)(2,1)} %bitcast.18), calls=%async_computation.1 | async-start | bytes 1048576 | tf_op jit(solution)/shard_map/all_to_all | solution.py:30
  78.2 20.1 %all-to-all-done.1 = bf16[16,1,32,512]{3,2,1,0:T(8,128)(2,1)S(1)} async-done(((bf16[16,1,32,512]{3,2,1,0:T(8,128)(2,1)}), bf16[16,1,32,512]{3,2,1,0:T(8,128)(2,1)S(1)}, u32[]{:S(2)}, u32[]{:S(2)}) %all-to-all-start.1) | async-done | bytes 524320 | tf_op jit(solution)/shard_map/all_to_all | solution.py:30
  98.5 1.0 convolution_add_fusion
  99.5 0.9 divide_subtract_fusion
  100.5 0.4 fusion.27
  100.8 2.1 fusion.12
  102.9 0.2 dynamic_update_slice.3
  103.3 1.1 copy-done.1
  104.5 110.9 %all-reduce.2 = (bf16[544,512]{1,0:T(8,128)(2,1)}, bf16[576,512]{1,0:T(8,128)(2,1)S(1)}) all-reduce(f32[544,512]{1,0:T(8,128)S(1)} %pad_maximum_fusion.1, f32[576,512]{1,0:T(8,128)S(1)} %pad_maximum_fusion), channel_id=1, replica_groups=mesh['wy'=8,'wz'=2,'wc'=2,'loop'=16] {'wy','wz','wc','loop'}, use_global_device_ids=true, to_apply=%region_2.3 | all-reduce | flops 573440 | bytes 3440640 | tf_op jit(solution)/shard_map/psum | solution.py:96
  215.4 0.8 slice.34
  216.2 0.8 add_bitcast_fusion
  217.0 0.8 slice.35
  217.8 0.6 dynamic_slice.20
  (29 shorter events, 0.9 us)
Async XLA Ops:
  0.6 97.7 %copy-start = (bf16[512,512]{1,0:T(8,128)(2,1)S(1)}, bf16[512,512]{1,0:T(8,128)(2,1)}, u32[]{:S(2)}) copy-start(bf16[512,512]{1,0:T(8,128)(2,1)} %param.14) | copy-start | bytes 1572868
  3.2 11.2 %copy-start.7 = (s32[1,1,4]{2,1,0:T(1,128)S(1)}, s32[1,1,4]{2,1,0:T(1,128)}, u32[]{:S(2)}) copy-start(s32[1,1,4]{2,1,0:T(1,128)} %param.12) | copy-start | bytes 52
  3.2 52.6 %copy-start.4 = (bf16[1,1,4,128,128]{4,3,2,1,0:T(8,128)(2,1)S(1)}, bf16[1,1,4,128,128]{4,3,2,1,0:T(8,128)(2,1)}, u32[]{:S(2)}) copy-start(bf16[1,1,4,128,128]{4,3,2,1,0:T(8,128)(2,1)} %param.10) | copy-start | bytes 393220
  3.2 52.0 %all-to-all-start = ((bf16[16,1,128,512]{3,2,1,0:T(8,128)(2,1)}), bf16[16,1,128,512]{3,2,1,0:T(8,128)(2,1)S(1)}, u32[]{:S(2)}, u32[]{:S(2)}) async-start(bf16[16,1,128,512]{3,2,1,0:T(8,128)(2,1)} %broadcast_in_dim.36), calls=%async_computation | async-start | bytes 4194304 | tf_op jit(solution)/shard_map/all_to_all | solution.py:9
  56.2 0.7 copy-start.6
  58.5 5.8 %collective-permute-start = (bf16[8,2,32,512]{3,2,1,0:T(8,128)(2,1)S(1)}, bf16[8,2,32,512]{3,2,1,0:T(8,128)(2,1)S(1)}, u32[]{:S(2)}, u32[]{:S(2)}) collective-permute-start(bf16[8,2,32,512]{3,2,1,0:T(8,128)(2,1)S(1)} %bitcast.50), channel_id=1, source_target_pairs={{0,16},{16,0},{1,17},{17,1},{2,18},{18,2},{3,19},{19,3},{4,20},{20... | collective-permute-start | bytes 1572872 | tf_op jit(solution)/shard_map/ppermute | solution.py:67
  65.4 33.2 %copy-start.3 = (bf16[512,512]{1,0:T(8,128)(2,1)S(1)}, bf16[512,512]{1,0:T(8,128)(2,1)}, u32[]{:S(2)}) copy-start(bf16[512,512]{1,0:T(8,128)(2,1)} %param.15) | copy-start | bytes 1572868
  65.4 32.9 %all-to-all-start.1 = ((bf16[16,1,32,512]{3,2,1,0:T(8,128)(2,1)}), bf16[16,1,32,512]{3,2,1,0:T(8,128)(2,1)S(1)}, u32[]{:S(2)}, u32[]{:S(2)}) async-start(bf16[16,1,32,512]{3,2,1,0:T(8,128)(2,1)} %bitcast.18), calls=%async_computation.1 | async-start | bytes 1048576 | tf_op jit(solution)/shard_map/all_to_all | solution.py:30
  78.1 21.4 %copy-start.5 = (f32[512]{0:T(512)S(1)}, f32[512]{0:T(512)}, u32[]{:S(2)}) copy-start(f32[512]{0:T(512)} %param.16) | copy-start | bytes 6148
  103.2 1.2 copy-start.1
  215.4 1.6 copy-start.2

commit v3 on v1

--- a/solution.py
+++ b/solution.py
@@ -84,9 +84,23 @@
     ).astype(jnp.bfloat16)
     grad_msg = jnp.einsum("na,nb->ab", message, pre_grad, preferred_element_type=jnp.float32)
     grad_self = jnp.einsum("na,nb->ab", node_feats, pre_grad, preferred_element_type=jnp.float32)
-    grad_msg, grad_self = lax.psum((grad_msg, grad_self), (*WIDE, "loop"))
-    out_logits = gather_directly(logits, WIDE, 0)
-    return (out_logits, grad_msg.astype(jnp.bfloat16), grad_self.astype(jnp.bfloat16))
+    loop_pos = lax.axis_index("loop")
+    all_logits = jnp.zeros((lax.axis_size("loop") * rows_dev,), jnp.float32)
+    all_logits = lax.dynamic_update_slice_in_dim(
+        all_logits, logits, loop_pos * rows_dev + wide_pos * share_rows, 0
+    ).reshape(-1, feat_width)
+    logit_hi = all_logits.astype(jnp.bfloat16).astype(jnp.float32)
+    logit_rest = all_logits - logit_hi
+    logit_mid = logit_rest.astype(jnp.bfloat16).astype(jnp.float32)
+    logit_lo = (logit_rest - logit_mid).astype(jnp.bfloat16).astype(jnp.float32)
+    logit_parts = jnp.concatenate([logit_hi, logit_mid, logit_lo], axis=0)
+    grad_msg, grad_self, logit_parts = lax.psum((grad_msg, grad_self, logit_parts), (*WIDE, "loop"))
+    grad_msg = grad_msg.astype(jnp.bfloat16)
+    grad_self = grad_self.astype(jnp.bfloat16)
+    logit_parts = logit_parts.astype(jnp.bfloat16).astype(jnp.float32).reshape(3, -1)
+    all_logits = logit_parts[0] + logit_parts[1] + logit_parts[2]
+    out_logits = lax.dynamic_slice_in_dim(all_logits, loop_pos * rows_dev, rows_dev, 0)
+    return (out_logits, grad_msg, grad_self)
 
 
 def solution(mesh):

time: 226 us -> 214 us (0.947)
  starting transfers between devices: 33.4 us -> 27.6 us
  blocking collectives: 116 us -> 111 us
    all_to_all x2 -> x1, starting transfers between devices: 16.3 us -> 10.5 us  [copy_for_each(): return lax.all_to_all(copies, axis, split_axis=0, concat_axis=0, tiled=True)]
    psum x1, blocking collectives: 116 us -> 111 us  [body(): lax.psum((grad_msg, grad_self, logit_parts), (*WIDE, 'loop'))]
    all_to_all x2 -> x1, waiting for transfers between devices: 40.8 us -> 40.8 us  [copy_for_each(): return lax.all_to_all(copies, axis, split_axis=0, concat_axis=0, tiled=True)]
  transfers between devices with their start and end apart: 4 -> 3, of which waited for: 3 -> 3; matrix products, arithmetic and copies ran while one was open for 0% -> 0% of each run, Pallas kernels for 0% -> 0%
where the time goes in v3:
time: 214 us
  blocking collectives  111 us (52%)
  waiting for transfers between devices  62.4 us (29%)
  starting transfers between devices  27.6 us (13%)
  matrix products  5.34 us (2%)
  local copies, waits for them, and re-layouts  3.82 us (2%)
  other arithmetic  2.14 us (1%)
    psum x1, blocking collectives, body(): lax.psum((grad_msg, grad_self, logit_parts), (*WIDE, 'loop'))  111 us
    all_to_all x1, waiting for transfers between devices, copy_for_each(): return lax.all_to_all(copies, axis, split_axis=0, concat_axis=0, tiled=True)  40.8 us
    all_to_all x1, waiting for transfers between devices, sum_at_owner(): lax.all_to_all(in_blocks(value, dim, devices), axis, 0, 0, tiled=True)  20.1 us
    all_to_all x1, starting transfers between devices, sum_at_owner(): lax.all_to_all(in_blocks(value, dim, devices), axis, 0, 0, tiled=True)  12.6 us
    all_to_all x1, starting transfers between devices, copy_for_each(): return lax.all_to_all(copies, axis, split_axis=0, concat_axis=0, tiled=True)  10.5 us
    ppermute x1, starting transfers between devices, body(): got = lax.ppermute(give, 'wc', [(0, 1), (1, 0)])  4.44 us
  transfers between devices with their start and end apart: 3, of which 3 were waited for; matrix products, arithmetic and copies ran while one was open for 0% of the time, Pallas kernels for 0%

profile of v3, /device:TPU:1, one launch (start us, length us, event | category | flops | bytes accessed | tf_op | source)
XLA Modules:
  0.0 213.9 jit_solution(3926937292707845144)
XLA Ops:
  0.7 1.0 fusion.5
  1.6 1.5 broadcast_in_dim.37
  3.2 10.5 %all-to-all-start = ((bf16[16,1,128,512]{3,2,1,0:T(8,128)(2,1)}), bf16[16,1,128,512]{3,2,1,0:T(8,128)(2,1)S(1)}, u32[]{:S(2)}, u32[]{:S(2)}) async-start(bf16[16,1,128,512]{3,2,1,0:T(8,128)(2,1)} %broadcast_in_dim.37), calls=%async_computation | async-start | bytes 4194304 | tf_op jit(solution)/shard_map/all_to_all | solution.py:9
  14.4 40.8 %all-to-all-done = bf16[16,1,128,512]{3,2,1,0:T(8,128)(2,1)S(1)} async-done(((bf16[16,1,128,512]{3,2,1,0:T(8,128)(2,1)}), bf16[16,1,128,512]{3,2,1,0:T(8,128)(2,1)S(1)}, u32[]{:S(2)}, u32[]{:S(2)}) %all-to-all-start) | async-done | bytes 2097184 | tf_op jit(solution)/shard_map/all_to_all | solution.py:9
  55.2 0.6 gather_fusion
  55.8 0.4 convolution_bitcast_fusion
  56.3 0.5 copy.24
  56.8 1.4 convolution_convert_fusion
  58.1 0.1 constant_dynamic-slice_fusion.1
  58.2 0.2 copy.35
  58.4 4.4 %collective-permute-start = (bf16[8,2,32,512]{3,2,1,0:T(8,128)(2,1)S(1)}, bf16[8,2,32,512]{3,2,1,0:T(8,128)(2,1)S(1)}, u32[]{:S(2)}, u32[]{:S(2)}) collective-permute-start(bf16[8,2,32,512]{3,2,1,0:T(8,128)(2,1)S(1)} %bitcast.50), channel_id=1, source_target_pairs={{0,16},{16,0},{1,17},{17,1},{2,18},{18,2},{3,19},{19,3},{4,20},{20... | collective-permute-start | bytes 1572872 | tf_op jit(solution)/shard_map/ppermute | solution.py:67
  62.9 1.5 collective-permute-done
  64.4 1.0 fusion
  65.4 12.6 %all-to-all-start.1 = ((bf16[16,1,32,512]{3,2,1,0:T(8,128)(2,1)}), bf16[16,1,32,512]{3,2,1,0:T(8,128)(2,1)S(1)}, u32[]{:S(2)}, u32[]{:S(2)}) async-start(bf16[16,1,32,512]{3,2,1,0:T(8,128)(2,1)} %bitcast.18), calls=%async_computation.1 | async-start | bytes 1048576 | tf_op jit(solution)/shard_map/all_to_all | solution.py:30
  78.0 20.1 %all-to-all-done.1 = bf16[16,1,32,512]{3,2,1,0:T(8,128)(2,1)S(1)} async-done(((bf16[16,1,32,512]{3,2,1,0:T(8,128)(2,1)}), bf16[16,1,32,512]{3,2,1,0:T(8,128)(2,1)S(1)}, u32[]{:S(2)}, u32[]{:S(2)}) %all-to-all-start.1) | async-done | bytes 524320 | tf_op jit(solution)/shard_map/all_to_all | solution.py:30
  98.1 0.1 reduce_sum.12
  98.2 0.2 fusion.29
  98.4 1.0 convolution_add_fusion
  99.4 0.9 divide_subtract_fusion
  100.3 0.4 fusion.28
  100.7 1.1 fusion.13
  101.8 0.3 dynamic_update_slice.3
  102.2 111.0 %all-reduce.2 = (bf16[96,512]{1,0:T(8,128)(2,1)S(1)}, bf16[512,512]{1,0:T(8,128)(2,1)}, bf16[512,512]{1,0:T(8,128)(2,1)}) all-reduce(f32[96,512]{1,0:T(8,128)S(1)} %pad_maximum_fusion, f32[512,512]{1,0:T(8,128)S(1)} %fusion.28, f32[512,512]{1,0:T(8,128)S(1)} %fusion.13), channel_id=1, replica_groups=mesh['wy'=8,'wz'=2,'wc'=2,'loop'=16] {'wy','wz','wc','loop'}, use_global_device_ids=true, to_apply=%region_1.2 | all-reduce | flops 573440 | bytes 3440640 | tf_op jit(solution)/shard_map/psum | solution.py:97
  213.3 0.6 dynamic_slice.19
  (23 shorter events, 0.2 us)
Async XLA Ops:
  0.6 97.6 %copy-start = (bf16[512,512]{1,0:T(8,128)(2,1)S(1)}, bf16[512,512]{1,0:T(8,128)(2,1)}, u32[]{:S(2)}) copy-start(bf16[512,512]{1,0:T(8,128)(2,1)} %param.14) | copy-start | bytes 1572868
  3.2 11.2 %copy-start.5 = (s32[1,1,4]{2,1,0:T(1,128)S(1)}, s32[1,1,4]{2,1,0:T(1,128)}, u32[]{:S(2)}) copy-start(s32[1,1,4]{2,1,0:T(1,128)} %param.12) | copy-start | bytes 52
  3.2 52.6 %copy-start.2 = (bf16[1,1,4,128,128]{4,3,2,1,0:T(8,128)(2,1)S(1)}, bf16[1,1,4,128,128]{4,3,2,1,0:T(8,128)(2,1)}, u32[]{:S(2)}) copy-start(bf16[1,1,4,128,128]{4,3,2,1,0:T(8,128)(2,1)} %param.10) | copy-start | bytes 393220
  3.2 52.0 %all-to-all-start = ((bf16[16,1,128,512]{3,2,1,0:T(8,128)(2,1)}), bf16[16,1,128,512]{3,2,1,0:T(8,128)(2,1)S(1)}, u32[]{:S(2)}, u32[]{:S(2)}) async-start(bf16[16,1,128,512]{3,2,1,0:T(8,128)(2,1)} %broadcast_in_dim.37), calls=%async_computation | async-start | bytes 4194304 | tf_op jit(solution)/shard_map/all_to_all | solution.py:9
  55.8 0.9 copy-start.4
  58.4 40.0 %copy-start.1 = (bf16[512,512]{1,0:T(8,128)(2,1)S(1)}, bf16[512,512]{1,0:T(8,128)(2,1)}, u32[]{:S(2)}) copy-start(bf16[512,512]{1,0:T(8,128)(2,1)} %param.15) | copy-start | bytes 1572868
  58.4 6.0 %collective-permute-start = (bf16[8,2,32,512]{3,2,1,0:T(8,128)(2,1)S(1)}, bf16[8,2,32,512]{3,2,1,0:T(8,128)(2,1)S(1)}, u32[]{:S(2)}, u32[]{:S(2)}) collective-permute-start(bf16[8,2,32,512]{3,2,1,0:T(8,128)(2,1)S(1)} %bitcast.50), channel_id=1, source_target_pairs={{0,16},{16,0},{1,17},{17,1},{2,18},{18,2},{3,19},{19,3},{4,20},{20... | collective-permute-start | bytes 1572872 | tf_op jit(solution)/shard_map/ppermute | solution.py:67
  64.4 35.0 %copy-start.3 = (f32[512]{0:T(512)S(1)}, f32[512]{0:T(512)}, u32[]{:S(2)}) copy-start(f32[512]{0:T(512)} %param.16) | copy-start | bytes 6148
  65.4 32.8 %all-to-all-start.1 = ((bf16[16,1,32,512]{3,2,1,0:T(8,128)(2,1)}), bf16[16,1,32,512]{3,2,1,0:T(8,128)(2,1)S(1)}, u32[]{:S(2)}, u32[]{:S(2)}) async-start(bf16[16,1,32,512]{3,2,1,0:T(8,128)(2,1)} %bitcast.18), calls=%async_computation.1 | async-start | bytes 1048576 | tf_op jit(solution)/shard_map/all_to_all | solution.py:30

commit v4 on v3

--- a/solution.py
+++ b/solution.py
@@ -66,8 +66,12 @@
     give = lax.dynamic_index_in_dim(by_owner, 1 - core, 2, keepdims=False)
     got = lax.ppermute(give, "wc", [(0, 1), (1, 0)])
     pair_sum = (keep.astype(jnp.float32) + got.astype(jnp.float32)).astype(jnp.bfloat16)
-    pair_sum = pair_sum.reshape(-1, pair_sum.shape[-2], feat_width)
-    message = sum_at_owner(pair_sum, ("wy", "wz"), 0).astype(jnp.bfloat16)
+    half = lax.axis_index("wz")
+    keep = lax.dynamic_index_in_dim(pair_sum, half, 1, keepdims=False)
+    give = lax.dynamic_index_in_dim(pair_sum, 1 - half, 1, keepdims=False)
+    got = lax.ppermute(give, "wz", [(0, 1), (1, 0)])
+    quad_sum = (keep.astype(jnp.float32) + got.astype(jnp.float32)).astype(jnp.bfloat16)
+    message = sum_at_owner(quad_sum, "wy", 0).astype(jnp.bfloat16)
     message = message.reshape(-1, feat_width)
     share_rows = rows_dev // wide_size
     node_feats = lax.dynamic_slice_in_dim(feats, wide_pos * share_rows, share_rows, 0)

time: 214 us -> 220 us (1.028)
  blocking collectives: 111 us -> 118 us
  waiting for transfers between devices: 62.4 us -> 58.9 us
    all_to_all x1, waiting for transfers between devices: 20.1 us -> 10.3 us  [sum_at_owner(): lax.all_to_all(in_blocks(value, dim, devices), axis, 0, 0, tiled=True)]
    ppermute x0 -> x1, starting transfers between devices: none -> 7.89 us  [body(): got = lax.ppermute(give, 'wz', [(0, 1), (1, 0)])]
    psum x1, blocking collectives: 111 us -> 118 us  [body(): lax.psum((grad_msg, grad_self, logit_parts), (*WIDE, 'loop'))]
    ppermute x0 -> x1, waiting for transfers between devices: none -> 6.3 us  [body(): got = lax.ppermute(give, 'wz', [(0, 1), (1, 0)])]
    all_to_all x1, starting transfers between devices: 12.6 us -> 6.82 us  [sum_at_owner(): lax.all_to_all(in_blocks(value, dim, devices), axis, 0, 0, tiled=True)]
  transfers between devices with their start and end apart: 3 -> 4, of which waited for: 3 -> 4; matrix products, arithmetic and copies ran while one was open for 0% -> 0% of each run, Pallas kernels for 0% -> 0%
where the time goes in v4:
time: 220 us
  blocking collectives  118 us (54%)
  waiting for transfers between devices  58.9 us (27%)
  starting transfers between devices  29.5 us (13%)
  matrix products  5.34 us (2%)
  local copies, waits for them, and re-layouts  3.84 us (2%)
    psum x1, blocking collectives, body(): lax.psum((grad_msg, grad_self, logit_parts), (*WIDE, 'loop'))  118 us
    all_to_all x1, waiting for transfers between devices, copy_for_each(): return lax.all_to_all(copies, axis, split_axis=0, concat_axis=0, tiled=True)  40.8 us
    all_to_all x1, starting transfers between devices, copy_for_each(): return lax.all_to_all(copies, axis, split_axis=0, concat_axis=0, tiled=True)  10.5 us
    all_to_all x1, waiting for transfers between devices, sum_at_owner(): lax.all_to_all(in_blocks(value, dim, devices), axis, 0, 0, tiled=True)  10.3 us
    ppermute x1, starting transfers between devices, body(): got = lax.ppermute(give, 'wz', [(0, 1), (1, 0)])  7.89 us
    all_to_all x1, starting transfers between devices, sum_at_owner(): lax.all_to_all(in_blocks(value, dim, devices), axis, 0, 0, tiled=True)  6.82 us
    ppermute x1, waiting for transfers between devices, body(): got = lax.ppermute(give, 'wz', [(0, 1), (1, 0)])  6.3 us
  transfers between devices with their start and end apart: 4, of which 4 were waited for; matrix products, arithmetic and copies ran while one was open for 0% of the time, Pallas kernels for 0%

profile of v4, /device:TPU:1, one launch (start us, length us, event | category | flops | bytes accessed | tf_op | source)
XLA Modules:
  0.0 219.5 jit_solution(15329335522334341801)
XLA Ops:
  0.7 1.0 fusion.9
  1.7 1.5 broadcast_in_dim.37
  3.2 10.5 %all-to-all-start = ((bf16[16,1,128,512]{3,2,1,0:T(8,128)(2,1)}), bf16[16,1,128,512]{3,2,1,0:T(8,128)(2,1)S(1)}, u32[]{:S(2)}, u32[]{:S(2)}) async-start(bf16[16,1,128,512]{3,2,1,0:T(8,128)(2,1)} %broadcast_in_dim.37), calls=%async_computation | async-start | bytes 4194304 | tf_op jit(solution)/shard_map/all_to_all | solution.py:9
  14.4 40.8 %all-to-all-done = bf16[16,1,128,512]{3,2,1,0:T(8,128)(2,1)S(1)} async-done(((bf16[16,1,128,512]{3,2,1,0:T(8,128)(2,1)}), bf16[16,1,128,512]{3,2,1,0:T(8,128)(2,1)S(1)}, u32[]{:S(2)}, u32[]{:S(2)}) %all-to-all-start) | async-done | bytes 2097184 | tf_op jit(solution)/shard_map/all_to_all | solution.py:9
  55.2 0.6 gather_fusion
  55.8 0.4 fusion.3
  56.3 0.5 copy.14
  56.8 1.4 convolution_convert_fusion
  58.4 4.3 %collective-permute-start = (bf16[8,2,32,512]{3,2,0,1:T(8,128)(2,1)S(1)}, bf16[8,2,32,512]{3,2,0,1:T(8,128)(2,1)S(1)}, u32[]{:S(2)}, u32[]{:S(2)}) collective-permute-start(bf16[8,2,32,512]{3,2,0,1:T(8,128)(2,1)S(1)} %bitcast.54), channel_id=1, source_target_pairs={{0,16},{16,0},{1,17},{17,1},{2,18},{18,2},{3,19},{19,3},{4,20},{20... | collective-permute-start | bytes 1572872 | tf_op jit(solution)/shard_map/ppermute | solution.py:67
  62.7 1.5 collective-permute-done
  64.2 0.2 fusion
  64.5 7.9 %collective-permute-start.1 = (bf16[8,32,512]{2,1,0:T(8,128)(2,1)S(1)}, bf16[8,32,512]{2,1,0:T(8,128)(2,1)S(1)}, u32[]{:S(2)}, u32[]{:S(2)}) collective-permute-start(bf16[8,32,512]{2,1,0:T(8,128)(2,1)S(1)} %dynamic-slice_bitcast_fusion), channel_id=1, source_target_pairs={{0,32},{32,0},{1,33},{33,1},{2,34},{34,2},{3,35},{35,3},{4,36},{36... | collective-permute-start | bytes 786440 | tf_op jit(solution)/shard_map/ppermute | solution.py:72
  72.4 6.3 %collective-permute-done.1 = bf16[8,32,512]{2,1,0:T(8,128)(2,1)S(1)} collective-permute-done((bf16[8,32,512]{2,1,0:T(8,128)(2,1)S(1)}, bf16[8,32,512]{2,1,0:T(8,128)(2,1)S(1)}, u32[]{:S(2)}, u32[]{:S(2)}) %collective-permute-start.1) | collective-permute-done | bytes 262176 | tf_op jit(solution)/shard_map/ppermute | solution.py:72
  78.7 0.8 fusion.6
  79.5 6.8 %all-to-all-start.1 = ((bf16[8,1,32,512]{3,2,1,0:T(8,128)(2,1)}), bf16[8,1,32,512]{3,2,1,0:T(8,128)(2,1)S(1)}, u32[]{:S(2)}, u32[]{:S(2)}) async-start(bf16[8,1,32,512]{3,2,1,0:T(8,128)(2,1)} %fusion.6), calls=%async_computation.1 | async-start | bytes 524288 | tf_op jit(solution)/shard_map/all_to_all | solution.py:30
  86.3 10.3 %all-to-all-done.1 = bf16[8,1,32,512]{3,2,1,0:T(8,128)(2,1)S(1)} async-done(((bf16[8,1,32,512]{3,2,1,0:T(8,128)(2,1)}), bf16[8,1,32,512]{3,2,1,0:T(8,128)(2,1)S(1)}, u32[]{:S(2)}, u32[]{:S(2)}) %all-to-all-start.1) | async-done | bytes 262176 | tf_op jit(solution)/shard_map/all_to_all | solution.py:30
  96.6 0.2 fusion.33
  96.8 1.0 convolution_add_fusion
  97.8 0.9 divide_subtract_fusion
  98.7 0.4 fusion.32
  99.1 1.1 fusion.17
  100.2 0.3 dynamic_update_slice.3
  100.6 118.3 %all-reduce.2 = (bf16[96,512]{1,0:T(8,128)(2,1)S(1)}, bf16[512,512]{1,0:T(8,128)(2,1)}, bf16[512,512]{1,0:T(8,128)(2,1)}) all-reduce(f32[96,512]{1,0:T(8,128)S(1)} %pad_maximum_fusion, f32[512,512]{1,0:T(8,128)S(1)} %fusion.32, f32[512,512]{1,0:T(8,128)S(1)} %fusion.17), channel_id=1, replica_groups=mesh['wy'=8,'wz'=2,'wc'=2,'loop'=16] {'wy','wz','wc','loop'}, use_global_device_ids=true, to_apply=%region_1.2 | all-reduce | flops 573440 | bytes 3440640 | tf_op jit(solution)/shard_map/psum | solution.py:101
  218.9 0.6 dynamic_slice.28
  (27 shorter events, 0.5 us)
Async XLA Ops:
  0.6 96.0 %copy-start = (bf16[512,512]{1,0:T(8,128)(2,1)S(1)}, bf16[512,512]{1,0:T(8,128)(2,1)}, u32[]{:S(2)}) copy-start(bf16[512,512]{1,0:T(8,128)(2,1)} %param.14) | copy-start | bytes 1572868
  3.2 11.2 %copy-start.5 = (s32[1,1,4]{2,1,0:T(1,128)S(1)}, s32[1,1,4]{2,1,0:T(1,128)}, u32[]{:S(2)}) copy-start(s32[1,1,4]{2,1,0:T(1,128)} %param.12) | copy-start | bytes 52
  3.2 52.6 %copy-start.2 = (bf16[1,1,4,128,128]{4,3,2,1,0:T(8,128)(2,1)S(1)}, bf16[1,1,4,128,128]{4,3,2,1,0:T(8,128)(2,1)}, u32[]{:S(2)}) copy-start(bf16[1,1,4,128,128]{4,3,2,1,0:T(8,128)(2,1)} %param.10) | copy-start | bytes 393220
  3.2 52.0 %all-to-all-start = ((bf16[16,1,128,512]{3,2,1,0:T(8,128)(2,1)}), bf16[16,1,128,512]{3,2,1,0:T(8,128)(2,1)S(1)}, u32[]{:S(2)}, u32[]{:S(2)}) async-start(bf16[16,1,128,512]{3,2,1,0:T(8,128)(2,1)} %broadcast_in_dim.37), calls=%async_computation | async-start | bytes 4194304 | tf_op jit(solution)/shard_map/all_to_all | solution.py:9
  55.8 0.9 copy-start.4
  58.4 5.8 %collective-permute-start = (bf16[8,2,32,512]{3,2,0,1:T(8,128)(2,1)S(1)}, bf16[8,2,32,512]{3,2,0,1:T(8,128)(2,1)S(1)}, u32[]{:S(2)}, u32[]{:S(2)}) collective-permute-start(bf16[8,2,32,512]{3,2,0,1:T(8,128)(2,1)S(1)} %bitcast.54), channel_id=1, source_target_pairs={{0,16},{16,0},{1,17},{17,1},{2,18},{18,2},{3,19},{19,3},{4,20},{20... | collective-permute-start | bytes 1572872 | tf_op jit(solution)/shard_map/ppermute | solution.py:67
  64.2 32.6 %copy-start.1 = (bf16[512,512]{1,0:T(8,128)(2,1)S(1)}, bf16[512,512]{1,0:T(8,128)(2,1)}, u32[]{:S(2)}) copy-start(bf16[512,512]{1,0:T(8,128)(2,1)} %param.15) | copy-start | bytes 1572868
  64.5 33.3 %copy-start.3 = (f32[512]{0:T(512)S(1)}, f32[512]{0:T(512)}, u32[]{:S(2)}) copy-start(f32[512]{0:T(512)} %param.16) | copy-start | bytes 6148
  64.5 14.2 %collective-permute-start.1 = (bf16[8,32,512]{2,1,0:T(8,128)(2,1)S(1)}, bf16[8,32,512]{2,1,0:T(8,128)(2,1)S(1)}, u32[]{:S(2)}, u32[]{:S(2)}) collective-permute-start(bf16[8,32,512]{2,1,0:T(8,128)(2,1)S(1)} %dynamic-slice_bitcast_fusion), channel_id=1, source_target_pairs={{0,32},{32,0},{1,33},{33,1},{2,34},{34,2},{3,35},{35,3},{4,36},{36... | collective-permute-start | bytes 786440 | tf_op jit(solution)/shard_map/ppermute | solution.py:72
  79.5 17.1 %all-to-all-start.1 = ((bf16[8,1,32,512]{3,2,1,0:T(8,128)(2,1)}), bf16[8,1,32,512]{3,2,1,0:T(8,128)(2,1)S(1)}, u32[]{:S(2)}, u32[]{:S(2)}) async-start(bf16[8,1,32,512]{3,2,1,0:T(8,128)(2,1)} %fusion.6), calls=%async_computation.1 | async-start | bytes 524288 | tf_op jit(solution)/shard_map/all_to_all | solution.py:30

commit v5 on v1

--- a/solution.py
+++ b/solution.py
@@ -84,9 +84,33 @@
     ).astype(jnp.bfloat16)
     grad_msg = jnp.einsum("na,nb->ab", message, pre_grad, preferred_element_type=jnp.float32)
     grad_self = jnp.einsum("na,nb->ab", node_feats, pre_grad, preferred_element_type=jnp.float32)
-    grad_msg, grad_self = lax.psum((grad_msg, grad_self), (*WIDE, "loop"))
-    out_logits = gather_directly(logits, WIDE, 0)
-    return (out_logits, grad_msg.astype(jnp.bfloat16), grad_self.astype(jnp.bfloat16))
+    swap = [(0, 1), (1, 0)]
+    others = ("wy", "wz", "loop")
+    peers = lax.axis_size(others)
+    both_grads = jnp.stack([grad_msg, grad_self]).reshape(2, -1)
+    mine = lax.dynamic_index_in_dim(both_grads, core, 0, keepdims=False)
+    theirs = lax.dynamic_index_in_dim(both_grads, 1 - core, 0, keepdims=False)
+    half_sum = mine + lax.ppermute(theirs, "wc", swap)
+    pieces = lax.all_to_all(half_sum.astype(jnp.bfloat16).reshape(peers, -1), others, 0, 0, tiled=True)
+    reduced = jnp.sum(pieces.astype(jnp.float32), axis=0).astype(jnp.bfloat16)
+    logit_hi = logits.astype(jnp.bfloat16)
+    logit_rest = logits - logit_hi.astype(jnp.float32)
+    logit_mid = logit_rest.astype(jnp.bfloat16)
+    logit_lo = (logit_rest - logit_mid.astype(jnp.float32)).astype(jnp.bfloat16)
+    payload = jnp.concatenate([reduced, logit_hi, logit_mid, logit_lo])
+    gathered = lax.all_to_all(jnp.broadcast_to(payload, (peers, payload.size)), others, 0, 0, tiled=True)
+    from_sibling = lax.ppermute(gathered, "wc", swap)
+    by_core = jnp.where(core == 0, jnp.stack([gathered, from_sibling]), jnp.stack([from_sibling, gathered]))
+    chunk = reduced.size
+    grads = by_core[:, :, :chunk].reshape(2, feat_width, feat_width)
+    parts = by_core[:, :, chunk:].reshape(
+        2, lax.axis_size("wy"), lax.axis_size("wz"), lax.axis_size("loop"), 3, share_rows
+    )
+    parts = lax.dynamic_index_in_dim(parts, lax.axis_index("loop"), 3, keepdims=False)
+    parts = jnp.transpose(parts, (1, 2, 0, 3, 4)).astype(jnp.float32)
+    out_logits = (parts[:, :, :, 0] + parts[:, :, :, 1] + parts[:, :, :, 2]).reshape(-1)
+    grad_msg, grad_self = grads[0], grads[1]
+    return (out_logits, grad_msg, grad_self)
 
 
 def solution(mesh):

time: 226 us -> 210 us (0.929)
  blocking collectives: 116 us -> 64.9 us
  other arithmetic: 2.77 us -> 17.5 us
  local copies, waits for them, and re-layouts: 4.69 us -> 15.2 us
  starting transfers between devices: 33.4 us -> 38.2 us
  waiting for transfers between devices: 62.4 us -> 66.1 us
    psum x1 -> x0, blocking collectives: 116 us -> none  [body(): grad_msg, grad_self = lax.psum((grad_msg, grad_self), (*WIDE, 'loop'))]
    all_to_all x0 -> x2, blocking collectives: none -> 64.9 us  [the longest x1 35.4 us: body(): lax.all_to_all(half_sum.astype(jnp.bfloat16).reshape(peers, -1), others,...]
    ppermute x0 -> x2, starting transfers between devices: none -> 10.6 us  [the longest x1 6.12 us: body(): from_sibling = lax.ppermute(gathered, 'wc', swap)]
    another operation x0 -> x1, other arithmetic: none -> 6.01 us  [body(): both_grads = jnp.stack([grad_msg, grad_self]).reshape(2, -1)]
    all_to_all x2 -> x1, starting transfers between devices: 16.3 us -> 10.5 us  [copy_for_each(): return lax.all_to_all(copies, axis, split_axis=0, concat_axis=0, tiled=True)]
    unnamed x12 -> x20, local copies, waits for them, and re-layouts: 0.04 us -> 5.56 us
    broadcast_in_dim x0 -> x1, other arithmetic: none -> 4.38 us  [body(): jnp.broadcast_to(payload, (peers, payload.size))]
    ppermute x0 -> x2, waiting for transfers between devices: none -> 3.66 us  [the longest x1 2.08 us: body(): half_sum = mine + lax.ppermute(theirs, 'wc', swap)]
  transfers between devices with their start and end apart: 4 -> 5, of which waited for: 3 -> 5; matrix products, arithmetic and copies ran while one was open for 0% -> 0% of each run, Pallas kernels for 0% -> 0%
where the time goes in v5:
time: 210 us; the launch traced here: 209 us
  waiting for transfers between devices  66.1 us (31%)
  blocking collectives  64.9 us (31%)
  starting transfers between devices  38.2 us (18%)
  other arithmetic  17.5 us (8%)
  local copies, waits for them, and re-layouts  15.2 us (7%)
  matrix products  5.32 us (3%)
    all_to_all x1, waiting for transfers between devices, copy_for_each(): return lax.all_to_all(copies, axis, split_axis=0, concat_axis=0, tiled=True)  40.8 us
    all_to_all x1, blocking collectives, body(): lax.all_to_all(half_sum.astype(jnp.bfloat16).reshape(peers, -1), others,...  35.4 us
    all_to_all x1, blocking collectives, body(): lax.all_to_all(jnp.broadcast_to(payload, (peers, payload.size)), others,...  29.5 us
    all_to_all x1, waiting for transfers between devices, sum_at_owner(): lax.all_to_all(in_blocks(value, dim, devices), axis, 0, 0, tiled=True)  20.1 us
    all_to_all x1, starting transfers between devices, sum_at_owner(): lax.all_to_all(in_blocks(value, dim, devices), axis, 0, 0, tiled=True)  12.8 us
    all_to_all x1, starting transfers between devices, copy_for_each(): return lax.all_to_all(copies, axis, split_axis=0, concat_axis=0, tiled=True)  10.5 us
    ppermute x1, starting transfers between devices, body(): from_sibling = lax.ppermute(gathered, 'wc', swap)  6.12 us
    another operation x1, other arithmetic, body(): both_grads = jnp.stack([grad_msg, grad_self]).reshape(2, -1)  6.01 us
  transfers between devices with their start and end apart: 5, of which 5 were waited for; matrix products, arithmetic and copies ran while one was open for 0% of the time, Pallas kernels for 0%

profile of v5, /device:TPU:1, one launch (start us, length us, event | category | flops | bytes accessed | tf_op | source)
XLA Modules:
  0.0 208.9 jit_solution(10483754656471368057)
XLA Ops:
  0.7 1.0 fusion.7
  1.6 1.5 broadcast_in_dim.36
  3.2 10.5 %all-to-all-start = ((bf16[16,1,128,512]{3,2,1,0:T(8,128)(2,1)}), bf16[16,1,128,512]{3,2,1,0:T(8,128)(2,1)S(1)}, u32[]{:S(2)}, u32[]{:S(2)}) async-start(bf16[16,1,128,512]{3,2,1,0:T(8,128)(2,1)} %broadcast_in_dim.36), calls=%async_computation | async-start | bytes 4194304 | tf_op jit(solution)/shard_map/all_to_all | solution.py:9
  14.4 40.8 %all-to-all-done = bf16[16,1,128,512]{3,2,1,0:T(8,128)(2,1)S(1)} async-done(((bf16[16,1,128,512]{3,2,1,0:T(8,128)(2,1)}), bf16[16,1,128,512]{3,2,1,0:T(8,128)(2,1)S(1)}, u32[]{:S(2)}, u32[]{:S(2)}) %all-to-all-start) | async-done | bytes 2097184 | tf_op jit(solution)/shard_map/all_to_all | solution.py:9
  56.9 1.4 convolution_convert_fusion
  58.5 4.3 %collective-permute-start = (bf16[8,2,32,512]{3,2,1,0:T(8,128)(2,1)S(1)}, bf16[8,2,32,512]{3,2,1,0:T(8,128)(2,1)S(1)}, u32[]{:S(2)}, u32[]{:S(2)}) collective-permute-start(bf16[8,2,32,512]{3,2,1,0:T(8,128)(2,1)S(1)} %bitcast.74), channel_id=1, source_target_pairs={{0,16},{16,0},{1,17},{17,1},{2,18},{18,2},{3,19},{19,3},{4,20},{20... | collective-permute-start | bytes 1572872 | tf_op jit(solution)/shard_map/ppermute | solution.py:67
  62.9 1.5 collective-permute-done
  64.4 1.0 fusion.2
  65.4 12.8 %all-to-all-start.1 = ((bf16[16,1,32,512]{3,2,1,0:T(8,128)(2,1)}), bf16[16,1,32,512]{3,2,1,0:T(8,128)(2,1)S(1)}, u32[]{:S(2)}, u32[]{:S(2)}) async-start(bf16[16,1,32,512]{3,2,1,0:T(8,128)(2,1)} %bitcast.18), calls=%async_computation.1 | async-start | bytes 1048576 | tf_op jit(solution)/shard_map/all_to_all | solution.py:30
  78.2 20.1 %all-to-all-done.1 = bf16[16,1,32,512]{3,2,1,0:T(8,128)(2,1)S(1)} async-done(((bf16[16,1,32,512]{3,2,1,0:T(8,128)(2,1)}), bf16[16,1,32,512]{3,2,1,0:T(8,128)(2,1)S(1)}, u32[]{:S(2)}, u32[]{:S(2)}) %all-to-all-start.1) | async-done | bytes 524320 | tf_op jit(solution)/shard_map/all_to_all | solution.py:30
  100.5 1.1 convolution_bitcast_fusion
  101.9 1.1 copy.60
  103.0 1.1 copy.59
  104.1 6.0 %fusion = (f32[1,262144]{1,0:T(1,128)S(1)}, f32[1,262144]{1,0:T(1,128)S(1)}) fusion(s32[]{:T(128)S(6)} %select_n.77, f32[1,262144]{1,0:T(1,128)S(1)} %bitcast.67, f32[1,262144]{1,0:T(1,128)S(1)} %bitcast.66, s32[]{:T(128)S(6)} %select_n.76), kind=kLoop, calls=%fused_computation.12 | loop fusion | flops 524288 | bytes 4194312 | tf_op jit(solution)/shard_map/stack | solution.py:90
  110.1 4.5 %collective-permute-start.1 = (f32[262144]{0:T(1024)S(1)}, f32[262144]{0:T(1024)S(1)}, u32[]{:S(2)}, u32[]{:S(2)}) collective-permute-start(f32[262144]{0:T(1024)S(1)} %bitcast.72), channel_id=1, source_target_pairs={{0,16},{16,0},{1,17},{17,1},{2,18},{18,2},{3,19},{19,3},{4,20},{20... | collective-permute-start | bytes 3145736 | tf_op jit(solution)/shard_map/ppermute | solution.py:93
  114.6 2.1 collective-permute-done.1
  117.7 3.7 %reduce.4 = bf16[256,1024]{1,0:T(8,128)(2,1)S(1)} reduce(bf16[256,1,1024]{2,1,0:T(2,128)(2,1)S(1)} %all_to_all.24, bf16[]{:T(256)} %broadcast.81), dimensions={1}, to_apply=%all_to_all.24.reduce_sub_computation | reduce | bytes 1048578 | tf_op jit(solution)/shard_map/all_to_all | solution.py:94
  121.7 35.4 %all_to_all.29 = bf16[256,2,512]{2,1,0:T(2,128)(2,1)S(1)} all-to-all(bf16[256,2,512]{2,1,0:T(2,128)(2,1)S(1)} %reshape.161), channel_id=1, replica_groups=mesh['wy'=8,'wz'=2,'wc'=2,'loop'=16] {'wy','wz','loop'}, dimensions={0} | all-to-all | bytes 1048576 | tf_op jit(solution)/shard_map/all_to_all | solution.py:94
  159.2 4.4 %reduce.5 = bf16[256,1120]{1,0:T(8,128)(2,1)S(1)} reduce(bf16[256,1,1120]{2,1,0:T(2,128)(2,1)S(1)} %broadcast_in_dim.38, bf16[]{:T(256)} %broadcast.81), dimensions={1}, to_apply=%broadcast_in_dim.38.reduce_sub_computation | reduce | bytes 1146882 | tf_op jit(solution)/shard_map/broadcast_in_dim | solution.py:101
  164.3 29.5 %all_to_all.30 = bf16[256,2,560]{2,1,0:T(2,128)(2,1)S(1)} all-to-all(bf16[256,2,560]{2,1,0:T(2,128)(2,1)S(1)} %reshape.163), channel_id=1, replica_groups=mesh['wy'=8,'wz'=2,'wc'=2,'loop'=16] {'wy','wz','loop'}, dimensions={0} | all-to-all | bytes 1146880 | tf_op jit(solution)/shard_map/all_to_all | solution.py:101
  193.8 1.0 reshape.164
  194.8 1.9 copy.51
  196.8 6.1 %collective-permute-start.2 = (bf16[256,1120]{0,1:T(8,128)(2,1)S(1)}, bf16[256,1120]{0,1:T(8,128)(2,1)S(1)}, u32[]{:S(2)}, u32[]{:S(2)}) collective-permute-start(bf16[256,1120]{0,1:T(8,128)(2,1)S(1)} %bitcast.70), channel_id=1, source_target_pairs={{0,16},{16,0},{1,17},{17,1},{2,18},{18,2},{3,19},{19,3},{4,20},{20... | collective-permute-start | bytes 1720328 | tf_op jit(solution)/shard_map/ppermute | solution.py:102
  202.9 1.6 collective-permute-done.2
  (51 shorter events, 12.9 us)
Async XLA Ops:
  0.6 97.7 %copy-start = (bf16[512,512]{1,0:T(8,128)(2,1)S(1)}, bf16[512,512]{1,0:T(8,128)(2,1)}, u32[]{:S(2)}) copy-start(bf16[512,512]{1,0:T(8,128)(2,1)} %param.14) | copy-start | bytes 1572868
  3.2 11.2 %copy-start.6 = (s32[1,1,4]{2,1,0:T(1,128)S(1)}, s32[1,1,4]{2,1,0:T(1,128)}, u32[]{:S(2)}) copy-start(s32[1,1,4]{2,1,0:T(1,128)} %param.12) | copy-start | bytes 52
  3.2 52.6 %copy-start.3 = (bf16[1,1,4,128,128]{4,3,2,1,0:T(8,128)(2,1)S(1)}, bf16[1,1,4,128,128]{4,3,2,1,0:T(8,128)(2,1)}, u32[]{:S(2)}) copy-start(bf16[1,1,4,128,128]{4,3,2,1,0:T(8,128)(2,1)} %param.10) | copy-start | bytes 393220
  3.2 52.0 %all-to-all-start = ((bf16[16,1,128,512]{3,2,1,0:T(8,128)(2,1)}), bf16[16,1,128,512]{3,2,1,0:T(8,128)(2,1)S(1)}, u32[]{:S(2)}, u32[]{:S(2)}) async-start(bf16[16,1,128,512]{3,2,1,0:T(8,128)(2,1)} %broadcast_in_dim.36), calls=%async_computation | async-start | bytes 4194304 | tf_op jit(solution)/shard_map/all_to_all | solution.py:9
  56.3 0.7 copy-start.5
  58.5 5.8 %collective-permute-start = (bf16[8,2,32,512]{3,2,1,0:T(8,128)(2,1)S(1)}, bf16[8,2,32,512]{3,2,1,0:T(8,128)(2,1)S(1)}, u32[]{:S(2)}, u32[]{:S(2)}) collective-permute-start(bf16[8,2,32,512]{3,2,1,0:T(8,128)(2,1)S(1)} %bitcast.74), channel_id=1, source_target_pairs={{0,16},{16,0},{1,17},{17,1},{2,18},{18,2},{3,19},{19,3},{4,20},{20... | collective-permute-start | bytes 1572872 | tf_op jit(solution)/shard_map/ppermute | solution.py:67
  65.4 33.2 %copy-start.2 = (bf16[512,512]{1,0:T(8,128)(2,1)S(1)}, bf16[512,512]{1,0:T(8,128)(2,1)}, u32[]{:S(2)}) copy-start(bf16[512,512]{1,0:T(8,128)(2,1)} %param.15) | copy-start | bytes 1572868
  65.4 32.9 %all-to-all-start.1 = ((bf16[16,1,32,512]{3,2,1,0:T(8,128)(2,1)}), bf16[16,1,32,512]{3,2,1,0:T(8,128)(2,1)S(1)}, u32[]{:S(2)}, u32[]{:S(2)}) async-start(bf16[16,1,32,512]{3,2,1,0:T(8,128)(2,1)} %bitcast.18), calls=%async_computation.1 | async-start | bytes 1048576 | tf_op jit(solution)/shard_map/all_to_all | solution.py:30
  78.1 21.4 %copy-start.4 = (f32[512]{0:T(512)S(1)}, f32[512]{0:T(512)}, u32[]{:S(2)}) copy-start(f32[512]{0:T(512)} %param.16) | copy-start | bytes 6148
  110.1 6.6 %collective-permute-start.1 = (f32[262144]{0:T(1024)S(1)}, f32[262144]{0:T(1024)S(1)}, u32[]{:S(2)}, u32[]{:S(2)}) collective-permute-start(f32[262144]{0:T(1024)S(1)} %bitcast.72), channel_id=1, source_target_pairs={{0,16},{16,0},{1,17},{17,1},{2,18},{18,2},{3,19},{19,3},{4,20},{20... | collective-permute-start | bytes 3145736 | tf_op jit(solution)/shard_map/ppermute | solution.py:93
  196.8 7.7 %collective-permute-start.2 = (bf16[256,1120]{0,1:T(8,128)(2,1)S(1)}, bf16[256,1120]{0,1:T(8,128)(2,1)S(1)}, u32[]{:S(2)}, u32[]{:S(2)}) collective-permute-start(bf16[256,1120]{0,1:T(8,128)(2,1)S(1)} %bitcast.70), channel_id=1, source_target_pairs={{0,16},{16,0},{1,17},{17,1},{2,18},{18,2},{3,19},{19,3},{4,20},{20... | collective-permute-start | bytes 1720328 | tf_op jit(solution)/shard_map/ppermute | solution.py:102
  204.7 1.0 copy-start.1
  206.6 1.2 slice-start

commit v6 on v5

--- a/solution.py
+++ b/solution.py
@@ -82,15 +82,18 @@
     pre_grad = (
         residual_grad[:, None] * readout[None, :] * gate_sig * (1.0 + pre_act * (1.0 - gate_sig))
     ).astype(jnp.bfloat16)
-    grad_msg = jnp.einsum("na,nb->ab", message, pre_grad, preferred_element_type=jnp.float32)
-    grad_self = jnp.einsum("na,nb->ab", node_feats, pre_grad, preferred_element_type=jnp.float32)
     swap = [(0, 1), (1, 0)]
     others = ("wy", "wz", "loop")
     peers = lax.axis_size(others)
-    both_grads = jnp.stack([grad_msg, grad_self]).reshape(2, -1)
-    mine = lax.dynamic_index_in_dim(both_grads, core, 0, keepdims=False)
-    theirs = lax.dynamic_index_in_dim(both_grads, 1 - core, 0, keepdims=False)
-    half_sum = mine + lax.ppermute(theirs, "wc", swap)
+    sib_message, sib_pre_grad = lax.ppermute((message, pre_grad), "wc", swap)
+    sib_feats = lax.dynamic_slice_in_dim(feats, (wide_pos + 1 - 2 * core) * share_rows, share_rows, 0)
+    pair_rows = jnp.where(
+        core == 0,
+        jnp.concatenate([message, sib_message]),
+        jnp.concatenate([node_feats, sib_feats]),
+    )
+    pair_grad = jnp.concatenate([pre_grad, sib_pre_grad])
+    half_sum = jnp.einsum("na,nb->ab", pair_rows, pair_grad, preferred_element_type=jnp.float32)
     pieces = lax.all_to_all(half_sum.astype(jnp.bfloat16).reshape(peers, -1), others, 0, 0, tiled=True)
     reduced = jnp.sum(pieces.astype(jnp.float32), axis=0).astype(jnp.bfloat16)
     logit_hi = logits.astype(jnp.bfloat16)

time: 210 us -> 201 us (0.957)
  other arithmetic: 17.5 us -> 11.4 us
    another operation x1 -> x0, other arithmetic: 6.01 us -> none  [body(): both_grads = jnp.stack([grad_msg, grad_self]).reshape(2, -1)]
    unnamed x20 -> x18, local copies, waits for them, and re-layouts: 5.56 us -> 3.61 us
    ppermute x1 -> x2, starting transfers between devices: 4.49 us -> 6.22 us  [body(): sib_message, sib_pre_grad = lax.ppermute((message, pre_grad), 'wc', swap)]
  transfers between devices with their start and end apart: 5 -> 6, of which waited for: 5 -> 5; matrix products, arithmetic and copies ran while one was open for 0% -> 0% of each run, Pallas kernels for 0% -> 0%
where the time goes in v6:
time: 201 us; the launch traced here: 200 us
  blocking collectives  65.4 us (33%)
  waiting for transfers between devices  64.3 us (32%)
  starting transfers between devices  39.7 us (20%)
  local copies, waits for them, and re-layouts  14.1 us (7%)
  other arithmetic  11.4 us (6%)
  matrix products  3.36 us (2%)
    all_to_all x1, waiting for transfers between devices, copy_for_each(): return lax.all_to_all(copies, axis, split_axis=0, concat_axis=0, tiled=True)  40.8 us
    all_to_all x1, blocking collectives, body(): lax.all_to_all(half_sum.astype(jnp.bfloat16).reshape(peers, -1), others,...  35.7 us
    all_to_all x1, blocking collectives, body(): lax.all_to_all(jnp.broadcast_to(payload, (peers, payload.size)), others,...  29.7 us
    all_to_all x1, waiting for transfers between devices, sum_at_owner(): lax.all_to_all(in_blocks(value, dim, devices), axis, 0, 0, tiled=True)  19.3 us
    all_to_all x1, starting transfers between devices, sum_at_owner(): lax.all_to_all(in_blocks(value, dim, devices), axis, 0, 0, tiled=True)  12.8 us
    all_to_all x1, starting transfers between devices, copy_for_each(): return lax.all_to_all(copies, axis, split_axis=0, concat_axis=0, tiled=True)  10.5 us
    ppermute x2, starting transfers between devices, body(): sib_message, sib_pre_grad = lax.ppermute((message, pre_grad), 'wc', swap)  6.22 us
    ppermute x1, starting transfers between devices, body(): from_sibling = lax.ppermute(gathered, 'wc', swap)  5.89 us
  transfers between devices with their start and end apart: 6, of which 5 were waited for; matrix products, arithmetic and copies ran while one was open for 0% of the time, Pallas kernels for 0%

profile of v6, /device:TPU:1, one launch (start us, length us, event | category | flops | bytes accessed | tf_op | source)
XLA Modules:
  0.0 200.0 jit_solution(16468628222692965395)
XLA Ops:
  0.7 1.0 fusion.5
  1.6 1.5 broadcast_in_dim.36
  3.2 10.5 %all-to-all-start = ((bf16[16,1,128,512]{3,2,1,0:T(8,128)(2,1)}), bf16[16,1,128,512]{3,2,1,0:T(8,128)(2,1)S(1)}, u32[]{:S(2)}, u32[]{:S(2)}) async-start(bf16[16,1,128,512]{3,2,1,0:T(8,128)(2,1)} %broadcast_in_dim.36), calls=%async_computation | async-start | bytes 4194304 | tf_op jit(solution)/shard_map/all_to_all | solution.py:9
  14.5 40.8 %all-to-all-done = bf16[16,1,128,512]{3,2,1,0:T(8,128)(2,1)S(1)} async-done(((bf16[16,1,128,512]{3,2,1,0:T(8,128)(2,1)}), bf16[16,1,128,512]{3,2,1,0:T(8,128)(2,1)S(1)}, u32[]{:S(2)}, u32[]{:S(2)}) %all-to-all-start) | async-done | bytes 2097184 | tf_op jit(solution)/shard_map/all_to_all | solution.py:9
  56.9 1.4 convolution_convert_fusion
  58.5 4.3 %collective-permute-start = (bf16[8,2,32,512]{3,2,1,0:T(8,128)(2,1)S(1)}, bf16[8,2,32,512]{3,2,1,0:T(8,128)(2,1)S(1)}, u32[]{:S(2)}, u32[]{:S(2)}) collective-permute-start(bf16[8,2,32,512]{3,2,1,0:T(8,128)(2,1)S(1)} %bitcast.60), channel_id=1, source_target_pairs={{0,16},{16,0},{1,17},{17,1},{2,18},{18,2},{3,19},{19,3},{4,20},{20... | collective-permute-start | bytes 1572872 | tf_op jit(solution)/shard_map/ppermute | solution.py:67
  62.8 1.5 collective-permute-done
  64.4 1.0 fusion
  65.4 12.8 %all-to-all-start.1 = ((bf16[16,1,32,512]{3,2,1,0:T(8,128)(2,1)}), bf16[16,1,32,512]{3,2,1,0:T(8,128)(2,1)S(1)}, u32[]{:S(2)}, u32[]{:S(2)}) async-start(bf16[16,1,32,512]{3,2,1,0:T(8,128)(2,1)} %bitcast.18), calls=%async_computation.1 | async-start | bytes 1048576 | tf_op jit(solution)/shard_map/all_to_all | solution.py:30
  78.9 19.3 %all-to-all-done.1 = bf16[16,1,32,512]{3,2,1,0:T(8,128)(2,1)S(1)} async-done(((bf16[16,1,32,512]{3,2,1,0:T(8,128)(2,1)}), bf16[16,1,32,512]{3,2,1,0:T(8,128)(2,1)S(1)}, u32[]{:S(2)}, u32[]{:S(2)}) %all-to-all-start.1) | async-done | bytes 524320 | tf_op jit(solution)/shard_map/all_to_all | solution.py:30
  99.7 4.3 %collective-permute-start.2 = (bf16[32,512]{1,0:T(8,128)(2,1)S(1)}, bf16[32,512]{1,0:T(8,128)(2,1)S(1)}, u32[]{:S(2)}, u32[]{:S(2)}) collective-permute-start(bf16[32,512]{1,0:T(8,128)(2,1)S(1)} %multiply_convert_fusion), channel_id=1, source_target_pairs={{0,16},{16,0},{1,17},{17,1},{2,18},{18,2},{3,19},{19,3},{4,20},{20... | collective-permute-start | bytes 98312 | tf_op jit(solution)/shard_map/ppermute | solution.py:88
  104.0 1.9 collective-permute-start.1
  106.0 1.2 collective-permute-done.1
  108.3 3.7 %reduce.4 = bf16[256,1024]{1,0:T(8,128)(2,1)S(1)} reduce(bf16[256,1,1024]{2,1,0:T(2,128)(2,1)S(1)} %all_to_all.24, bf16[]{:T(256)} %broadcast.81), dimensions={1}, to_apply=%all_to_all.24.reduce_sub_computation | reduce | bytes 1048578 | tf_op jit(solution)/shard_map/all_to_all | solution.py:97
  112.4 35.7 %all_to_all.29 = bf16[256,2,512]{2,1,0:T(2,128)(2,1)S(1)} all-to-all(bf16[256,2,512]{2,1,0:T(2,128)(2,1)S(1)} %reshape.156), channel_id=1, replica_groups=mesh['wy'=8,'wz'=2,'wc'=2,'loop'=16] {'wy','wz','loop'}, dimensions={0} | all-to-all | bytes 1048576 | tf_op jit(solution)/shard_map/all_to_all | solution.py:97
  148.6 0.9 reduce_sum.25
  150.2 4.4 %reduce.5 = bf16[256,1120]{1,0:T(8,128)(2,1)S(1)} reduce(bf16[256,1,1120]{2,1,0:T(2,128)(2,1)S(1)} %broadcast_in_dim.38, bf16[]{:T(256)} %broadcast.81), dimensions={1}, to_apply=%broadcast_in_dim.38.reduce_sub_computation | reduce | bytes 1146882 | tf_op jit(solution)/shard_map/broadcast_in_dim | solution.py:104
  155.2 29.7 %all_to_all.30 = bf16[256,2,560]{2,1,0:T(2,128)(2,1)S(1)} all-to-all(bf16[256,2,560]{2,1,0:T(2,128)(2,1)S(1)} %reshape.158), channel_id=1, replica_groups=mesh['wy'=8,'wz'=2,'wc'=2,'loop'=16] {'wy','wz','loop'}, dimensions={0} | all-to-all | bytes 1146880 | tf_op jit(solution)/shard_map/all_to_all | solution.py:104
  184.9 1.0 reshape.159
  185.9 1.9 copy.51
  187.9 5.9 %collective-permute-start.3 = (bf16[256,1120]{0,1:T(8,128)(2,1)S(1)}, bf16[256,1120]{0,1:T(8,128)(2,1)S(1)}, u32[]{:S(2)}, u32[]{:S(2)}) collective-permute-start(bf16[256,1120]{0,1:T(8,128)(2,1)S(1)} %bitcast.57), channel_id=1, source_target_pairs={{0,16},{16,0},{1,17},{17,1},{2,18},{18,2},{3,19},{19,3},{4,20},{20... | collective-permute-start | bytes 1720328 | tf_op jit(solution)/shard_map/ppermute | solution.py:105
  193.7 1.6 collective-permute-done.3
  196.7 1.0 squeeze.17
  197.9 1.0 squeeze.18
  (50 shorter events, 10.1 us)
Async XLA Ops:
  0.6 97.7 %copy-start = (bf16[512,512]{1,0:T(8,128)(2,1)S(1)}, bf16[512,512]{1,0:T(8,128)(2,1)}, u32[]{:S(2)}) copy-start(bf16[512,512]{1,0:T(8,128)(2,1)} %param.14) | copy-start | bytes 1572868
  3.2 11.2 %copy-start.6 = (s32[1,1,4]{2,1,0:T(1,128)S(1)}, s32[1,1,4]{2,1,0:T(1,128)}, u32[]{:S(2)}) copy-start(s32[1,1,4]{2,1,0:T(1,128)} %param.12) | copy-start | bytes 52
  3.2 52.0 %all-to-all-start = ((bf16[16,1,128,512]{3,2,1,0:T(8,128)(2,1)}), bf16[16,1,128,512]{3,2,1,0:T(8,128)(2,1)S(1)}, u32[]{:S(2)}, u32[]{:S(2)}) async-start(bf16[16,1,128,512]{3,2,1,0:T(8,128)(2,1)} %broadcast_in_dim.36), calls=%async_computation | async-start | bytes 4194304 | tf_op jit(solution)/shard_map/all_to_all | solution.py:9
  13.7 42.1 %copy-start.3 = (bf16[1,1,4,128,128]{4,3,2,1,0:T(8,128)(2,1)S(1)}, bf16[1,1,4,128,128]{4,3,2,1,0:T(8,128)(2,1)}, u32[]{:S(2)}) copy-start(bf16[1,1,4,128,128]{4,3,2,1,0:T(8,128)(2,1)} %param.10) | copy-start | bytes 393220
  56.2 0.7 copy-start.5
  58.5 5.8 %collective-permute-start = (bf16[8,2,32,512]{3,2,1,0:T(8,128)(2,1)S(1)}, bf16[8,2,32,512]{3,2,1,0:T(8,128)(2,1)S(1)}, u32[]{:S(2)}, u32[]{:S(2)}) collective-permute-start(bf16[8,2,32,512]{3,2,1,0:T(8,128)(2,1)S(1)} %bitcast.60), channel_id=1, source_target_pairs={{0,16},{16,0},{1,17},{17,1},{2,18},{18,2},{3,19},{19,3},{4,20},{20... | collective-permute-start | bytes 1572872 | tf_op jit(solution)/shard_map/ppermute | solution.py:67
  65.4 33.2 %copy-start.2 = (bf16[512,512]{1,0:T(8,128)(2,1)S(1)}, bf16[512,512]{1,0:T(8,128)(2,1)}, u32[]{:S(2)}) copy-start(bf16[512,512]{1,0:T(8,128)(2,1)} %param.15) | copy-start | bytes 1572868
  65.4 32.9 %all-to-all-start.1 = ((bf16[16,1,32,512]{3,2,1,0:T(8,128)(2,1)}), bf16[16,1,32,512]{3,2,1,0:T(8,128)(2,1)S(1)}, u32[]{:S(2)}, u32[]{:S(2)}) async-start(bf16[16,1,32,512]{3,2,1,0:T(8,128)(2,1)} %bitcast.18), calls=%async_computation.1 | async-start | bytes 1048576 | tf_op jit(solution)/shard_map/all_to_all | solution.py:30
  78.1 20.6 %copy-start.4 = (f32[512]{0:T(512)S(1)}, f32[512]{0:T(512)}, u32[]{:S(2)}) copy-start(f32[512]{0:T(512)} %param.16) | copy-start | bytes 6148
  99.7 6.2 %collective-permute-start.2 = (bf16[32,512]{1,0:T(8,128)(2,1)S(1)}, bf16[32,512]{1,0:T(8,128)(2,1)S(1)}, u32[]{:S(2)}, u32[]{:S(2)}) collective-permute-start(bf16[32,512]{1,0:T(8,128)(2,1)S(1)} %multiply_convert_fusion), channel_id=1, source_target_pairs={{0,16},{16,0},{1,17},{17,1},{2,18},{18,2},{3,19},{19,3},{4,20},{20... | collective-permute-start | bytes 98312 | tf_op jit(solution)/shard_map/ppermute | solution.py:88
  104.0 3.1 %collective-permute-start.1 = (bf16[32,512]{1,0:T(8,128)(2,1)S(1)}, bf16[32,512]{1,0:T(8,128)(2,1)S(1)}, u32[]{:S(2)}, u32[]{:S(2)}) collective-permute-start(bf16[32,512]{1,0:T(8,128)(2,1)S(1)} %reduce_sum.24), channel_id=1, source_target_pairs={{0,16},{16,0},{1,17},{17,1},{2,18},{18,2},{3,19},{19,3},{4,20},{20... | collective-permute-start | bytes 98312 | tf_op jit(solution)/shard_map/ppermute | solution.py:88
  187.9 7.5 %collective-permute-start.3 = (bf16[256,1120]{0,1:T(8,128)(2,1)S(1)}, bf16[256,1120]{0,1:T(8,128)(2,1)S(1)}, u32[]{:S(2)}, u32[]{:S(2)}) collective-permute-start(bf16[256,1120]{0,1:T(8,128)(2,1)S(1)} %bitcast.57), channel_id=1, source_target_pairs={{0,16},{16,0},{1,17},{17,1},{2,18},{18,2},{3,19},{19,3},{4,20},{20... | collective-permute-start | bytes 1720328 | tf_op jit(solution)/shard_map/ppermute | solution.py:105
  195.5 1.0 copy-start.1
  197.7 1.2 slice-start

commit v7 on v6

--- a/solution.py
+++ b/solution.py
@@ -94,19 +94,21 @@
     )
     pair_grad = jnp.concatenate([pre_grad, sib_pre_grad])
     half_sum = jnp.einsum("na,nb->ab", pair_rows, pair_grad, preferred_element_type=jnp.float32)
-    pieces = lax.all_to_all(half_sum.astype(jnp.bfloat16).reshape(peers, -1), others, 0, 0, tiled=True)
+    pieces = lax.all_to_all(
+        half_sum.astype(jnp.bfloat16).reshape(peers, -1, feat_width), others, 0, 0, tiled=True
+    )
     reduced = jnp.sum(pieces.astype(jnp.float32), axis=0).astype(jnp.bfloat16)
     logit_hi = logits.astype(jnp.bfloat16)
     logit_rest = logits - logit_hi.astype(jnp.float32)
     logit_mid = logit_rest.astype(jnp.bfloat16)
     logit_lo = (logit_rest - logit_mid.astype(jnp.float32)).astype(jnp.bfloat16)
-    payload = jnp.concatenate([reduced, logit_hi, logit_mid, logit_lo])
-    gathered = lax.all_to_all(jnp.broadcast_to(payload, (peers, payload.size)), others, 0, 0, tiled=True)
+    logit_parts = jnp.concatenate([logit_hi, logit_mid, logit_lo]).reshape(reduced.shape[0], -1)
+    payload = jnp.concatenate([reduced, logit_parts], axis=1)
+    gathered = lax.all_to_all(jnp.broadcast_to(payload, (peers, *payload.shape)), others, 0, 0, tiled=True)
     from_sibling = lax.ppermute(gathered, "wc", swap)
     by_core = jnp.where(core == 0, jnp.stack([gathered, from_sibling]), jnp.stack([from_sibling, gathered]))
-    chunk = reduced.size
-    grads = by_core[:, :, :chunk].reshape(2, feat_width, feat_width)
-    parts = by_core[:, :, chunk:].reshape(
+    grads = by_core[:, :, :, :feat_width].reshape(2, feat_width, feat_width)
+    parts = by_core[:, :, :, feat_width:].reshape(
         2, lax.axis_size("wy"), lax.axis_size("wz"), lax.axis_size("loop"), 3, share_rows
     )
     parts = lax.dynamic_index_in_dim(parts, lax.axis_index("loop"), 3, keepdims=False)

time: 201 us -> 192 us (0.955)
  blocking collectives: 65.4 us -> 29.7 us
  starting transfers between devices: 39.7 us -> 57.9 us
  waiting for transfers between devices: 64.3 us -> 82 us
  other arithmetic: 11.4 us -> 5.07 us
  local copies, waits for them, and re-layouts: 14.1 us -> 11.3 us
    all_to_all x2 -> x1, blocking collectives: 65.4 us -> 29.7 us  [body(): lax.all_to_all(jnp.broadcast_to(payload, (peers, *payload.shape)), others...]
    all_to_all x0 -> x1, starting transfers between devices: none -> 18.2 us  [body(): lax.all_to_all(half_sum.astype(jnp.bfloat16).reshape(peers, -1, feat_widt...]
    all_to_all x0 -> x1, waiting for transfers between devices: none -> 17.6 us  [body(): lax.all_to_all(half_sum.astype(jnp.bfloat16).reshape(peers, -1, feat_widt...]
    broadcast_in_dim x1 -> x0, other arithmetic: 4.38 us -> none  [body(): jnp.broadcast_to(payload, (peers, payload.size))]
    all_to_all x1 -> x0, other arithmetic: 3.69 us -> none  [body(): lax.all_to_all(half_sum.astype(jnp.bfloat16).reshape(peers, -1), others,...]
    unnamed x18 -> x14, local copies, waits for them, and re-layouts: 3.61 us -> 0.53 us
    select_n x1, other arithmetic: 0.19 us -> 2.23 us  [body(): jnp.where(core == 0, jnp.stack([gathered, from_sibling]), jnp.stack([from...]
  transfers between devices with their start and end apart: 6 -> 7, of which waited for: 5 -> 6; matrix products, arithmetic and copies ran while one was open for 0% -> 1% of each run, Pallas kernels for 0% -> 0%
where the time goes in v7:
time: 192 us; the launch traced here: 191 us
  waiting for transfers between devices  82 us (43%)
  starting transfers between devices  57.9 us (30%)
  blocking collectives  29.7 us (15%)
  local copies, waits for them, and re-layouts  11.3 us (6%)
  other arithmetic  5.07 us (3%)
  matrix products  3.36 us (2%)
    all_to_all x1, waiting for transfers between devices, copy_for_each(): return lax.all_to_all(copies, axis, split_axis=0, concat_axis=0, tiled=True)  40.8 us
    all_to_all x1, blocking collectives, body(): lax.all_to_all(jnp.broadcast_to(payload, (peers, *payload.shape)), others...  29.7 us
    all_to_all x1, waiting for transfers between devices, sum_at_owner(): lax.all_to_all(in_blocks(value, dim, devices), axis, 0, 0, tiled=True)  19.3 us
    all_to_all x1, starting transfers between devices, body(): lax.all_to_all(half_sum.astype(jnp.bfloat16).reshape(peers, -1, feat_widt...  18.2 us
    all_to_all x1, waiting for transfers between devices, body(): lax.all_to_all(half_sum.astype(jnp.bfloat16).reshape(peers, -1, feat_widt...  17.6 us
    all_to_all x1, starting transfers between devices, sum_at_owner(): lax.all_to_all(in_blocks(value, dim, devices), axis, 0, 0, tiled=True)  12.8 us
    all_to_all x1, starting transfers between devices, copy_for_each(): return lax.all_to_all(copies, axis, split_axis=0, concat_axis=0, tiled=True)  10.5 us
    ppermute x2, starting transfers between devices, body(): sib_message, sib_pre_grad = lax.ppermute((message, pre_grad), 'wc', swap)  6.22 us
  transfers between devices with their start and end apart: 7, of which 6 were waited for; matrix products, arithmetic and copies ran while one was open for 1% of the time, Pallas kernels for 0%

profile of v7, /device:TPU:1, one launch (start us, length us, event | category | flops | bytes accessed | tf_op | source)
XLA Modules:
  0.0 190.9 jit_solution(13767910555640002807)
XLA Ops:
  0.7 1.0 fusion.5
  1.6 1.5 broadcast_in_dim.36
  3.2 10.5 %all-to-all-start = ((bf16[16,1,128,512]{3,2,1,0:T(8,128)(2,1)}), bf16[16,1,128,512]{3,2,1,0:T(8,128)(2,1)S(1)}, u32[]{:S(2)}, u32[]{:S(2)}) async-start(bf16[16,1,128,512]{3,2,1,0:T(8,128)(2,1)} %broadcast_in_dim.36), calls=%async_computation | async-start | bytes 4194304 | tf_op jit(solution)/shard_map/all_to_all | solution.py:9
  14.4 40.8 %all-to-all-done = bf16[16,1,128,512]{3,2,1,0:T(8,128)(2,1)S(1)} async-done(((bf16[16,1,128,512]{3,2,1,0:T(8,128)(2,1)}), bf16[16,1,128,512]{3,2,1,0:T(8,128)(2,1)S(1)}, u32[]{:S(2)}, u32[]{:S(2)}) %all-to-all-start) | async-done | bytes 2097184 | tf_op jit(solution)/shard_map/all_to_all | solution.py:9
  56.9 1.4 convolution_convert_fusion
  58.5 4.3 %collective-permute-start = (bf16[8,2,32,512]{3,2,1,0:T(8,128)(2,1)S(1)}, bf16[8,2,32,512]{3,2,1,0:T(8,128)(2,1)S(1)}, u32[]{:S(2)}, u32[]{:S(2)}) collective-permute-start(bf16[8,2,32,512]{3,2,1,0:T(8,128)(2,1)S(1)} %bitcast.58), channel_id=1, source_target_pairs={{0,16},{16,0},{1,17},{17,1},{2,18},{18,2},{3,19},{19,3},{4,20},{20... | collective-permute-start | bytes 1572872 | tf_op jit(solution)/shard_map/ppermute | solution.py:67
  62.9 1.5 collective-permute-done
  64.4 1.0 fusion
  65.4 12.8 %all-to-all-start.1 = ((bf16[16,1,32,512]{3,2,1,0:T(8,128)(2,1)}), bf16[16,1,32,512]{3,2,1,0:T(8,128)(2,1)S(1)}, u32[]{:S(2)}, u32[]{:S(2)}) async-start(bf16[16,1,32,512]{3,2,1,0:T(8,128)(2,1)} %bitcast.18), calls=%async_computation.1 | async-start | bytes 1048576 | tf_op jit(solution)/shard_map/all_to_all | solution.py:30
  78.9 19.3 %all-to-all-done.1 = bf16[16,1,32,512]{3,2,1,0:T(8,128)(2,1)S(1)} async-done(((bf16[16,1,32,512]{3,2,1,0:T(8,128)(2,1)}), bf16[16,1,32,512]{3,2,1,0:T(8,128)(2,1)S(1)}, u32[]{:S(2)}, u32[]{:S(2)}) %all-to-all-start.1) | async-done | bytes 524320 | tf_op jit(solution)/shard_map/all_to_all | solution.py:30
  99.8 4.3 %collective-permute-start.2 = (bf16[32,512]{1,0:T(8,128)(2,1)S(1)}, bf16[32,512]{1,0:T(8,128)(2,1)S(1)}, u32[]{:S(2)}, u32[]{:S(2)}) collective-permute-start(bf16[32,512]{1,0:T(8,128)(2,1)S(1)} %multiply_convert_fusion), channel_id=1, source_target_pairs={{0,16},{16,0},{1,17},{17,1},{2,18},{18,2},{3,19},{19,3},{4,20},{20... | collective-permute-start | bytes 98312 | tf_op jit(solution)/shard_map/ppermute | solution.py:88
  104.1 1.9 %collective-permute-start.1 = (bf16[32,512]{1,0:T(8,128)(2,1)S(1)}, bf16[32,512]{1,0:T(8,128)(2,1)S(1)}, u32[]{:S(2)}, u32[]{:S(2)}) collective-permute-start(bf16[32,512]{1,0:T(8,128)(2,1)S(1)} %reduce_sum.24), channel_id=1, source_target_pairs={{0,16},{16,0},{1,17},{17,1},{2,18},{18,2},{3,19},{19,3},{4,20},{20... | collective-permute-start | bytes 98312 | tf_op jit(solution)/shard_map/ppermute | solution.py:88
  106.0 1.2 collective-permute-done.1
  107.5 1.0 reshape.111
  108.5 18.2 %all-to-all-start.2 = ((bf16[256,2,512]{2,1,0:T(2,128)(2,1)}), bf16[256,2,512]{2,1,0:T(2,128)(2,1)S(1)}, u32[]{:S(2)}, u32[]{:S(2)}) async-start(bf16[256,2,512]{2,1,0:T(2,128)(2,1)} %reshape.111), calls=%async_computation.2 | async-start | bytes 1048576 | tf_op jit(solution)/shard_map/all_to_all | solution.py:97
  126.9 17.6 %all-to-all-done.2 = bf16[256,2,512]{2,1,0:T(2,128)(2,1)S(1)} async-done(((bf16[256,2,512]{2,1,0:T(2,128)(2,1)}), bf16[256,2,512]{2,1,0:T(2,128)(2,1)S(1)}, u32[]{:S(2)}, u32[]{:S(2)}) %all-to-all-start.2) | async-done | bytes 524320 | tf_op jit(solution)/shard_map/all_to_all | solution.py:97
  145.3 29.7 %all_to_all.20 = bf16[256,2,560]{2,1,0:T(2,128)(2,1)S(1)} all-to-all(bf16[256,2,560]{2,1,0:T(2,128)(2,1)S(1)} %broadcast_in_dim.38), channel_id=1, replica_groups=mesh['wy'=8,'wz'=2,'wc'=2,'loop'=16] {'wy','wz','loop'}, dimensions={0} | all-to-all | bytes 1146880 | tf_op jit(solution)/shard_map/all_to_all | solution.py:107
  175.0 1.0 copy.35
  176.0 5.9 %collective-permute-start.3 = (bf16[256,2,560]{0,2,1:T(8,128)(2,1)S(1)}, bf16[256,2,560]{0,2,1:T(8,128)(2,1)S(1)}, u32[]{:S(2)}, u32[]{:S(2)}) collective-permute-start(bf16[256,2,560]{0,2,1:T(8,128)(2,1)S(1)} %copy.35), channel_id=1, source_target_pairs={{0,16},{16,0},{1,17},{17,1},{2,18},{18,2},{3,19},{19,3},{4,20},{20... | collective-permute-start | bytes 1720328 | tf_op jit(solution)/shard_map/ppermute | solution.py:108
  181.9 1.6 collective-permute-done.3
  183.5 1.1 copy.36
  184.6 2.2 %broadcast_select_fusion = bf16[2,256,2,560]{3,2,1,0:T(2,128)(2,1)S(1)} fusion(pred[]{:T(512)S(6)} %eq.21, bf16[1,256,2,560]{3,2,1,0:T(2,128)(2,1)S(1)} %bitcast.57, bf16[1,256,2,560]{3,2,1,0:T(2,128)(2,1)S(1)} %bitcast.54), kind=kLoop, calls=%fused_computation.1 | loop fusion | flops 1720320 | bytes 2293761 | tf_op jit(solution)/shard_map/jit(_where)/select_n | solution.py:109
  187.9 1.0 squeeze.17
  188.9 1.0 squeeze.18
  (44 shorter events, 7.6 us)
Async XLA Ops:
  0.6 97.7 %copy-start = (bf16[512,512]{1,0:T(8,128)(2,1)S(1)}, bf16[512,512]{1,0:T(8,128)(2,1)}, u32[]{:S(2)}) copy-start(bf16[512,512]{1,0:T(8,128)(2,1)} %param.14) | copy-start | bytes 1572868
  3.2 11.2 %copy-start.6 = (s32[1,1,4]{2,1,0:T(1,128)S(1)}, s32[1,1,4]{2,1,0:T(1,128)}, u32[]{:S(2)}) copy-start(s32[1,1,4]{2,1,0:T(1,128)} %param.12) | copy-start | bytes 52
  3.2 52.6 %copy-start.3 = (bf16[1,1,4,128,128]{4,3,2,1,0:T(8,128)(2,1)S(1)}, bf16[1,1,4,128,128]{4,3,2,1,0:T(8,128)(2,1)}, u32[]{:S(2)}) copy-start(bf16[1,1,4,128,128]{4,3,2,1,0:T(8,128)(2,1)} %param.10) | copy-start | bytes 393220
  3.2 52.0 %all-to-all-start = ((bf16[16,1,128,512]{3,2,1,0:T(8,128)(2,1)}), bf16[16,1,128,512]{3,2,1,0:T(8,128)(2,1)S(1)}, u32[]{:S(2)}, u32[]{:S(2)}) async-start(bf16[16,1,128,512]{3,2,1,0:T(8,128)(2,1)} %broadcast_in_dim.36), calls=%async_computation | async-start | bytes 4194304 | tf_op jit(solution)/shard_map/all_to_all | solution.py:9
  56.3 0.7 copy-start.5
  58.5 5.8 %collective-permute-start = (bf16[8,2,32,512]{3,2,1,0:T(8,128)(2,1)S(1)}, bf16[8,2,32,512]{3,2,1,0:T(8,128)(2,1)S(1)}, u32[]{:S(2)}, u32[]{:S(2)}) collective-permute-start(bf16[8,2,32,512]{3,2,1,0:T(8,128)(2,1)S(1)} %bitcast.58), channel_id=1, source_target_pairs={{0,16},{16,0},{1,17},{17,1},{2,18},{18,2},{3,19},{19,3},{4,20},{20... | collective-permute-start | bytes 1572872 | tf_op jit(solution)/shard_map/ppermute | solution.py:67
  65.4 33.2 %copy-start.2 = (bf16[512,512]{1,0:T(8,128)(2,1)S(1)}, bf16[512,512]{1,0:T(8,128)(2,1)}, u32[]{:S(2)}) copy-start(bf16[512,512]{1,0:T(8,128)(2,1)} %param.15) | copy-start | bytes 1572868
  65.4 33.4 %copy-start.4 = (f32[512]{0:T(512)S(1)}, f32[512]{0:T(512)}, u32[]{:S(2)}) copy-start(f32[512]{0:T(512)} %param.16) | copy-start | bytes 6148
  65.4 32.9 %all-to-all-start.1 = ((bf16[16,1,32,512]{3,2,1,0:T(8,128)(2,1)}), bf16[16,1,32,512]{3,2,1,0:T(8,128)(2,1)S(1)}, u32[]{:S(2)}, u32[]{:S(2)}) async-start(bf16[16,1,32,512]{3,2,1,0:T(8,128)(2,1)} %bitcast.18), calls=%async_computation.1 | async-start | bytes 1048576 | tf_op jit(solution)/shard_map/all_to_all | solution.py:30
  99.8 6.2 %collective-permute-start.2 = (bf16[32,512]{1,0:T(8,128)(2,1)S(1)}, bf16[32,512]{1,0:T(8,128)(2,1)S(1)}, u32[]{:S(2)}, u32[]{:S(2)}) collective-permute-start(bf16[32,512]{1,0:T(8,128)(2,1)S(1)} %multiply_convert_fusion), channel_id=1, source_target_pairs={{0,16},{16,0},{1,17},{17,1},{2,18},{18,2},{3,19},{19,3},{4,20},{20... | collective-permute-start | bytes 98312 | tf_op jit(solution)/shard_map/ppermute | solution.py:88
  104.1 3.1 %collective-permute-start.1 = (bf16[32,512]{1,0:T(8,128)(2,1)S(1)}, bf16[32,512]{1,0:T(8,128)(2,1)S(1)}, u32[]{:S(2)}, u32[]{:S(2)}) collective-permute-start(bf16[32,512]{1,0:T(8,128)(2,1)S(1)} %reduce_sum.24), channel_id=1, source_target_pairs={{0,16},{16,0},{1,17},{17,1},{2,18},{18,2},{3,19},{19,3},{4,20},{20... | collective-permute-start | bytes 98312 | tf_op jit(solution)/shard_map/ppermute | solution.py:88
  108.5 35.9 %all-to-all-start.2 = ((bf16[256,2,512]{2,1,0:T(2,128)(2,1)}), bf16[256,2,512]{2,1,0:T(2,128)(2,1)S(1)}, u32[]{:S(2)}, u32[]{:S(2)}) async-start(bf16[256,2,512]{2,1,0:T(2,128)(2,1)} %reshape.111), calls=%async_computation.2 | async-start | bytes 1048576 | tf_op jit(solution)/shard_map/all_to_all | solution.py:97
  176.0 7.5 %collective-permute-start.3 = (bf16[256,2,560]{0,2,1:T(8,128)(2,1)S(1)}, bf16[256,2,560]{0,2,1:T(8,128)(2,1)S(1)}, u32[]{:S(2)}, u32[]{:S(2)}) collective-permute-start(bf16[256,2,560]{0,2,1:T(8,128)(2,1)S(1)} %copy.35), channel_id=1, source_target_pairs={{0,16},{16,0},{1,17},{17,1},{2,18},{18,2},{3,19},{19,3},{4,20},{20... | collective-permute-start | bytes 1720328 | tf_op jit(solution)/shard_map/ppermute | solution.py:108
  186.8 1.1 copy-start.1
  187.9 2.0 %slice-start = ((bf16[2,256,2,560]{3,2,1,0:T(2,128)(2,1)}), bf16[2,256,2,48]{3,2,1,0:T(2,128)(2,1)S(1)}, s32[]{:S(2)}) async-start(bf16[2,256,2,560]{3,2,1,0:T(2,128)(2,1)} %copy-done.1), calls=%async_computation.4 | async-start | bytes 524288 | tf_op jit(solution)/shard_map/slice | solution.py:111

commit v8 on v7

--- a/solution.py
+++ b/solution.py
@@ -106,15 +106,17 @@
     payload = jnp.concatenate([reduced, logit_parts], axis=1)
     gathered = lax.all_to_all(jnp.broadcast_to(payload, (peers, *payload.shape)), others, 0, 0, tiled=True)
     from_sibling = lax.ppermute(gathered, "wc", swap)
-    by_core = jnp.where(core == 0, jnp.stack([gathered, from_sibling]), jnp.stack([from_sibling, gathered]))
-    grads = by_core[:, :, :, :feat_width].reshape(2, feat_width, feat_width)
-    parts = by_core[:, :, :, feat_width:].reshape(
+    from_core0 = jnp.where(core == 0, gathered, from_sibling)
+    from_core1 = jnp.where(core == 0, from_sibling, gathered)
+    grad_msg = from_core0[:, :, :feat_width].reshape(feat_width, feat_width)
+    grad_self = from_core1[:, :, :feat_width].reshape(feat_width, feat_width)
+    by_core = jnp.stack([from_core0[:, :, feat_width:], from_core1[:, :, feat_width:]])
+    parts = by_core.reshape(
         2, lax.axis_size("wy"), lax.axis_size("wz"), lax.axis_size("loop"), 3, share_rows
     )
     parts = lax.dynamic_index_in_dim(parts, lax.axis_index("loop"), 3, keepdims=False)
     parts = jnp.transpose(parts, (1, 2, 0, 3, 4)).astype(jnp.float32)
     out_logits = (parts[:, :, :, 0] + parts[:, :, :, 1] + parts[:, :, :, 2]).reshape(-1)
-    grad_msg, grad_self = grads[0], grads[1]
     return (out_logits, grad_msg, grad_self)
 
 

time: 192 us -> 189 us (0.984)
  other arithmetic: 5.07 us -> 2.97 us
    select_n x1, other arithmetic: 2.23 us -> 0.13 us  [body(): from_core0 = jnp.where(core == 0, gathered, from_sibling)]
    squeeze x2 -> x0, local copies, waits for them, and re-layouts: 1.98 us -> none  [body(): grad_msg, grad_self = (grads[0], grads[1])]
where the time goes in v8:
time: 189 us
  waiting for transfers between devices  82 us (43%)
  starting transfers between devices  57.9 us (31%)
  blocking collectives  29.7 us (16%)
  local copies, waits for them, and re-layouts  11.1 us (6%)
  matrix products  3.36 us (2%)
  other arithmetic  2.97 us (2%)
    all_to_all x1, waiting for transfers between devices, copy_for_each(): return lax.all_to_all(copies, axis, split_axis=0, concat_axis=0, tiled=True)  40.8 us
    all_to_all x1, blocking collectives, body(): lax.all_to_all(jnp.broadcast_to(payload, (peers, *payload.shape)), others...  29.7 us
    all_to_all x1, waiting for transfers between devices, sum_at_owner(): lax.all_to_all(in_blocks(value, dim, devices), axis, 0, 0, tiled=True)  19.3 us
    all_to_all x1, starting transfers between devices, body(): lax.all_to_all(half_sum.astype(jnp.bfloat16).reshape(peers, -1, feat_widt...  18.2 us
    all_to_all x1, waiting for transfers between devices, body(): lax.all_to_all(half_sum.astype(jnp.bfloat16).reshape(peers, -1, feat_widt...  17.6 us
    all_to_all x1, starting transfers between devices, sum_at_owner(): lax.all_to_all(in_blocks(value, dim, devices), axis, 0, 0, tiled=True)  12.6 us
    all_to_all x1, starting transfers between devices, copy_for_each(): return lax.all_to_all(copies, axis, split_axis=0, concat_axis=0, tiled=True)  10.5 us
    ppermute x2, starting transfers between devices, body(): sib_message, sib_pre_grad = lax.ppermute((message, pre_grad), 'wc', swap)  6.22 us
  transfers between devices with their start and end apart: 7, of which 6 were waited for; matrix products, arithmetic and copies ran while one was open for 1% of the time, Pallas kernels for 0%

profile of v8, /device:TPU:1, one launch (start us, length us, event | category | flops | bytes accessed | tf_op | source)
XLA Modules:
  0.0 188.6 jit_solution(4691766665021466339)
XLA Ops:
  0.7 1.0 fusion.5
  1.6 1.5 broadcast_in_dim.36
  3.2 10.5 %all-to-all-start = ((bf16[16,1,128,512]{3,2,1,0:T(8,128)(2,1)}), bf16[16,1,128,512]{3,2,1,0:T(8,128)(2,1)S(1)}, u32[]{:S(2)}, u32[]{:S(2)}) async-start(bf16[16,1,128,512]{3,2,1,0:T(8,128)(2,1)} %broadcast_in_dim.36), calls=%async_computation | async-start | bytes 4194304 | tf_op jit(solution)/shard_map/all_to_all | solution.py:9
  14.4 40.8 %all-to-all-done = bf16[16,1,128,512]{3,2,1,0:T(8,128)(2,1)S(1)} async-done(((bf16[16,1,128,512]{3,2,1,0:T(8,128)(2,1)}), bf16[16,1,128,512]{3,2,1,0:T(8,128)(2,1)S(1)}, u32[]{:S(2)}, u32[]{:S(2)}) %all-to-all-start) | async-done | bytes 2097184 | tf_op jit(solution)/shard_map/all_to_all | solution.py:9
  56.8 1.4 convolution_convert_fusion
  58.4 4.4 %collective-permute-start = (bf16[8,2,32,512]{3,2,1,0:T(8,128)(2,1)S(1)}, bf16[8,2,32,512]{3,2,1,0:T(8,128)(2,1)S(1)}, u32[]{:S(2)}, u32[]{:S(2)}) collective-permute-start(bf16[8,2,32,512]{3,2,1,0:T(8,128)(2,1)S(1)} %bitcast.64), channel_id=1, source_target_pairs={{0,16},{16,0},{1,17},{17,1},{2,18},{18,2},{3,19},{19,3},{4,20},{20... | collective-permute-start | bytes 1572872 | tf_op jit(solution)/shard_map/ppermute | solution.py:67
  62.9 1.5 collective-permute-done
  64.4 1.0 fusion
  65.4 12.6 %all-to-all-start.1 = ((bf16[16,1,32,512]{3,2,1,0:T(8,128)(2,1)}), bf16[16,1,32,512]{3,2,1,0:T(8,128)(2,1)S(1)}, u32[]{:S(2)}, u32[]{:S(2)}) async-start(bf16[16,1,32,512]{3,2,1,0:T(8,128)(2,1)} %bitcast.18), calls=%async_computation.1 | async-start | bytes 1048576 | tf_op jit(solution)/shard_map/all_to_all | solution.py:30
  78.8 19.3 %all-to-all-done.1 = bf16[16,1,32,512]{3,2,1,0:T(8,128)(2,1)S(1)} async-done(((bf16[16,1,32,512]{3,2,1,0:T(8,128)(2,1)}), bf16[16,1,32,512]{3,2,1,0:T(8,128)(2,1)S(1)}, u32[]{:S(2)}, u32[]{:S(2)}) %all-to-all-start.1) | async-done | bytes 524320 | tf_op jit(solution)/shard_map/all_to_all | solution.py:30
  98.6 0.9 divide_subtract_fusion
  99.6 4.3 %collective-permute-start.2 = (bf16[32,512]{1,0:T(8,128)(2,1)S(1)}, bf16[32,512]{1,0:T(8,128)(2,1)S(1)}, u32[]{:S(2)}, u32[]{:S(2)}) collective-permute-start(bf16[32,512]{1,0:T(8,128)(2,1)S(1)} %multiply_convert_fusion), channel_id=1, source_target_pairs={{0,16},{16,0},{1,17},{17,1},{2,18},{18,2},{3,19},{19,3},{4,20},{20... | collective-permute-start | bytes 98312 | tf_op jit(solution)/shard_map/ppermute | solution.py:88
  103.9 1.9 %collective-permute-start.1 = (bf16[32,512]{1,0:T(8,128)(2,1)S(1)}, bf16[32,512]{1,0:T(8,128)(2,1)S(1)}, u32[]{:S(2)}, u32[]{:S(2)}) collective-permute-start(bf16[32,512]{1,0:T(8,128)(2,1)S(1)} %reduce_sum.24), channel_id=1, source_target_pairs={{0,16},{16,0},{1,17},{17,1},{2,18},{18,2},{3,19},{19,3},{4,20},{20... | collective-permute-start | bytes 98312 | tf_op jit(solution)/shard_map/ppermute | solution.py:88
  105.9 1.2 collective-permute-done.1
  107.4 1.0 reshape.114
  108.4 18.2 %all-to-all-start.2 = ((bf16[256,2,512]{2,1,0:T(2,128)(2,1)}), bf16[256,2,512]{2,1,0:T(2,128)(2,1)S(1)}, u32[]{:S(2)}, u32[]{:S(2)}) async-start(bf16[256,2,512]{2,1,0:T(2,128)(2,1)} %reshape.114), calls=%async_computation.2 | async-start | bytes 1048576 | tf_op jit(solution)/shard_map/all_to_all | solution.py:97
  126.7 17.6 %all-to-all-done.2 = bf16[256,2,512]{2,1,0:T(2,128)(2,1)S(1)} async-done(((bf16[256,2,512]{2,1,0:T(2,128)(2,1)}), bf16[256,2,512]{2,1,0:T(2,128)(2,1)S(1)}, u32[]{:S(2)}, u32[]{:S(2)}) %all-to-all-start.2) | async-done | bytes 524320 | tf_op jit(solution)/shard_map/all_to_all | solution.py:97
  145.1 29.7 %all_to_all.20 = bf16[256,2,560]{2,1,0:T(2,128)(2,1)S(1)} all-to-all(bf16[256,2,560]{2,1,0:T(2,128)(2,1)S(1)} %broadcast_in_dim.38), channel_id=1, replica_groups=mesh['wy'=8,'wz'=2,'wc'=2,'loop'=16] {'wy','wz','loop'}, dimensions={0} | all-to-all | bytes 1146880 | tf_op jit(solution)/shard_map/all_to_all | solution.py:107
  174.8 1.0 copy.37
  175.9 5.9 %collective-permute-start.3 = (bf16[256,2,560]{0,2,1:T(8,128)(2,1)S(1)}, bf16[256,2,560]{0,2,1:T(8,128)(2,1)S(1)}, u32[]{:S(2)}, u32[]{:S(2)}) collective-permute-start(bf16[256,2,560]{0,2,1:T(8,128)(2,1)S(1)} %copy.37), channel_id=1, source_target_pairs={{0,16},{16,0},{1,17},{17,1},{2,18},{18,2},{3,19},{19,3},{4,20},{20... | collective-permute-start | bytes 1720328 | tf_op jit(solution)/shard_map/ppermute | solution.py:108
  181.8 1.6 collective-permute-done.3
  183.4 1.1 copy.38
  185.5 1.0 reshape.116
  186.5 1.0 reshape.117
  (44 shorter events, 6.6 us)
Async XLA Ops:
  0.6 97.6 %copy-start = (bf16[512,512]{1,0:T(8,128)(2,1)S(1)}, bf16[512,512]{1,0:T(8,128)(2,1)}, u32[]{:S(2)}) copy-start(bf16[512,512]{1,0:T(8,128)(2,1)} %param.14) | copy-start | bytes 1572868
  3.2 11.2 %copy-start.5 = (s32[1,1,4]{2,1,0:T(1,128)S(1)}, s32[1,1,4]{2,1,0:T(1,128)}, u32[]{:S(2)}) copy-start(s32[1,1,4]{2,1,0:T(1,128)} %param.12) | copy-start | bytes 52
  3.2 52.6 %copy-start.2 = (bf16[1,1,4,128,128]{4,3,2,1,0:T(8,128)(2,1)S(1)}, bf16[1,1,4,128,128]{4,3,2,1,0:T(8,128)(2,1)}, u32[]{:S(2)}) copy-start(bf16[1,1,4,128,128]{4,3,2,1,0:T(8,128)(2,1)} %param.10) | copy-start | bytes 393220
  3.2 52.0 %all-to-all-start = ((bf16[16,1,128,512]{3,2,1,0:T(8,128)(2,1)}), bf16[16,1,128,512]{3,2,1,0:T(8,128)(2,1)S(1)}, u32[]{:S(2)}, u32[]{:S(2)}) async-start(bf16[16,1,128,512]{3,2,1,0:T(8,128)(2,1)} %broadcast_in_dim.36), calls=%async_computation | async-start | bytes 4194304 | tf_op jit(solution)/shard_map/all_to_all | solution.py:9
  55.8 0.9 copy-start.4
  58.4 40.0 %copy-start.1 = (bf16[512,512]{1,0:T(8,128)(2,1)S(1)}, bf16[512,512]{1,0:T(8,128)(2,1)}, u32[]{:S(2)}) copy-start(bf16[512,512]{1,0:T(8,128)(2,1)} %param.15) | copy-start | bytes 1572868
  58.4 6.0 %collective-permute-start = (bf16[8,2,32,512]{3,2,1,0:T(8,128)(2,1)S(1)}, bf16[8,2,32,512]{3,2,1,0:T(8,128)(2,1)S(1)}, u32[]{:S(2)}, u32[]{:S(2)}) collective-permute-start(bf16[8,2,32,512]{3,2,1,0:T(8,128)(2,1)S(1)} %bitcast.64), channel_id=1, source_target_pairs={{0,16},{16,0},{1,17},{17,1},{2,18},{18,2},{3,19},{19,3},{4,20},{20... | collective-permute-start | bytes 1572872 | tf_op jit(solution)/shard_map/ppermute | solution.py:67
  64.4 34.3 %copy-start.3 = (f32[512]{0:T(512)S(1)}, f32[512]{0:T(512)}, u32[]{:S(2)}) copy-start(f32[512]{0:T(512)} %param.16) | copy-start | bytes 6148
  65.4 32.8 %all-to-all-start.1 = ((bf16[16,1,32,512]{3,2,1,0:T(8,128)(2,1)}), bf16[16,1,32,512]{3,2,1,0:T(8,128)(2,1)S(1)}, u32[]{:S(2)}, u32[]{:S(2)}) async-start(bf16[16,1,32,512]{3,2,1,0:T(8,128)(2,1)} %bitcast.18), calls=%async_computation.1 | async-start | bytes 1048576 | tf_op jit(solution)/shard_map/all_to_all | solution.py:30
  99.6 6.2 %collective-permute-start.2 = (bf16[32,512]{1,0:T(8,128)(2,1)S(1)}, bf16[32,512]{1,0:T(8,128)(2,1)S(1)}, u32[]{:S(2)}, u32[]{:S(2)}) collective-permute-start(bf16[32,512]{1,0:T(8,128)(2,1)S(1)} %multiply_convert_fusion), channel_id=1, source_target_pairs={{0,16},{16,0},{1,17},{17,1},{2,18},{18,2},{3,19},{19,3},{4,20},{20... | collective-permute-start | bytes 98312 | tf_op jit(solution)/shard_map/ppermute | solution.py:88
  103.9 3.1 %collective-permute-start.1 = (bf16[32,512]{1,0:T(8,128)(2,1)S(1)}, bf16[32,512]{1,0:T(8,128)(2,1)S(1)}, u32[]{:S(2)}, u32[]{:S(2)}) collective-permute-start(bf16[32,512]{1,0:T(8,128)(2,1)S(1)} %reduce_sum.24), channel_id=1, source_target_pairs={{0,16},{16,0},{1,17},{17,1},{2,18},{18,2},{3,19},{19,3},{4,20},{20... | collective-permute-start | bytes 98312 | tf_op jit(solution)/shard_map/ppermute | solution.py:88
  108.4 35.9 %all-to-all-start.2 = ((bf16[256,2,512]{2,1,0:T(2,128)(2,1)}), bf16[256,2,512]{2,1,0:T(2,128)(2,1)S(1)}, u32[]{:S(2)}, u32[]{:S(2)}) async-start(bf16[256,2,512]{2,1,0:T(2,128)(2,1)} %reshape.114), calls=%async_computation.2 | async-start | bytes 1048576 | tf_op jit(solution)/shard_map/all_to_all | solution.py:97
  175.9 7.5 %collective-permute-start.3 = (bf16[256,2,560]{0,2,1:T(8,128)(2,1)S(1)}, bf16[256,2,560]{0,2,1:T(8,128)(2,1)S(1)}, u32[]{:S(2)}, u32[]{:S(2)}) collective-permute-start(bf16[256,2,560]{0,2,1:T(8,128)(2,1)S(1)} %copy.37), channel_id=1, source_target_pairs={{0,16},{16,0},{1,17},{17,1},{2,18},{18,2},{3,19},{19,3},{4,20},{20... | collective-permute-start | bytes 1720328 | tf_op jit(solution)/shard_map/ppermute | solution.py:108

commit v9 on v8

--- a/solution.py
+++ b/solution.py
@@ -104,13 +104,13 @@
     logit_lo = (logit_rest - logit_mid.astype(jnp.float32)).astype(jnp.bfloat16)
     logit_parts = jnp.concatenate([logit_hi, logit_mid, logit_lo]).reshape(reduced.shape[0], -1)
     payload = jnp.concatenate([reduced, logit_parts], axis=1)
-    gathered = lax.all_to_all(jnp.broadcast_to(payload, (peers, *payload.shape)), others, 0, 0, tiled=True)
+    gathered = lax.all_to_all(jnp.tile(payload, (peers, 1)), others, 0, 0, tiled=True)
     from_sibling = lax.ppermute(gathered, "wc", swap)
     from_core0 = jnp.where(core == 0, gathered, from_sibling)
     from_core1 = jnp.where(core == 0, from_sibling, gathered)
-    grad_msg = from_core0[:, :, :feat_width].reshape(feat_width, feat_width)
-    grad_self = from_core1[:, :, :feat_width].reshape(feat_width, feat_width)
-    by_core = jnp.stack([from_core0[:, :, feat_width:], from_core1[:, :, feat_width:]])
+    grad_msg = from_core0[:, :feat_width]
+    grad_self = from_core1[:, :feat_width]
+    by_core = jnp.stack([from_core0[:, feat_width:], from_core1[:, feat_width:]])
     parts = by_core.reshape(
         2, lax.axis_size("wy"), lax.axis_size("wz"), lax.axis_size("loop"), 3, share_rows
     )

time: 189 us -> 187 us (0.989)
  local copies, waits for them, and re-layouts: 11.1 us -> 8.84 us
    reshape x2 -> x0, local copies, waits for them, and re-layouts: 1.98 us -> none  [the longest x1 0.99 us: body(): grad_msg = from_core0[:, :, :feat_width].reshape(feat_width, feat_width)]
where the time goes in v9:
time: 187 us; the launch traced here: 186 us
  waiting for transfers between devices  82 us (44%)
  starting transfers between devices  57.9 us (31%)
  blocking collectives  29.7 us (16%)
  local copies, waits for them, and re-layouts  8.84 us (5%)
  matrix products  3.36 us (2%)
  other arithmetic  2.97 us (2%)
    all_to_all x1, waiting for transfers between devices, copy_for_each(): return lax.all_to_all(copies, axis, split_axis=0, concat_axis=0, tiled=True)  40.8 us
    all_to_all x1, blocking collectives, body(): lax.all_to_all(jnp.tile(payload, (peers, 1)), others, 0, 0, tiled=True)  29.7 us
    all_to_all x1, waiting for transfers between devices, sum_at_owner(): lax.all_to_all(in_blocks(value, dim, devices), axis, 0, 0, tiled=True)  19.3 us
    all_to_all x1, starting transfers between devices, body(): lax.all_to_all(half_sum.astype(jnp.bfloat16).reshape(peers, -1, feat_widt...  18.2 us
    all_to_all x1, waiting for transfers between devices, body(): lax.all_to_all(half_sum.astype(jnp.bfloat16).reshape(peers, -1, feat_widt...  17.6 us
    all_to_all x1, starting transfers between devices, sum_at_owner(): lax.all_to_all(in_blocks(value, dim, devices), axis, 0, 0, tiled=True)  12.6 us
    all_to_all x1, starting transfers between devices, copy_for_each(): return lax.all_to_all(copies, axis, split_axis=0, concat_axis=0, tiled=True)  10.5 us
    ppermute x2, starting transfers between devices, body(): sib_message, sib_pre_grad = lax.ppermute((message, pre_grad), 'wc', swap)  6.22 us
  transfers between devices with their start and end apart: 7, of which 6 were waited for; matrix products, arithmetic and copies ran while one was open for 1% of the time, Pallas kernels for 0%

profile of v9, /device:TPU:1, one launch (start us, length us, event | category | flops | bytes accessed | tf_op | source)
XLA Modules:
  0.0 186.3 jit_solution(10948386506102455052)
XLA Ops:
  0.7 1.0 fusion.5
  1.6 1.5 broadcast_in_dim.33
  3.2 10.5 %all-to-all-start = ((bf16[16,1,128,512]{3,2,1,0:T(8,128)(2,1)}), bf16[16,1,128,512]{3,2,1,0:T(8,128)(2,1)S(1)}, u32[]{:S(2)}, u32[]{:S(2)}) async-start(bf16[16,1,128,512]{3,2,1,0:T(8,128)(2,1)} %broadcast_in_dim.33), calls=%async_computation | async-start | bytes 4194304 | tf_op jit(solution)/shard_map/all_to_all | solution.py:9
  14.4 40.8 %all-to-all-done = bf16[16,1,128,512]{3,2,1,0:T(8,128)(2,1)S(1)} async-done(((bf16[16,1,128,512]{3,2,1,0:T(8,128)(2,1)}), bf16[16,1,128,512]{3,2,1,0:T(8,128)(2,1)S(1)}, u32[]{:S(2)}, u32[]{:S(2)}) %all-to-all-start) | async-done | bytes 2097184 | tf_op jit(solution)/shard_map/all_to_all | solution.py:9
  56.8 1.4 convolution_convert_fusion
  58.4 4.4 %collective-permute-start = (bf16[8,2,32,512]{3,2,1,0:T(8,128)(2,1)S(1)}, bf16[8,2,32,512]{3,2,1,0:T(8,128)(2,1)S(1)}, u32[]{:S(2)}, u32[]{:S(2)}) collective-permute-start(bf16[8,2,32,512]{3,2,1,0:T(8,128)(2,1)S(1)} %bitcast.54), channel_id=1, source_target_pairs={{0,16},{16,0},{1,17},{17,1},{2,18},{18,2},{3,19},{19,3},{4,20},{20... | collective-permute-start | bytes 1572872 | tf_op jit(solution)/shard_map/ppermute | solution.py:67
  62.9 1.5 collective-permute-done
  64.4 1.0 fusion
  65.4 12.6 %all-to-all-start.1 = ((bf16[16,1,32,512]{3,2,1,0:T(8,128)(2,1)}), bf16[16,1,32,512]{3,2,1,0:T(8,128)(2,1)S(1)}, u32[]{:S(2)}, u32[]{:S(2)}) async-start(bf16[16,1,32,512]{3,2,1,0:T(8,128)(2,1)} %bitcast.18), calls=%async_computation.1 | async-start | bytes 1048576 | tf_op jit(solution)/shard_map/all_to_all | solution.py:30
  78.0 0.8 constant_dynamic-slice_fusion
  78.8 19.3 %all-to-all-done.1 = bf16[16,1,32,512]{3,2,1,0:T(8,128)(2,1)S(1)} async-done(((bf16[16,1,32,512]{3,2,1,0:T(8,128)(2,1)}), bf16[16,1,32,512]{3,2,1,0:T(8,128)(2,1)S(1)}, u32[]{:S(2)}, u32[]{:S(2)}) %all-to-all-start.1) | async-done | bytes 524320 | tf_op jit(solution)/shard_map/all_to_all | solution.py:30
  98.6 0.9 divide_subtract_fusion
  99.6 4.3 %collective-permute-start.2 = (bf16[32,512]{1,0:T(8,128)(2,1)S(1)}, bf16[32,512]{1,0:T(8,128)(2,1)S(1)}, u32[]{:S(2)}, u32[]{:S(2)}) collective-permute-start(bf16[32,512]{1,0:T(8,128)(2,1)S(1)} %multiply_convert_fusion), channel_id=1, source_target_pairs={{0,16},{16,0},{1,17},{17,1},{2,18},{18,2},{3,19},{19,3},{4,20},{20... | collective-permute-start | bytes 98312 | tf_op jit(solution)/shard_map/ppermute | solution.py:88
  103.9 1.9 %collective-permute-start.1 = (bf16[32,512]{1,0:T(8,128)(2,1)S(1)}, bf16[32,512]{1,0:T(8,128)(2,1)S(1)}, u32[]{:S(2)}, u32[]{:S(2)}) collective-permute-start(bf16[32,512]{1,0:T(8,128)(2,1)S(1)} %reduce_sum.24), channel_id=1, source_target_pairs={{0,16},{16,0},{1,17},{17,1},{2,18},{18,2},{3,19},{19,3},{4,20},{20... | collective-permute-start | bytes 98312 | tf_op jit(solution)/shard_map/ppermute | solution.py:88
  105.9 1.2 collective-permute-done.1
  107.4 1.0 reshape.115
  108.4 18.2 %all-to-all-start.2 = ((bf16[256,2,512]{2,1,0:T(2,128)(2,1)}), bf16[256,2,512]{2,1,0:T(2,128)(2,1)S(1)}, u32[]{:S(2)}, u32[]{:S(2)}) async-start(bf16[256,2,512]{2,1,0:T(2,128)(2,1)} %reshape.115), calls=%async_computation.2 | async-start | bytes 1048576 | tf_op jit(solution)/shard_map/all_to_all | solution.py:97
  126.7 17.6 %all-to-all-done.2 = bf16[256,2,512]{2,1,0:T(2,128)(2,1)S(1)} async-done(((bf16[256,2,512]{2,1,0:T(2,128)(2,1)}), bf16[256,2,512]{2,1,0:T(2,128)(2,1)S(1)}, u32[]{:S(2)}, u32[]{:S(2)}) %all-to-all-start.2) | async-done | bytes 524320 | tf_op jit(solution)/shard_map/all_to_all | solution.py:97
  145.1 29.7 %all_to_all.24 = bf16[256,2,560]{2,1,0:T(2,128)(2,1)S(1)} all-to-all(bf16[256,2,560]{2,1,0:T(2,128)(2,1)S(1)} %tile.2), channel_id=1, replica_groups=mesh['wy'=8,'wz'=2,'wc'=2,'loop'=16] {'wy','wz','loop'}, dimensions={0} | all-to-all | bytes 1146880 | tf_op jit(solution)/shard_map/all_to_all | solution.py:107
  175.6 5.9 %collective-permute-start.3 = (bf16[512,560]{0,1:T(8,128)(2,1)S(1)}, bf16[512,560]{0,1:T(8,128)(2,1)S(1)}, u32[]{:S(2)}, u32[]{:S(2)}) collective-permute-start(bf16[512,560]{0,1:T(8,128)(2,1)S(1)} %copy.37), channel_id=1, source_target_pairs={{0,16},{16,0},{1,17},{17,1},{2,18},{18,2},{3,19},{19,3},{4,20},{20... | collective-permute-start | bytes 1720328 | tf_op jit(solution)/shard_map/ppermute | solution.py:108
  181.5 1.6 collective-permute-done.3
  183.5 0.8 slice.44
  184.4 0.8 slice.45
  185.7 0.7 add.107
  (43 shorter events, 5.3 us)
Async XLA Ops:
  0.6 97.6 %copy-start = (bf16[512,512]{1,0:T(8,128)(2,1)S(1)}, bf16[512,512]{1,0:T(8,128)(2,1)}, u32[]{:S(2)}) copy-start(bf16[512,512]{1,0:T(8,128)(2,1)} %param.14) | copy-start | bytes 1572868
  3.2 11.2 %copy-start.5 = (s32[1,1,4]{2,1,0:T(1,128)S(1)}, s32[1,1,4]{2,1,0:T(1,128)}, u32[]{:S(2)}) copy-start(s32[1,1,4]{2,1,0:T(1,128)} %param.12) | copy-start | bytes 52
  3.2 52.6 %copy-start.2 = (bf16[1,1,4,128,128]{4,3,2,1,0:T(8,128)(2,1)S(1)}, bf16[1,1,4,128,128]{4,3,2,1,0:T(8,128)(2,1)}, u32[]{:S(2)}) copy-start(bf16[1,1,4,128,128]{4,3,2,1,0:T(8,128)(2,1)} %param.10) | copy-start | bytes 393220
  3.2 52.0 %all-to-all-start = ((bf16[16,1,128,512]{3,2,1,0:T(8,128)(2,1)}), bf16[16,1,128,512]{3,2,1,0:T(8,128)(2,1)S(1)}, u32[]{:S(2)}, u32[]{:S(2)}) async-start(bf16[16,1,128,512]{3,2,1,0:T(8,128)(2,1)} %broadcast_in_dim.33), calls=%async_computation | async-start | bytes 4194304 | tf_op jit(solution)/shard_map/all_to_all | solution.py:9
  55.8 0.9 copy-start.4
  58.4 40.0 %copy-start.1 = (bf16[512,512]{1,0:T(8,128)(2,1)S(1)}, bf16[512,512]{1,0:T(8,128)(2,1)}, u32[]{:S(2)}) copy-start(bf16[512,512]{1,0:T(8,128)(2,1)} %param.15) | copy-start | bytes 1572868
  58.4 6.0 %collective-permute-start = (bf16[8,2,32,512]{3,2,1,0:T(8,128)(2,1)S(1)}, bf16[8,2,32,512]{3,2,1,0:T(8,128)(2,1)S(1)}, u32[]{:S(2)}, u32[]{:S(2)}) collective-permute-start(bf16[8,2,32,512]{3,2,1,0:T(8,128)(2,1)S(1)} %bitcast.54), channel_id=1, source_target_pairs={{0,16},{16,0},{1,17},{17,1},{2,18},{18,2},{3,19},{19,3},{4,20},{20... | collective-permute-start | bytes 1572872 | tf_op jit(solution)/shard_map/ppermute | solution.py:67
  64.4 34.3 %copy-start.3 = (f32[512]{0:T(512)S(1)}, f32[512]{0:T(512)}, u32[]{:S(2)}) copy-start(f32[512]{0:T(512)} %param.16) | copy-start | bytes 6148
  65.4 32.8 %all-to-all-start.1 = ((bf16[16,1,32,512]{3,2,1,0:T(8,128)(2,1)}), bf16[16,1,32,512]{3,2,1,0:T(8,128)(2,1)S(1)}, u32[]{:S(2)}, u32[]{:S(2)}) async-start(bf16[16,1,32,512]{3,2,1,0:T(8,128)(2,1)} %bitcast.18), calls=%async_computation.1 | async-start | bytes 1048576 | tf_op jit(solution)/shard_map/all_to_all | solution.py:30
  99.6 6.2 %collective-permute-start.2 = (bf16[32,512]{1,0:T(8,128)(2,1)S(1)}, bf16[32,512]{1,0:T(8,128)(2,1)S(1)}, u32[]{:S(2)}, u32[]{:S(2)}) collective-permute-start(bf16[32,512]{1,0:T(8,128)(2,1)S(1)} %multiply_convert_fusion), channel_id=1, source_target_pairs={{0,16},{16,0},{1,17},{17,1},{2,18},{18,2},{3,19},{19,3},{4,20},{20... | collective-permute-start | bytes 98312 | tf_op jit(solution)/shard_map/ppermute | solution.py:88
  103.9 3.1 %collective-permute-start.1 = (bf16[32,512]{1,0:T(8,128)(2,1)S(1)}, bf16[32,512]{1,0:T(8,128)(2,1)S(1)}, u32[]{:S(2)}, u32[]{:S(2)}) collective-permute-start(bf16[32,512]{1,0:T(8,128)(2,1)S(1)} %reduce_sum.24), channel_id=1, source_target_pairs={{0,16},{16,0},{1,17},{17,1},{2,18},{18,2},{3,19},{19,3},{4,20},{20... | collective-permute-start | bytes 98312 | tf_op jit(solution)/shard_map/ppermute | solution.py:88
  108.4 35.9 %all-to-all-start.2 = ((bf16[256,2,512]{2,1,0:T(2,128)(2,1)}), bf16[256,2,512]{2,1,0:T(2,128)(2,1)S(1)}, u32[]{:S(2)}, u32[]{:S(2)}) async-start(bf16[256,2,512]{2,1,0:T(2,128)(2,1)} %reshape.115), calls=%async_computation.2 | async-start | bytes 1048576 | tf_op jit(solution)/shard_map/all_to_all | solution.py:97
  175.6 7.5 %collective-permute-start.3 = (bf16[512,560]{0,1:T(8,128)(2,1)S(1)}, bf16[512,560]{0,1:T(8,128)(2,1)S(1)}, u32[]{:S(2)}, u32[]{:S(2)}) collective-permute-start(bf16[512,560]{0,1:T(8,128)(2,1)S(1)} %copy.37), channel_id=1, source_target_pairs={{0,16},{16,0},{1,17},{17,1},{2,18},{18,2},{3,19},{19,3},{4,20},{20... | collective-permute-start | bytes 1720328 | tf_op jit(solution)/shard_map/ppermute | solution.py:108

commit v10 on v9

--- a/solution.py
+++ b/solution.py
@@ -94,10 +94,9 @@
     )
     pair_grad = jnp.concatenate([pre_grad, sib_pre_grad])
     half_sum = jnp.einsum("na,nb->ab", pair_rows, pair_grad, preferred_element_type=jnp.float32)
-    pieces = lax.all_to_all(
-        half_sum.astype(jnp.bfloat16).reshape(peers, -1, feat_width), others, 0, 0, tiled=True
-    )
-    reduced = jnp.sum(pieces.astype(jnp.float32), axis=0).astype(jnp.bfloat16)
+    pieces = lax.all_to_all(half_sum.astype(jnp.bfloat16), others, 0, 0, tiled=True)
+    reduced = jnp.sum(pieces.reshape(peers, -1, feat_width).astype(jnp.float32), axis=0)
+    reduced = reduced.astype(jnp.bfloat16)
     logit_hi = logits.astype(jnp.bfloat16)
     logit_rest = logits - logit_hi.astype(jnp.float32)
     logit_mid = logit_rest.astype(jnp.bfloat16)

time: 187 us -> 187 us (level)
  no operation moved by 1% of the time
where the time goes in v10:
time: 187 us; the launch traced here: 186 us
  waiting for transfers between devices  82 us (44%)
  starting transfers between devices  57.9 us (31%)
  blocking collectives  29.7 us (16%)
  local copies, waits for them, and re-layouts  8.84 us (5%)
  matrix products  3.36 us (2%)
  other arithmetic  2.97 us (2%)
    all_to_all x1, waiting for transfers between devices, copy_for_each(): return lax.all_to_all(copies, axis, split_axis=0, concat_axis=0, tiled=True)  40.8 us
    all_to_all x1, blocking collectives, body(): lax.all_to_all(jnp.tile(payload, (peers, 1)), others, 0, 0, tiled=True)  29.7 us
    all_to_all x1, waiting for transfers between devices, sum_at_owner(): lax.all_to_all(in_blocks(value, dim, devices), axis, 0, 0, tiled=True)  19.3 us
    all_to_all x1, starting transfers between devices, body(): lax.all_to_all(half_sum.astype(jnp.bfloat16), others, 0, 0, tiled=True)  18.2 us
    all_to_all x1, waiting for transfers between devices, body(): lax.all_to_all(half_sum.astype(jnp.bfloat16), others, 0, 0, tiled=True)  17.6 us
    all_to_all x1, starting transfers between devices, sum_at_owner(): lax.all_to_all(in_blocks(value, dim, devices), axis, 0, 0, tiled=True)  12.6 us
    all_to_all x1, starting transfers between devices, copy_for_each(): return lax.all_to_all(copies, axis, split_axis=0, concat_axis=0, tiled=True)  10.5 us
    ppermute x2, starting transfers between devices, body(): sib_message, sib_pre_grad = lax.ppermute((message, pre_grad), 'wc', swap)  6.22 us
  transfers between devices with their start and end apart: 7, of which 6 were waited for; matrix products, arithmetic and copies ran while one was open for 1% of the time, Pallas kernels for 0%

profile of v10, /device:TPU:1, one launch (start us, length us, event | category | flops | bytes accessed | tf_op | source)
XLA Modules:
  0.0 186.3 jit_solution(10948386506102455052)
XLA Ops:
  0.7 1.0 fusion.5
  1.6 1.5 broadcast_in_dim.33
  3.2 10.5 %all-to-all-start = ((bf16[16,1,128,512]{3,2,1,0:T(8,128)(2,1)}), bf16[16,1,128,512]{3,2,1,0:T(8,128)(2,1)S(1)}, u32[]{:S(2)}, u32[]{:S(2)}) async-start(bf16[16,1,128,512]{3,2,1,0:T(8,128)(2,1)} %broadcast_in_dim.33), calls=%async_computation | async-start | bytes 4194304 | tf_op jit(solution)/shard_map/all_to_all | solution.py:9
  14.4 40.8 %all-to-all-done = bf16[16,1,128,512]{3,2,1,0:T(8,128)(2,1)S(1)} async-done(((bf16[16,1,128,512]{3,2,1,0:T(8,128)(2,1)}), bf16[16,1,128,512]{3,2,1,0:T(8,128)(2,1)S(1)}, u32[]{:S(2)}, u32[]{:S(2)}) %all-to-all-start) | async-done | bytes 2097184 | tf_op jit(solution)/shard_map/all_to_all | solution.py:9
  56.8 1.4 convolution_convert_fusion
  58.4 4.4 %collective-permute-start = (bf16[8,2,32,512]{3,2,1,0:T(8,128)(2,1)S(1)}, bf16[8,2,32,512]{3,2,1,0:T(8,128)(2,1)S(1)}, u32[]{:S(2)}, u32[]{:S(2)}) collective-permute-start(bf16[8,2,32,512]{3,2,1,0:T(8,128)(2,1)S(1)} %bitcast.54), channel_id=1, source_target_pairs={{0,16},{16,0},{1,17},{17,1},{2,18},{18,2},{3,19},{19,3},{4,20},{20... | collective-permute-start | bytes 1572872 | tf_op jit(solution)/shard_map/ppermute | solution.py:67
  62.9 1.5 collective-permute-done
  64.4 1.0 fusion
  65.4 12.6 %all-to-all-start.1 = ((bf16[16,1,32,512]{3,2,1,0:T(8,128)(2,1)}), bf16[16,1,32,512]{3,2,1,0:T(8,128)(2,1)S(1)}, u32[]{:S(2)}, u32[]{:S(2)}) async-start(bf16[16,1,32,512]{3,2,1,0:T(8,128)(2,1)} %bitcast.18), calls=%async_computation.1 | async-start | bytes 1048576 | tf_op jit(solution)/shard_map/all_to_all | solution.py:30
  78.0 0.8 constant_dynamic-slice_fusion
  78.8 19.3 %all-to-all-done.1 = bf16[16,1,32,512]{3,2,1,0:T(8,128)(2,1)S(1)} async-done(((bf16[16,1,32,512]{3,2,1,0:T(8,128)(2,1)}), bf16[16,1,32,512]{3,2,1,0:T(8,128)(2,1)S(1)}, u32[]{:S(2)}, u32[]{:S(2)}) %all-to-all-start.1) | async-done | bytes 524320 | tf_op jit(solution)/shard_map/all_to_all | solution.py:30
  98.6 0.9 divide_subtract_fusion
  99.6 4.3 %collective-permute-start.2 = (bf16[32,512]{1,0:T(8,128)(2,1)S(1)}, bf16[32,512]{1,0:T(8,128)(2,1)S(1)}, u32[]{:S(2)}, u32[]{:S(2)}) collective-permute-start(bf16[32,512]{1,0:T(8,128)(2,1)S(1)} %multiply_convert_fusion), channel_id=1, source_target_pairs={{0,16},{16,0},{1,17},{17,1},{2,18},{18,2},{3,19},{19,3},{4,20},{20... | collective-permute-start | bytes 98312 | tf_op jit(solution)/shard_map/ppermute | solution.py:88
  103.9 1.9 %collective-permute-start.1 = (bf16[32,512]{1,0:T(8,128)(2,1)S(1)}, bf16[32,512]{1,0:T(8,128)(2,1)S(1)}, u32[]{:S(2)}, u32[]{:S(2)}) collective-permute-start(bf16[32,512]{1,0:T(8,128)(2,1)S(1)} %reduce_sum.24), channel_id=1, source_target_pairs={{0,16},{16,0},{1,17},{17,1},{2,18},{18,2},{3,19},{19,3},{4,20},{20... | collective-permute-start | bytes 98312 | tf_op jit(solution)/shard_map/ppermute | solution.py:88
  105.9 1.2 collective-permute-done.1
  107.4 1.0 all_to_all.20
  108.4 18.2 %all-to-all-start.2 = ((bf16[256,2,512]{2,1,0:T(2,128)(2,1)}), bf16[256,2,512]{2,1,0:T(2,128)(2,1)S(1)}, u32[]{:S(2)}, u32[]{:S(2)}) async-start(bf16[256,2,512]{2,1,0:T(2,128)(2,1)} %all_to_all.20), calls=%async_computation.2 | async-start | bytes 1048576 | tf_op jit(solution)/shard_map/all_to_all | solution.py:97
  126.7 17.6 %all-to-all-done.2 = bf16[256,2,512]{2,1,0:T(2,128)(2,1)S(1)} async-done(((bf16[256,2,512]{2,1,0:T(2,128)(2,1)}), bf16[256,2,512]{2,1,0:T(2,128)(2,1)S(1)}, u32[]{:S(2)}, u32[]{:S(2)}) %all-to-all-start.2) | async-done | bytes 524320 | tf_op jit(solution)/shard_map/all_to_all | solution.py:97
  145.1 29.7 %all_to_all.28 = bf16[256,2,560]{2,1,0:T(2,128)(2,1)S(1)} all-to-all(bf16[256,2,560]{2,1,0:T(2,128)(2,1)S(1)} %tile.2), channel_id=1, replica_groups=mesh['wy'=8,'wz'=2,'wc'=2,'loop'=16] {'wy','wz','loop'}, dimensions={0} | all-to-all | bytes 1146880 | tf_op jit(solution)/shard_map/all_to_all | solution.py:106
  175.6 5.9 %collective-permute-start.3 = (bf16[512,560]{0,1:T(8,128)(2,1)S(1)}, bf16[512,560]{0,1:T(8,128)(2,1)S(1)}, u32[]{:S(2)}, u32[]{:S(2)}) collective-permute-start(bf16[512,560]{0,1:T(8,128)(2,1)S(1)} %copy.37), channel_id=1, source_target_pairs={{0,16},{16,0},{1,17},{17,1},{2,18},{18,2},{3,19},{19,3},{4,20},{20... | collective-permute-start | bytes 1720328 | tf_op jit(solution)/shard_map/ppermute | solution.py:107
  181.5 1.6 collective-permute-done.3
  183.5 0.8 slice.44
  184.4 0.8 slice.45
  185.7 0.7 add.107
  (43 shorter events, 5.3 us)
Async XLA Ops:
  0.6 97.6 %copy-start = (bf16[512,512]{1,0:T(8,128)(2,1)S(1)}, bf16[512,512]{1,0:T(8,128)(2,1)}, u32[]{:S(2)}) copy-start(bf16[512,512]{1,0:T(8,128)(2,1)} %param.14) | copy-start | bytes 1572868
  3.2 11.2 %copy-start.5 = (s32[1,1,4]{2,1,0:T(1,128)S(1)}, s32[1,1,4]{2,1,0:T(1,128)}, u32[]{:S(2)}) copy-start(s32[1,1,4]{2,1,0:T(1,128)} %param.12) | copy-start | bytes 52
  3.2 52.6 %copy-start.2 = (bf16[1,1,4,128,128]{4,3,2,1,0:T(8,128)(2,1)S(1)}, bf16[1,1,4,128,128]{4,3,2,1,0:T(8,128)(2,1)}, u32[]{:S(2)}) copy-start(bf16[1,1,4,128,128]{4,3,2,1,0:T(8,128)(2,1)} %param.10) | copy-start | bytes 393220
  3.2 52.0 %all-to-all-start = ((bf16[16,1,128,512]{3,2,1,0:T(8,128)(2,1)}), bf16[16,1,128,512]{3,2,1,0:T(8,128)(2,1)S(1)}, u32[]{:S(2)}, u32[]{:S(2)}) async-start(bf16[16,1,128,512]{3,2,1,0:T(8,128)(2,1)} %broadcast_in_dim.33), calls=%async_computation | async-start | bytes 4194304 | tf_op jit(solution)/shard_map/all_to_all | solution.py:9
  55.8 0.9 copy-start.4
  58.4 40.0 %copy-start.1 = (bf16[512,512]{1,0:T(8,128)(2,1)S(1)}, bf16[512,512]{1,0:T(8,128)(2,1)}, u32[]{:S(2)}) copy-start(bf16[512,512]{1,0:T(8,128)(2,1)} %param.15) | copy-start | bytes 1572868
  58.4 6.0 %collective-permute-start = (bf16[8,2,32,512]{3,2,1,0:T(8,128)(2,1)S(1)}, bf16[8,2,32,512]{3,2,1,0:T(8,128)(2,1)S(1)}, u32[]{:S(2)}, u32[]{:S(2)}) collective-permute-start(bf16[8,2,32,512]{3,2,1,0:T(8,128)(2,1)S(1)} %bitcast.54), channel_id=1, source_target_pairs={{0,16},{16,0},{1,17},{17,1},{2,18},{18,2},{3,19},{19,3},{4,20},{20... | collective-permute-start | bytes 1572872 | tf_op jit(solution)/shard_map/ppermute | solution.py:67
  64.4 34.3 %copy-start.3 = (f32[512]{0:T(512)S(1)}, f32[512]{0:T(512)}, u32[]{:S(2)}) copy-start(f32[512]{0:T(512)} %param.16) | copy-start | bytes 6148
  65.4 32.8 %all-to-all-start.1 = ((bf16[16,1,32,512]{3,2,1,0:T(8,128)(2,1)}), bf16[16,1,32,512]{3,2,1,0:T(8,128)(2,1)S(1)}, u32[]{:S(2)}, u32[]{:S(2)}) async-start(bf16[16,1,32,512]{3,2,1,0:T(8,128)(2,1)} %bitcast.18), calls=%async_computation.1 | async-start | bytes 1048576 | tf_op jit(solution)/shard_map/all_to_all | solution.py:30
  99.6 6.2 %collective-permute-start.2 = (bf16[32,512]{1,0:T(8,128)(2,1)S(1)}, bf16[32,512]{1,0:T(8,128)(2,1)S(1)}, u32[]{:S(2)}, u32[]{:S(2)}) collective-permute-start(bf16[32,512]{1,0:T(8,128)(2,1)S(1)} %multiply_convert_fusion), channel_id=1, source_target_pairs={{0,16},{16,0},{1,17},{17,1},{2,18},{18,2},{3,19},{19,3},{4,20},{20... | collective-permute-start | bytes 98312 | tf_op jit(solution)/shard_map/ppermute | solution.py:88
  103.9 3.1 %collective-permute-start.1 = (bf16[32,512]{1,0:T(8,128)(2,1)S(1)}, bf16[32,512]{1,0:T(8,128)(2,1)S(1)}, u32[]{:S(2)}, u32[]{:S(2)}) collective-permute-start(bf16[32,512]{1,0:T(8,128)(2,1)S(1)} %reduce_sum.24), channel_id=1, source_target_pairs={{0,16},{16,0},{1,17},{17,1},{2,18},{18,2},{3,19},{19,3},{4,20},{20... | collective-permute-start | bytes 98312 | tf_op jit(solution)/shard_map/ppermute | solution.py:88
  108.4 35.9 %all-to-all-start.2 = ((bf16[256,2,512]{2,1,0:T(2,128)(2,1)}), bf16[256,2,512]{2,1,0:T(2,128)(2,1)S(1)}, u32[]{:S(2)}, u32[]{:S(2)}) async-start(bf16[256,2,512]{2,1,0:T(2,128)(2,1)} %all_to_all.20), calls=%async_computation.2 | async-start | bytes 1048576 | tf_op jit(solution)/shard_map/all_to_all | solution.py:97
  175.6 7.5 %collective-permute-start.3 = (bf16[512,560]{0,1:T(8,128)(2,1)S(1)}, bf16[512,560]{0,1:T(8,128)(2,1)S(1)}, u32[]{:S(2)}, u32[]{:S(2)}) collective-permute-start(bf16[512,560]{0,1:T(8,128)(2,1)S(1)} %copy.37), channel_id=1, source_target_pairs={{0,16},{16,0},{1,17},{17,1},{2,18},{18,2},{3,19},{19,3},{4,20},{20... | collective-permute-start | bytes 1720328 | tf_op jit(solution)/shard_map/ppermute | solution.py:107

commit v11 on v9

--- a/solution.py
+++ b/solution.py
@@ -45,7 +45,10 @@
         "wc"
     ) + lax.axis_index("wc")
     picked_blocks = wide_pos % blocks_dev + wide_size * jnp.arange(cols_own, dtype=jnp.int32)
-    own_blocks = jnp.take(feats.reshape(blocks_dev, size_tb, feat_width), picked_blocks, axis=0)
+    if cols_own == 1:
+        own_blocks = lax.dynamic_slice_in_dim(feats, picked_blocks[0] * size_tb, size_tb, 0)[None]
+    else:
+        own_blocks = jnp.take(feats.reshape(blocks_dev, size_tb, feat_width), picked_blocks, axis=0)
     gathered = gather_directly(own_blocks, "loop", 0)
     tile_vals = tiles.reshape(slot_count, size_tb, size_tb)
     chosen = jnp.take(gathered, tile_cols.reshape(slot_count), axis=0)

time: 187 us -> 187 us (level)
  no operation moved by 1% of the time
where the time goes in v11:
time: 187 us; the launch traced here: 186 us
  waiting for transfers between devices  82 us (44%)
  starting transfers between devices  57.9 us (31%)
  blocking collectives  29.7 us (16%)
  local copies, waits for them, and re-layouts  9.81 us (5%)
  matrix products  3.36 us (2%)
  other arithmetic  2 us (1%)
    all_to_all x1, waiting for transfers between devices, copy_for_each(): return lax.all_to_all(copies, axis, split_axis=0, concat_axis=0, tiled=True)  40.8 us
    all_to_all x1, blocking collectives, body(): lax.all_to_all(jnp.tile(payload, (peers, 1)), others, 0, 0, tiled=True)  29.7 us
    all_to_all x1, waiting for transfers between devices, sum_at_owner(): lax.all_to_all(in_blocks(value, dim, devices), axis, 0, 0, tiled=True)  19.3 us
    all_to_all x1, starting transfers between devices, body(): lax.all_to_all(half_sum.astype(jnp.bfloat16).reshape(peers, -1, feat_widt...  18.2 us
    all_to_all x1, waiting for transfers between devices, body(): lax.all_to_all(half_sum.astype(jnp.bfloat16).reshape(peers, -1, feat_widt...  17.6 us
    all_to_all x1, starting transfers between devices, sum_at_owner(): lax.all_to_all(in_blocks(value, dim, devices), axis, 0, 0, tiled=True)  12.6 us
    all_to_all x1, starting transfers between devices, copy_for_each(): return lax.all_to_all(copies, axis, split_axis=0, concat_axis=0, tiled=True)  10.5 us
    ppermute x2, starting transfers between devices, body(): sib_message, sib_pre_grad = lax.ppermute((message, pre_grad), 'wc', swap)  6.22 us
  transfers between devices with their start and end apart: 7, of which 6 were waited for; matrix products, arithmetic and copies ran while one was open for 1% of the time, Pallas kernels for 0%

profile of v11, /device:TPU:1, one launch (start us, length us, event | category | flops | bytes accessed | tf_op | source)
XLA Modules:
  0.0 186.3 jit_solution(5918583221397112758)
XLA Ops:
  0.7 1.0 constant_dynamic-slice_fusion.4
  1.6 1.5 broadcast_in_dim.19
  3.2 10.5 %all-to-all-start = ((bf16[16,1,128,512]{3,2,1,0:T(8,128)(2,1)}), bf16[16,1,128,512]{3,2,1,0:T(8,128)(2,1)S(1)}, u32[]{:S(2)}, u32[]{:S(2)}) async-start(bf16[16,1,128,512]{3,2,1,0:T(8,128)(2,1)} %broadcast_in_dim.19), calls=%async_computation | async-start | bytes 4194304 | tf_op jit(solution)/shard_map/all_to_all | solution.py:9
  14.4 40.8 %all-to-all-done = bf16[16,1,128,512]{3,2,1,0:T(8,128)(2,1)S(1)} async-done(((bf16[16,1,128,512]{3,2,1,0:T(8,128)(2,1)}), bf16[16,1,128,512]{3,2,1,0:T(8,128)(2,1)S(1)}, u32[]{:S(2)}, u32[]{:S(2)}) %all-to-all-start) | async-done | bytes 2097184 | tf_op jit(solution)/shard_map/all_to_all | solution.py:9
  56.8 1.4 convolution_convert_fusion
  58.4 4.4 %collective-permute-start = (bf16[8,2,32,512]{3,2,1,0:T(8,128)(2,1)S(1)}, bf16[8,2,32,512]{3,2,1,0:T(8,128)(2,1)S(1)}, u32[]{:S(2)}, u32[]{:S(2)}) collective-permute-start(bf16[8,2,32,512]{3,2,1,0:T(8,128)(2,1)S(1)} %bitcast.48), channel_id=1, source_target_pairs={{0,16},{16,0},{1,17},{17,1},{2,18},{18,2},{3,19},{19,3},{4,20},{20... | collective-permute-start | bytes 1572872 | tf_op jit(solution)/shard_map/ppermute | solution.py:70
  62.9 1.5 collective-permute-done
  64.4 1.0 fusion
  65.4 12.6 %all-to-all-start.1 = ((bf16[16,1,32,512]{3,2,1,0:T(8,128)(2,1)}), bf16[16,1,32,512]{3,2,1,0:T(8,128)(2,1)S(1)}, u32[]{:S(2)}, u32[]{:S(2)}) async-start(bf16[16,1,32,512]{3,2,1,0:T(8,128)(2,1)} %bitcast.13), calls=%async_computation.1 | async-start | bytes 1048576 | tf_op jit(solution)/shard_map/all_to_all | solution.py:30
  78.0 0.8 constant_dynamic-slice_fusion
  78.8 19.3 %all-to-all-done.1 = bf16[16,1,32,512]{3,2,1,0:T(8,128)(2,1)S(1)} async-done(((bf16[16,1,32,512]{3,2,1,0:T(8,128)(2,1)}), bf16[16,1,32,512]{3,2,1,0:T(8,128)(2,1)S(1)}, u32[]{:S(2)}, u32[]{:S(2)}) %all-to-all-start.1) | async-done | bytes 524320 | tf_op jit(solution)/shard_map/all_to_all | solution.py:30
  98.6 0.9 divide_subtract_fusion
  99.6 4.3 %collective-permute-start.2 = (bf16[32,512]{1,0:T(8,128)(2,1)S(1)}, bf16[32,512]{1,0:T(8,128)(2,1)S(1)}, u32[]{:S(2)}, u32[]{:S(2)}) collective-permute-start(bf16[32,512]{1,0:T(8,128)(2,1)S(1)} %multiply_convert_fusion), channel_id=1, source_target_pairs={{0,16},{16,0},{1,17},{17,1},{2,18},{18,2},{3,19},{19,3},{4,20},{20... | collective-permute-start | bytes 98312 | tf_op jit(solution)/shard_map/ppermute | solution.py:91
  103.9 1.9 %collective-permute-start.1 = (bf16[32,512]{1,0:T(8,128)(2,1)S(1)}, bf16[32,512]{1,0:T(8,128)(2,1)S(1)}, u32[]{:S(2)}, u32[]{:S(2)}) collective-permute-start(bf16[32,512]{1,0:T(8,128)(2,1)S(1)} %reduce_sum.24), channel_id=1, source_target_pairs={{0,16},{16,0},{1,17},{17,1},{2,18},{18,2},{3,19},{19,3},{4,20},{20... | collective-permute-start | bytes 98312 | tf_op jit(solution)/shard_map/ppermute | solution.py:91
  105.9 1.2 collective-permute-done.1
  107.3 1.0 reshape.101
  108.3 18.2 %all-to-all-start.2 = ((bf16[256,2,512]{2,1,0:T(2,128)(2,1)}), bf16[256,2,512]{2,1,0:T(2,128)(2,1)S(1)}, u32[]{:S(2)}, u32[]{:S(2)}) async-start(bf16[256,2,512]{2,1,0:T(2,128)(2,1)} %reshape.101), calls=%async_computation.2 | async-start | bytes 1048576 | tf_op jit(solution)/shard_map/all_to_all | solution.py:100
  126.7 17.6 %all-to-all-done.2 = bf16[256,2,512]{2,1,0:T(2,128)(2,1)S(1)} async-done(((bf16[256,2,512]{2,1,0:T(2,128)(2,1)}), bf16[256,2,512]{2,1,0:T(2,128)(2,1)S(1)}, u32[]{:S(2)}, u32[]{:S(2)}) %all-to-all-start.2) | async-done | bytes 524320 | tf_op jit(solution)/shard_map/all_to_all | solution.py:100
  145.1 29.7 %all_to_all.24 = bf16[256,2,560]{2,1,0:T(2,128)(2,1)S(1)} all-to-all(bf16[256,2,560]{2,1,0:T(2,128)(2,1)S(1)} %tile.2), channel_id=1, replica_groups=mesh['wy'=8,'wz'=2,'wc'=2,'loop'=16] {'wy','wz','loop'}, dimensions={0} | all-to-all | bytes 1146880 | tf_op jit(solution)/shard_map/all_to_all | solution.py:110
  175.6 5.9 %collective-permute-start.3 = (bf16[512,560]{0,1:T(8,128)(2,1)S(1)}, bf16[512,560]{0,1:T(8,128)(2,1)S(1)}, u32[]{:S(2)}, u32[]{:S(2)}) collective-permute-start(bf16[512,560]{0,1:T(8,128)(2,1)S(1)} %copy.37), channel_id=1, source_target_pairs={{0,16},{16,0},{1,17},{17,1},{2,18},{18,2},{3,19},{19,3},{4,20},{20... | collective-permute-start | bytes 1720328 | tf_op jit(solution)/shard_map/ppermute | solution.py:111
  181.5 1.6 collective-permute-done.3
  183.5 0.8 slice.35
  184.4 0.8 slice.36
  185.6 0.7 add.102
  (43 shorter events, 5.3 us)
Async XLA Ops:
  0.6 97.6 %copy-start = (bf16[512,512]{1,0:T(8,128)(2,1)S(1)}, bf16[512,512]{1,0:T(8,128)(2,1)}, u32[]{:S(2)}) copy-start(bf16[512,512]{1,0:T(8,128)(2,1)} %param.14) | copy-start | bytes 1572868
  3.2 11.2 %copy-start.5 = (s32[1,1,4]{2,1,0:T(1,128)S(1)}, s32[1,1,4]{2,1,0:T(1,128)}, u32[]{:S(2)}) copy-start(s32[1,1,4]{2,1,0:T(1,128)} %param.12) | copy-start | bytes 52
  3.2 52.6 %copy-start.2 = (bf16[1,1,4,128,128]{4,3,2,1,0:T(8,128)(2,1)S(1)}, bf16[1,1,4,128,128]{4,3,2,1,0:T(8,128)(2,1)}, u32[]{:S(2)}) copy-start(bf16[1,1,4,128,128]{4,3,2,1,0:T(8,128)(2,1)} %param.10) | copy-start | bytes 393220
  3.2 52.0 %all-to-all-start = ((bf16[16,1,128,512]{3,2,1,0:T(8,128)(2,1)}), bf16[16,1,128,512]{3,2,1,0:T(8,128)(2,1)S(1)}, u32[]{:S(2)}, u32[]{:S(2)}) async-start(bf16[16,1,128,512]{3,2,1,0:T(8,128)(2,1)} %broadcast_in_dim.19), calls=%async_computation | async-start | bytes 4194304 | tf_op jit(solution)/shard_map/all_to_all | solution.py:9
  55.8 0.9 copy-start.4
  58.4 40.0 %copy-start.1 = (bf16[512,512]{1,0:T(8,128)(2,1)S(1)}, bf16[512,512]{1,0:T(8,128)(2,1)}, u32[]{:S(2)}) copy-start(bf16[512,512]{1,0:T(8,128)(2,1)} %param.15) | copy-start | bytes 1572868
  58.4 6.0 %collective-permute-start = (bf16[8,2,32,512]{3,2,1,0:T(8,128)(2,1)S(1)}, bf16[8,2,32,512]{3,2,1,0:T(8,128)(2,1)S(1)}, u32[]{:S(2)}, u32[]{:S(2)}) collective-permute-start(bf16[8,2,32,512]{3,2,1,0:T(8,128)(2,1)S(1)} %bitcast.48), channel_id=1, source_target_pairs={{0,16},{16,0},{1,17},{17,1},{2,18},{18,2},{3,19},{19,3},{4,20},{20... | collective-permute-start | bytes 1572872 | tf_op jit(solution)/shard_map/ppermute | solution.py:70
  64.4 34.2 %copy-start.3 = (f32[512]{0:T(512)S(1)}, f32[512]{0:T(512)}, u32[]{:S(2)}) copy-start(f32[512]{0:T(512)} %param.16) | copy-start | bytes 6148
  65.4 32.7 %all-to-all-start.1 = ((bf16[16,1,32,512]{3,2,1,0:T(8,128)(2,1)}), bf16[16,1,32,512]{3,2,1,0:T(8,128)(2,1)S(1)}, u32[]{:S(2)}, u32[]{:S(2)}) async-start(bf16[16,1,32,512]{3,2,1,0:T(8,128)(2,1)} %bitcast.13), calls=%async_computation.1 | async-start | bytes 1048576 | tf_op jit(solution)/shard_map/all_to_all | solution.py:30
  99.6 6.2 %collective-permute-start.2 = (bf16[32,512]{1,0:T(8,128)(2,1)S(1)}, bf16[32,512]{1,0:T(8,128)(2,1)S(1)}, u32[]{:S(2)}, u32[]{:S(2)}) collective-permute-start(bf16[32,512]{1,0:T(8,128)(2,1)S(1)} %multiply_convert_fusion), channel_id=1, source_target_pairs={{0,16},{16,0},{1,17},{17,1},{2,18},{18,2},{3,19},{19,3},{4,20},{20... | collective-permute-start | bytes 98312 | tf_op jit(solution)/shard_map/ppermute | solution.py:91
  103.9 3.1 %collective-permute-start.1 = (bf16[32,512]{1,0:T(8,128)(2,1)S(1)}, bf16[32,512]{1,0:T(8,128)(2,1)S(1)}, u32[]{:S(2)}, u32[]{:S(2)}) collective-permute-start(bf16[32,512]{1,0:T(8,128)(2,1)S(1)} %reduce_sum.24), channel_id=1, source_target_pairs={{0,16},{16,0},{1,17},{17,1},{2,18},{18,2},{3,19},{19,3},{4,20},{20... | collective-permute-start | bytes 98312 | tf_op jit(solution)/shard_map/ppermute | solution.py:91
  108.3 35.9 %all-to-all-start.2 = ((bf16[256,2,512]{2,1,0:T(2,128)(2,1)}), bf16[256,2,512]{2,1,0:T(2,128)(2,1)S(1)}, u32[]{:S(2)}, u32[]{:S(2)}) async-start(bf16[256,2,512]{2,1,0:T(2,128)(2,1)} %reshape.101), calls=%async_computation.2 | async-start | bytes 1048576 | tf_op jit(solution)/shard_map/all_to_all | solution.py:100
  175.6 7.5 %collective-permute-start.3 = (bf16[512,560]{0,1:T(8,128)(2,1)S(1)}, bf16[512,560]{0,1:T(8,128)(2,1)S(1)}, u32[]{:S(2)}, u32[]{:S(2)}) collective-permute-start(bf16[512,560]{0,1:T(8,128)(2,1)S(1)} %copy.37), channel_id=1, source_target_pairs={{0,16},{16,0},{1,17},{17,1},{2,18},{18,2},{3,19},{19,3},{4,20},{20... | collective-permute-start | bytes 1720328 | tf_op jit(solution)/shard_map/ppermute | solution.py:111

commit v12 on v11

--- a/solution.py
+++ b/solution.py
@@ -108,12 +108,11 @@
     logit_parts = jnp.concatenate([logit_hi, logit_mid, logit_lo]).reshape(reduced.shape[0], -1)
     payload = jnp.concatenate([reduced, logit_parts], axis=1)
     gathered = lax.all_to_all(jnp.tile(payload, (peers, 1)), others, 0, 0, tiled=True)
-    from_sibling = lax.ppermute(gathered, "wc", swap)
-    from_core0 = jnp.where(core == 0, gathered, from_sibling)
-    from_core1 = jnp.where(core == 0, from_sibling, gathered)
-    grad_msg = from_core0[:, :feat_width]
-    grad_self = from_core1[:, :feat_width]
-    by_core = jnp.stack([from_core0[:, feat_width:], from_core1[:, feat_width:]])
+    own_grad, own_parts = gathered[:, :feat_width], gathered[:, feat_width:]
+    sib_grad, sib_parts = lax.ppermute((own_grad, own_parts), "wc", swap)
+    grad_msg = jnp.where(core == 0, own_grad, sib_grad)
+    grad_self = jnp.where(core == 0, sib_grad, own_grad)
+    by_core = jnp.where(core == 0, jnp.stack([own_parts, sib_parts]), jnp.stack([sib_parts, own_parts]))
     parts = by_core.reshape(
         2, lax.axis_size("wy"), lax.axis_size("wz"), lax.axis_size("loop"), 3, share_rows
     )

time: 187 us -> 187 us (level)
  local copies, waits for them, and re-layouts: 9.81 us -> 7.65 us
  starting transfers between devices: 57.9 us -> 59.8 us
    ppermute x1 -> x2, starting transfers between devices: 5.91 us -> 7.83 us  [body(): sib_grad, sib_parts = lax.ppermute((own_grad, own_parts), 'wc', swap)]
  transfers between devices with their start and end apart: 7 -> 8, of which waited for: 6 -> 6; matrix products, arithmetic and copies ran while one was open for 1% -> 1% of each run, Pallas kernels for 0% -> 0%
where the time goes in v12:
time: 187 us
  waiting for transfers between devices  81.5 us (44%)
  starting transfers between devices  59.8 us (32%)
  blocking collectives  29.7 us (16%)
  local copies, waits for them, and re-layouts  7.65 us (4%)
  matrix products  3.36 us (2%)
  other arithmetic  2.91 us (2%)
    all_to_all x1, waiting for transfers between devices, copy_for_each(): return lax.all_to_all(copies, axis, split_axis=0, concat_axis=0, tiled=True)  40.8 us
    all_to_all x1, blocking collectives, body(): lax.all_to_all(jnp.tile(payload, (peers, 1)), others, 0, 0, tiled=True)  29.7 us
    all_to_all x1, waiting for transfers between devices, sum_at_owner(): lax.all_to_all(in_blocks(value, dim, devices), axis, 0, 0, tiled=True)  19.3 us
    all_to_all x1, starting transfers between devices, body(): lax.all_to_all(half_sum.astype(jnp.bfloat16).reshape(peers, -1, feat_widt...  18.2 us
    all_to_all x1, waiting for transfers between devices, body(): lax.all_to_all(half_sum.astype(jnp.bfloat16).reshape(peers, -1, feat_widt...  17.6 us
    all_to_all x1, starting transfers between devices, sum_at_owner(): lax.all_to_all(in_blocks(value, dim, devices), axis, 0, 0, tiled=True)  12.6 us
    all_to_all x1, starting transfers between devices, copy_for_each(): return lax.all_to_all(copies, axis, split_axis=0, concat_axis=0, tiled=True)  10.5 us
    ppermute x2, starting transfers between devices, body(): sib_grad, sib_parts = lax.ppermute((own_grad, own_parts), 'wc', swap)  7.83 us
  transfers between devices with their start and end apart: 8, of which 6 were waited for; matrix products, arithmetic and copies ran while one was open for 1% of the time, Pallas kernels for 0%

profile of v12, /device:TPU:1, one launch (start us, length us, event | category | flops | bytes accessed | tf_op | source)
XLA Modules:
  0.0 186.5 jit_solution(5829930279454376809)
XLA Ops:
  0.7 1.0 constant_dynamic-slice_fusion.4
  1.6 1.5 broadcast_in_dim.19
  3.2 10.5 %all-to-all-start = ((bf16[16,1,128,512]{3,2,1,0:T(8,128)(2,1)}), bf16[16,1,128,512]{3,2,1,0:T(8,128)(2,1)S(1)}, u32[]{:S(2)}, u32[]{:S(2)}) async-start(bf16[16,1,128,512]{3,2,1,0:T(8,128)(2,1)} %broadcast_in_dim.19), calls=%async_computation | async-start | bytes 4194304 | tf_op jit(solution)/shard_map/all_to_all | solution.py:9
  14.4 40.8 %all-to-all-done = bf16[16,1,128,512]{3,2,1,0:T(8,128)(2,1)S(1)} async-done(((bf16[16,1,128,512]{3,2,1,0:T(8,128)(2,1)}), bf16[16,1,128,512]{3,2,1,0:T(8,128)(2,1)S(1)}, u32[]{:S(2)}, u32[]{:S(2)}) %all-to-all-start) | async-done | bytes 2097184 | tf_op jit(solution)/shard_map/all_to_all | solution.py:9
  56.8 1.4 convolution_convert_fusion
  58.4 4.4 %collective-permute-start = (bf16[8,2,32,512]{3,2,1,0:T(8,128)(2,1)S(1)}, bf16[8,2,32,512]{3,2,1,0:T(8,128)(2,1)S(1)}, u32[]{:S(2)}, u32[]{:S(2)}) collective-permute-start(bf16[8,2,32,512]{3,2,1,0:T(8,128)(2,1)S(1)} %bitcast.48), channel_id=1, source_target_pairs={{0,16},{16,0},{1,17},{17,1},{2,18},{18,2},{3,19},{19,3},{4,20},{20... | collective-permute-start | bytes 1572872 | tf_op jit(solution)/shard_map/ppermute | solution.py:70
  62.8 1.5 collective-permute-done
  64.4 1.0 fusion
  65.4 12.6 %all-to-all-start.1 = ((bf16[16,1,32,512]{3,2,1,0:T(8,128)(2,1)}), bf16[16,1,32,512]{3,2,1,0:T(8,128)(2,1)S(1)}, u32[]{:S(2)}, u32[]{:S(2)}) async-start(bf16[16,1,32,512]{3,2,1,0:T(8,128)(2,1)} %bitcast.13), calls=%async_computation.1 | async-start | bytes 1048576 | tf_op jit(solution)/shard_map/all_to_all | solution.py:30
  78.0 0.8 constant_dynamic-slice_fusion
  78.8 19.3 %all-to-all-done.1 = bf16[16,1,32,512]{3,2,1,0:T(8,128)(2,1)S(1)} async-done(((bf16[16,1,32,512]{3,2,1,0:T(8,128)(2,1)}), bf16[16,1,32,512]{3,2,1,0:T(8,128)(2,1)S(1)}, u32[]{:S(2)}, u32[]{:S(2)}) %all-to-all-start.1) | async-done | bytes 524320 | tf_op jit(solution)/shard_map/all_to_all | solution.py:30
  98.6 0.9 divide_subtract_fusion
  99.6 4.3 %collective-permute-start.2 = (bf16[32,512]{1,0:T(8,128)(2,1)S(1)}, bf16[32,512]{1,0:T(8,128)(2,1)S(1)}, u32[]{:S(2)}, u32[]{:S(2)}) collective-permute-start(bf16[32,512]{1,0:T(8,128)(2,1)S(1)} %multiply_convert_fusion), channel_id=1, source_target_pairs={{0,16},{16,0},{1,17},{17,1},{2,18},{18,2},{3,19},{19,3},{4,20},{20... | collective-permute-start | bytes 98312 | tf_op jit(solution)/shard_map/ppermute | solution.py:91
  103.9 1.9 %collective-permute-start.1 = (bf16[32,512]{1,0:T(8,128)(2,1)S(1)}, bf16[32,512]{1,0:T(8,128)(2,1)S(1)}, u32[]{:S(2)}, u32[]{:S(2)}) collective-permute-start(bf16[32,512]{1,0:T(8,128)(2,1)S(1)} %reduce_sum.24), channel_id=1, source_target_pairs={{0,16},{16,0},{1,17},{17,1},{2,18},{18,2},{3,19},{19,3},{4,20},{20... | collective-permute-start | bytes 98312 | tf_op jit(solution)/shard_map/ppermute | solution.py:91
  105.9 1.2 collective-permute-done.1
  107.3 1.0 reshape.105
  108.3 18.2 %all-to-all-start.2 = ((bf16[256,2,512]{2,1,0:T(2,128)(2,1)}), bf16[256,2,512]{2,1,0:T(2,128)(2,1)S(1)}, u32[]{:S(2)}, u32[]{:S(2)}) async-start(bf16[256,2,512]{2,1,0:T(2,128)(2,1)} %reshape.105), calls=%async_computation.2 | async-start | bytes 1048576 | tf_op jit(solution)/shard_map/all_to_all | solution.py:100
  126.7 17.6 %all-to-all-done.2 = bf16[256,2,512]{2,1,0:T(2,128)(2,1)S(1)} async-done(((bf16[256,2,512]{2,1,0:T(2,128)(2,1)}), bf16[256,2,512]{2,1,0:T(2,128)(2,1)S(1)}, u32[]{:S(2)}, u32[]{:S(2)}) %all-to-all-start.2) | async-done | bytes 524320 | tf_op jit(solution)/shard_map/all_to_all | solution.py:100
  145.1 29.7 %all_to_all.24 = bf16[256,2,560]{2,1,0:T(2,128)(2,1)S(1)} all-to-all(bf16[256,2,560]{2,1,0:T(2,128)(2,1)S(1)} %tile.2), channel_id=1, replica_groups=mesh['wy'=8,'wz'=2,'wc'=2,'loop'=16] {'wy','wz','loop'}, dimensions={0} | all-to-all | bytes 1146880 | tf_op jit(solution)/shard_map/all_to_all | solution.py:110
  175.4 5.9 %collective-permute-start.4 = (bf16[512,512]{1,0:T(8,128)(2,1)S(1)}, bf16[512,512]{1,0:T(8,128)(2,1)S(1)}, u32[]{:S(2)}, u32[]{:S(2)}) collective-permute-start(bf16[512,512]{1,0:T(8,128)(2,1)S(1)} %slice.26), channel_id=1, source_target_pairs={{0,16},{16,0},{1,17},{17,1},{2,18},{18,2},{3,19},{19,3},{4,20},{20... | collective-permute-start | bytes 1572872 | tf_op jit(solution)/shard_map/ppermute | solution.py:112
  181.3 1.9 %collective-permute-start.3 = (bf16[512,48]{1,0:T(8,128)(2,1)S(1)}, bf16[512,48]{1,0:T(8,128)(2,1)S(1)}, u32[]{:S(2)}, u32[]{:S(2)}) collective-permute-start(bf16[512,48]{1,0:T(8,128)(2,1)S(1)} %slice.22), channel_id=1, source_target_pairs={{0,16},{16,0},{1,17},{17,1},{2,18},{18,2},{3,19},{19,3},{4,20},{20... | collective-permute-start | bytes 147464 | tf_op jit(solution)/shard_map/ppermute | solution.py:112
  183.4 1.1 collective-permute-done.3
  184.8 0.7 add.102
  185.5 1.0 broadcast_select_fusion
  (41 shorter events, 4.7 us)
Async XLA Ops:
  0.6 97.6 %copy-start = (bf16[512,512]{1,0:T(8,128)(2,1)S(1)}, bf16[512,512]{1,0:T(8,128)(2,1)}, u32[]{:S(2)}) copy-start(bf16[512,512]{1,0:T(8,128)(2,1)} %param.14) | copy-start | bytes 1572868
  3.2 11.2 %copy-start.5 = (s32[1,1,4]{2,1,0:T(1,128)S(1)}, s32[1,1,4]{2,1,0:T(1,128)}, u32[]{:S(2)}) copy-start(s32[1,1,4]{2,1,0:T(1,128)} %param.12) | copy-start | bytes 52
  3.2 52.6 %copy-start.2 = (bf16[1,1,4,128,128]{4,3,2,1,0:T(8,128)(2,1)S(1)}, bf16[1,1,4,128,128]{4,3,2,1,0:T(8,128)(2,1)}, u32[]{:S(2)}) copy-start(bf16[1,1,4,128,128]{4,3,2,1,0:T(8,128)(2,1)} %param.10) | copy-start | bytes 393220
  3.2 52.0 %all-to-all-start = ((bf16[16,1,128,512]{3,2,1,0:T(8,128)(2,1)}), bf16[16,1,128,512]{3,2,1,0:T(8,128)(2,1)S(1)}, u32[]{:S(2)}, u32[]{:S(2)}) async-start(bf16[16,1,128,512]{3,2,1,0:T(8,128)(2,1)} %broadcast_in_dim.19), calls=%async_computation | async-start | bytes 4194304 | tf_op jit(solution)/shard_map/all_to_all | solution.py:9
  55.8 0.9 copy-start.4
  58.4 40.0 %copy-start.1 = (bf16[512,512]{1,0:T(8,128)(2,1)S(1)}, bf16[512,512]{1,0:T(8,128)(2,1)}, u32[]{:S(2)}) copy-start(bf16[512,512]{1,0:T(8,128)(2,1)} %param.15) | copy-start | bytes 1572868
  58.4 6.0 %collective-permute-start = (bf16[8,2,32,512]{3,2,1,0:T(8,128)(2,1)S(1)}, bf16[8,2,32,512]{3,2,1,0:T(8,128)(2,1)S(1)}, u32[]{:S(2)}, u32[]{:S(2)}) collective-permute-start(bf16[8,2,32,512]{3,2,1,0:T(8,128)(2,1)S(1)} %bitcast.48), channel_id=1, source_target_pairs={{0,16},{16,0},{1,17},{17,1},{2,18},{18,2},{3,19},{19,3},{4,20},{20... | collective-permute-start | bytes 1572872 | tf_op jit(solution)/shard_map/ppermute | solution.py:70
  64.4 34.3 %copy-start.3 = (f32[512]{0:T(512)S(1)}, f32[512]{0:T(512)}, u32[]{:S(2)}) copy-start(f32[512]{0:T(512)} %param.16) | copy-start | bytes 6148
  65.4 32.8 %all-to-all-start.1 = ((bf16[16,1,32,512]{3,2,1,0:T(8,128)(2,1)}), bf16[16,1,32,512]{3,2,1,0:T(8,128)(2,1)S(1)}, u32[]{:S(2)}, u32[]{:S(2)}) async-start(bf16[16,1,32,512]{3,2,1,0:T(8,128)(2,1)} %bitcast.13), calls=%async_computation.1 | async-start | bytes 1048576 | tf_op jit(solution)/shard_map/all_to_all | solution.py:30
  99.6 6.2 %collective-permute-start.2 = (bf16[32,512]{1,0:T(8,128)(2,1)S(1)}, bf16[32,512]{1,0:T(8,128)(2,1)S(1)}, u32[]{:S(2)}, u32[]{:S(2)}) collective-permute-start(bf16[32,512]{1,0:T(8,128)(2,1)S(1)} %multiply_convert_fusion), channel_id=1, source_target_pairs={{0,16},{16,0},{1,17},{17,1},{2,18},{18,2},{3,19},{19,3},{4,20},{20... | collective-permute-start | bytes 98312 | tf_op jit(solution)/shard_map/ppermute | solution.py:91
  103.9 3.1 %collective-permute-start.1 = (bf16[32,512]{1,0:T(8,128)(2,1)S(1)}, bf16[32,512]{1,0:T(8,128)(2,1)S(1)}, u32[]{:S(2)}, u32[]{:S(2)}) collective-permute-start(bf16[32,512]{1,0:T(8,128)(2,1)S(1)} %reduce_sum.24), channel_id=1, source_target_pairs={{0,16},{16,0},{1,17},{17,1},{2,18},{18,2},{3,19},{19,3},{4,20},{20... | collective-permute-start | bytes 98312 | tf_op jit(solution)/shard_map/ppermute | solution.py:91
  108.3 35.9 %all-to-all-start.2 = ((bf16[256,2,512]{2,1,0:T(2,128)(2,1)}), bf16[256,2,512]{2,1,0:T(2,128)(2,1)S(1)}, u32[]{:S(2)}, u32[]{:S(2)}) async-start(bf16[256,2,512]{2,1,0:T(2,128)(2,1)} %reshape.105), calls=%async_computation.2 | async-start | bytes 1048576 | tf_op jit(solution)/shard_map/all_to_all | solution.py:100
  175.4 10.1 %collective-permute-start.4 = (bf16[512,512]{1,0:T(8,128)(2,1)S(1)}, bf16[512,512]{1,0:T(8,128)(2,1)S(1)}, u32[]{:S(2)}, u32[]{:S(2)}) collective-permute-start(bf16[512,512]{1,0:T(8,128)(2,1)S(1)} %slice.26), channel_id=1, source_target_pairs={{0,16},{16,0},{1,17},{17,1},{2,18},{18,2},{3,19},{19,3},{4,20},{20... | collective-permute-start | bytes 1572872 | tf_op jit(solution)/shard_map/ppermute | solution.py:112
  181.3 3.2 %collective-permute-start.3 = (bf16[512,48]{1,0:T(8,128)(2,1)S(1)}, bf16[512,48]{1,0:T(8,128)(2,1)S(1)}, u32[]{:S(2)}, u32[]{:S(2)}) collective-permute-start(bf16[512,48]{1,0:T(8,128)(2,1)S(1)} %slice.22), channel_id=1, source_target_pairs={{0,16},{16,0},{1,17},{17,1},{2,18},{18,2},{3,19},{19,3},{4,20},{20... | collective-permute-start | bytes 147464 | tf_op jit(solution)/shard_map/ppermute | solution.py:112
